TPU v7x, 1024 devices: a whole 8x8x8 slice. The times are simulated.
1024 devices in a mesh: az: 16 (over x, core), rad: 8 (over y), vert: 8 (over z).
Axes of the slice: x: 8, y: 8, z: 8, core: 2. Of those that a mesh axis runs over, the one named last changes fastest.
Arguments:
- fields: float32 [8, 128, 64, 2048], P(None, 'rad', 'vert', 'az'), may hold values from -6 to 6
- shear_shift: int32 [128], P('rad'), may hold values from 0 to 2047, as said below
- remap_fraction: float32 [128], P('rad'), may hold values from 0 to 1
- diffusivity: float32 [8], replicated, may hold values from 0.03 to 0.12
Outputs:
- advected: float32 [8, 128, 64, 2048], P(None, 'rad', 'vert', 'az')
Inputs may be any that keep to these rules, and one draw needn't show every extreme that they name: `shear_shift`: each radial row's integer shift; some row has 0 and some row has 2047.
All inputs are finite; a program needn't handle non-finite values.
Results may differ from a plain program's by a relative error of at most 0.00002.
Values sent between devices are 32-bit elements; how exact they have to be, the bound alone decides.
No kernel may reach another device: no remote copies, remote signals or barrier semaphores. Data moves between devices by JAX's collectives and lax.ppermute only.
A program may use at most 32 MiB of HBM per device.

v0:
```python
import jax
import jax.numpy as jnp
from jax import lax
from jax.sharding import PartitionSpec as P


def shifted_2(array, axis, by):
    peers = lax.axis_size(axis)
    return lax.ppermute(array, axis, [(i, (i + by) % peers) for i in range(peers)])


def extended_2(array, sides, width, wrap):
    for axis, dim in sides:
        peers, length = (lax.axis_size(axis), array.shape[dim])
        up = [(i, (i + 1) % peers) for i in range(peers if wrap else peers - 1)]
        down = [(j, i) for i, j in up]
        last = lax.slice_in_dim(array, length - width, length, axis=dim)
        initial = lax.slice_in_dim(array, 0, width, axis=dim)
        before = lax.ppermute(last, axis, up)
        after = lax.ppermute(initial, axis, down)
        array = jnp.concatenate([before, array, after], axis=dim)
    return array


def barrel(block, amounts, span):
    result = block
    for level in range(span.bit_length()):
        moved = jnp.roll(result, 1 << level, axis=3)
        chosen = amounts // (1 << level) % 2 == 1
        result = jnp.where(chosen[None, :, None, None], moved, result)
    return result


def per_device(fields, shear_shift, remap_fraction, diffusivity):
    width = fields.shape[3]
    loop_size = lax.axis_size("az")
    blocks = shear_shift // width
    remainder = shear_shift % width
    current = fields
    for level in range(loop_size.bit_length() - 1):
        moved = shifted_2(current, "az", 1 << level)
        chosen = blocks // (1 << level) % 2 == 1
        current = jnp.where(chosen[None, :, None, None], moved, current)
    previous = shifted_2(current, "az", 1)
    joined = jnp.concatenate([previous, current], axis=3)
    shifted = barrel(joined, remainder, width - 1)[..., width:]
    padded = extended_2(shifted, (("rad", 1), ("vert", 2)), 1, False)
    laplace = (
        padded[:, 2:, 1:-1]
        + padded[:, :-2, 1:-1]
        + padded[:, 1:-1, 2:]
        + padded[:, 1:-1, :-2]
        - 4.0 * shifted
    )
    diffused = shifted + diffusivity[:, None, None, None] * laplace
    extended = extended_2(diffused, (("az", 3),), 1, True)
    after = extended[..., 2:]
    before = extended[..., :-2]
    fraction = remap_fraction[None, :, None, None]
    return (
        diffused
        - 0.5 * fraction * (after - before)
        + 0.5 * fraction * fraction * (after - 2.0 * diffused + before)
    )


def solution(mesh):
    in_specs = (P(None, "rad", "vert", "az"), P("rad"), P("rad"), P())
    out_specs = P(None, "rad", "vert", "az")
    return jax.shard_map(
        per_device, mesh=mesh, in_specs=in_specs, out_specs=out_specs, check_vma=False
    )
```

profile of v0, /device:TPU:1, one launch (start us, length us, event | category | flops | bytes accessed | tf_op | source)
XLA Modules:
  0.0 143.1 jit_solution(12512028352732422093)
XLA Ops:
  0.0 1.4 copy.5
  1.4 2.6 %collective-permute-start = (f32[8,16,8,128]{3,0,2,1:T(8,128)S(1)}, f32[8,16,8,128]{3,0,2,1:T(8,128)S(1)}, u32[]{:S(2)}, u32[]{:S(2)}) collective-permute-start(f32[8,16,8,128]{3,0,2,1:T(8,128)S(1)} %copy.5), channel_id=1, source_target_pairs={{0,64},{64,128},{128,192},{192,256},{256,320},{320,384},{384,448},... | collective-permute-start | bytes 1572872 | tf_op jit(solution)/shard_map/ppermute | solution.py:9
  4.1 12.9 %collective-permute-done = f32[8,16,8,128]{3,0,2,1:T(8,128)S(1)} collective-permute-done((f32[8,16,8,128]{3,0,2,1:T(8,128)S(1)}, f32[8,16,8,128]{3,0,2,1:T(8,128)S(1)}, u32[]{:S(2)}, u32[]{:S(2)}) %collective-permute-start) | collective-permute-done | bytes 524320 | tf_op jit(solution)/shard_map/ppermute | solution.py:9
  17.0 0.3 broadcast_select_fusion
  17.3 1.9 %collective-permute-start.1 = (f32[8,16,8,128]{3,0,2,1:T(8,128)S(1)}, f32[8,16,8,128]{3,0,2,1:T(8,128)S(1)}, u32[]{:S(2)}, u32[]{:S(2)}) collective-permute-start(f32[8,16,8,128]{3,0,2,1:T(8,128)S(1)} %broadcast_select_fusion), channel_id=1, source_target_pairs={{0,128},{64,192},{128,256},{192,320},{256,384},{320,448},{384,512}... | collective-permute-start | bytes 1572872 | tf_op jit(solution)/shard_map/ppermute | solution.py:9
  19.2 15.5 %collective-permute-done.1 = f32[8,16,8,128]{3,0,2,1:T(8,128)S(1)} collective-permute-done((f32[8,16,8,128]{3,0,2,1:T(8,128)S(1)}, f32[8,16,8,128]{3,0,2,1:T(8,128)S(1)}, u32[]{:S(2)}, u32[]{:S(2)}) %collective-permute-start.1) | collective-permute-done | bytes 524320 | tf_op jit(solution)/shard_map/ppermute | solution.py:9
  34.8 1.9 %collective-permute-start.2 = (f32[8,16,8,128]{3,0,2,1:T(8,128)S(1)}, f32[8,16,8,128]{3,0,2,1:T(8,128)S(1)}, u32[]{:S(2)}, u32[]{:S(2)}) collective-permute-start(f32[8,16,8,128]{3,0,2,1:T(8,128)S(1)} %broadcast_select_fusion.1), channel_id=1, source_target_pairs={{0,256},{64,320},{128,384},{192,448},{256,512},{320,576},{384,640}... | collective-permute-start | bytes 1572872 | tf_op jit(solution)/shard_map/ppermute | solution.py:9
  36.7 24.2 %collective-permute-done.2 = f32[8,16,8,128]{3,0,2,1:T(8,128)S(1)} collective-permute-done((f32[8,16,8,128]{3,0,2,1:T(8,128)S(1)}, f32[8,16,8,128]{3,0,2,1:T(8,128)S(1)}, u32[]{:S(2)}, u32[]{:S(2)}) %collective-permute-start.2) | collective-permute-done | bytes 524320 | tf_op jit(solution)/shard_map/ppermute | solution.py:9
  61.0 1.9 %collective-permute-start.3 = (f32[8,16,8,128]{3,0,2,1:T(8,128)S(1)}, f32[8,16,8,128]{3,0,2,1:T(8,128)S(1)}, u32[]{:S(2)}, u32[]{:S(2)}) collective-permute-start(f32[8,16,8,128]{3,0,2,1:T(8,128)S(1)} %broadcast_select_fusion.2), channel_id=1, source_target_pairs={{0,512},{64,576},{128,640},{192,704},{256,768},{320,832},{384,896}... | collective-permute-start | bytes 1572872 | tf_op jit(solution)/shard_map/ppermute | solution.py:9
  63.0 26.7 %collective-permute-done.3 = f32[8,16,8,128]{3,0,2,1:T(8,128)S(1)} collective-permute-done((f32[8,16,8,128]{3,0,2,1:T(8,128)S(1)}, f32[8,16,8,128]{3,0,2,1:T(8,128)S(1)}, u32[]{:S(2)}, u32[]{:S(2)}) %collective-permute-start.3) | collective-permute-done | bytes 524320 | tf_op jit(solution)/shard_map/ppermute | solution.py:9
  90.1 5.9 %collective-permute-done.4 = f32[8,16,8,128]{3,0,2,1:T(8,128)S(1)} collective-permute-done((f32[8,16,8,128]{3,0,2,1:T(8,128)S(1)}, f32[8,16,8,128]{3,0,2,1:T(8,128)S(1)}, u32[]{:S(2)}, u32[]{:S(2)}) %collective-permute-start.4) | collective-permute-done | bytes 524320 | tf_op jit(solution)/shard_map/ppermute | solution.py:9
  96.0 0.4 fusion.1
  96.4 0.2 slice.134
  96.6 0.4 maximum_select_fusion
  97.2 0.4 maximum_select_fusion.1
  97.7 0.4 maximum_select_fusion.2
  98.3 0.4 maximum_select_fusion.3
  98.9 0.4 maximum_select_fusion.4
  99.4 0.4 maximum_select_fusion.5
  99.8 1.3 collective-permute-start.5
  101.1 17.7 %collective-permute-start.6 = (f32[8,1,8,128]{3,0,2,1:T(8,128)S(1)}, f32[8,1,8,128]{3,0,2,1:T(8,128)S(1)}, u32[]{:S(2)}, u32[]{:S(2)}) collective-permute-start(f32[8,1,8,128]{3,0,2,1:T(8,128)S(1)} %get-tuple-element.9), channel_id=1, source_target_pairs={{0,8},{8,16},{16,24},{24,32},{32,40},{40,48},{48,56},{1,9},{9,17},... | collective-permute-start | bytes 98312 | tf_op jit(solution)/shard_map/ppermute | solution.py:19
  118.9 0.9 collective-permute-done.6
  119.9 1.3 collective-permute-start.7
  121.2 5.6 %collective-permute-start.8 = (f32[8,18,1,128]{3,0,2,1:T(8,128)S(1)}, f32[8,18,1,128]{3,0,2,1:T(8,128)S(1)}, u32[]{:S(2)}, u32[]{:S(2)}) collective-permute-start(f32[8,18,1,128]{3,0,2,1:T(8,128)S(1)} %get-tuple-element.12), channel_id=1, source_target_pairs={{0,1},{1,2},{2,3},{3,4},{4,5},{5,6},{6,7},{8,9},{9,10},{10,11},{11... | collective-permute-start | bytes 221192 | tf_op jit(solution)/shard_map/ppermute | solution.py:19
  126.8 0.7 collective-permute-done.7
  127.5 0.9 collective-permute-done.8
  128.6 0.2 fusion.30
  128.8 4.3 %collective-permute-start.10 = (f32[8,16,8,1]{3,0,2,1:T(8,128)S(1)}, f32[8,16,8,1]{3,0,2,1:T(8,128)S(1)}, u32[]{:S(2)}, u32[]{:S(2)}) collective-permute-start(f32[8,16,8,1]{3,0,2,1:T(8,128)S(1)} %get-tuple-element.13), channel_id=1, source_target_pairs={{0,64},{64,128},{128,192},{192,256},{256,320},{320,384},{384,448},... | collective-permute-start | bytes 12296 | tf_op jit(solution)/shard_map/ppermute | solution.py:19
  133.1 6.1 %collective-permute-done.10 = f32[8,16,8,1]{3,0,2,1:T(8,128)S(1)} collective-permute-done((f32[8,16,8,1]{3,0,2,1:T(8,128)S(1)}, f32[8,16,8,1]{3,0,2,1:T(8,128)S(1)}, u32[]{:S(2)}, u32[]{:S(2)}) %collective-permute-start.10) | collective-permute-done | bytes 4128 | tf_op jit(solution)/shard_map/ppermute | solution.py:19
  139.2 2.5 %collective-permute-done.9 = f32[8,16,8,1]{3,0,2,1:T(8,128)S(1)} collective-permute-done((f32[8,16,8,1]{3,0,2,1:T(8,128)S(1)}, f32[8,16,8,1]{3,0,2,1:T(8,128)S(1)}, u32[]{:S(2)}, u32[]{:S(2)}) %collective-permute-start.9) | collective-permute-done | bytes 4128 | tf_op jit(solution)/shard_map/ppermute | solution.py:20
  141.7 0.5 multiply_add_fusion
  142.2 0.9 copy.7
  (29 shorter events, 2.0 us)
Async XLA Ops:
  0.0 17.0 %copy-start = (f32[8,16,8,128]{3,2,1,0:T(8,128)S(1)}, f32[8,16,8,128]{3,2,1,0:T(8,128)}, u32[]{:S(2)}) copy-start(f32[8,16,8,128]{3,2,1,0:T(8,128)} %param.4) | copy-start | bytes 1572868
  0.0 4.0 %copy-start.2 = (s32[16]{0:T(128)S(1)}, s32[16]{0:T(128)}, u32[]{:S(2)}) copy-start(s32[16]{0:T(128)} %param.5) | copy-start | bytes 196
  1.4 15.5 %collective-permute-start = (f32[8,16,8,128]{3,0,2,1:T(8,128)S(1)}, f32[8,16,8,128]{3,0,2,1:T(8,128)S(1)}, u32[]{:S(2)}, u32[]{:S(2)}) collective-permute-start(f32[8,16,8,128]{3,0,2,1:T(8,128)S(1)} %copy.5), channel_id=1, source_target_pairs={{0,64},{64,128},{128,192},{192,256},{256,320},{320,384},{384,448},... | collective-permute-start | bytes 1572872 | tf_op jit(solution)/shard_map/ppermute | solution.py:9
  17.3 17.4 %collective-permute-start.1 = (f32[8,16,8,128]{3,0,2,1:T(8,128)S(1)}, f32[8,16,8,128]{3,0,2,1:T(8,128)S(1)}, u32[]{:S(2)}, u32[]{:S(2)}) collective-permute-start(f32[8,16,8,128]{3,0,2,1:T(8,128)S(1)} %broadcast_select_fusion), channel_id=1, source_target_pairs={{0,128},{64,192},{128,256},{192,320},{256,384},{320,448},{384,512}... | collective-permute-start | bytes 1572872 | tf_op jit(solution)/shard_map/ppermute | solution.py:9
  34.8 26.1 %collective-permute-start.2 = (f32[8,16,8,128]{3,0,2,1:T(8,128)S(1)}, f32[8,16,8,128]{3,0,2,1:T(8,128)S(1)}, u32[]{:S(2)}, u32[]{:S(2)}) collective-permute-start(f32[8,16,8,128]{3,0,2,1:T(8,128)S(1)} %broadcast_select_fusion.1), channel_id=1, source_target_pairs={{0,256},{64,320},{128,384},{192,448},{256,512},{320,576},{384,640}... | collective-permute-start | bytes 1572872 | tf_op jit(solution)/shard_map/ppermute | solution.py:9
  61.0 28.7 %collective-permute-start.3 = (f32[8,16,8,128]{3,0,2,1:T(8,128)S(1)}, f32[8,16,8,128]{3,0,2,1:T(8,128)S(1)}, u32[]{:S(2)}, u32[]{:S(2)}) collective-permute-start(f32[8,16,8,128]{3,0,2,1:T(8,128)S(1)} %broadcast_select_fusion.2), channel_id=1, source_target_pairs={{0,512},{64,576},{128,640},{192,704},{256,768},{320,832},{384,896}... | collective-permute-start | bytes 1572872 | tf_op jit(solution)/shard_map/ppermute | solution.py:9
  89.8 6.1 %collective-permute-start.4 = (f32[8,16,8,128]{3,0,2,1:T(8,128)S(1)}, f32[8,16,8,128]{3,0,2,1:T(8,128)S(1)}, u32[]{:S(2)}, u32[]{:S(2)}) collective-permute-start(f32[8,16,8,128]{3,0,2,1:T(8,128)S(1)} %broadcast_select_fusion.3), channel_id=1, source_target_pairs={{0,64},{64,128},{128,192},{192,256},{256,320},{320,384},{384,448},... | collective-permute-start | bytes 1572872 | tf_op jit(solution)/shard_map/ppermute | solution.py:9
  99.8 19.1 %collective-permute-start.5 = (f32[8,1,8,128]{3,0,2,1:T(8,128)S(1)}, f32[8,1,8,128]{3,0,2,1:T(8,128)S(1)}, u32[]{:S(2)}, u32[]{:S(2)}) collective-permute-start(f32[8,1,8,128]{3,0,2,1:T(8,128)S(1)} %get-tuple-element.10), channel_id=1, source_target_pairs={{8,0},{16,8},{24,16},{32,24},{40,32},{48,40},{56,48},{9,1},{17,9},... | collective-permute-start | bytes 98312 | tf_op jit(solution)/shard_map/ppermute | solution.py:20
  101.1 18.8 %collective-permute-start.6 = (f32[8,1,8,128]{3,0,2,1:T(8,128)S(1)}, f32[8,1,8,128]{3,0,2,1:T(8,128)S(1)}, u32[]{:S(2)}, u32[]{:S(2)}) collective-permute-start(f32[8,1,8,128]{3,0,2,1:T(8,128)S(1)} %get-tuple-element.9), channel_id=1, source_target_pairs={{0,8},{8,16},{16,24},{24,32},{32,40},{40,48},{48,56},{1,9},{9,17},... | collective-permute-start | bytes 98312 | tf_op jit(solution)/shard_map/ppermute | solution.py:19
  119.9 8.5 %copy-start.1 = (f32[8]{0:T(128)S(1)}, f32[8]{0:T(128)}, u32[]{:S(2)}) copy-start(f32[8]{0:T(128)} %param.7) | copy-start | bytes 100
  119.9 7.6 %collective-permute-start.7 = (f32[8,18,1,128]{3,0,2,1:T(8,128)S(1)}, f32[8,18,1,128]{3,0,2,1:T(8,128)S(1)}, u32[]{:S(2)}, u32[]{:S(2)}) collective-permute-start(f32[8,18,1,128]{3,0,2,1:T(8,128)S(1)} %get-tuple-element.11), channel_id=1, source_target_pairs={{1,0},{2,1},{3,2},{4,3},{5,4},{6,5},{7,6},{9,8},{10,9},{11,10},{12... | collective-permute-start | bytes 221192 | tf_op jit(solution)/shard_map/ppermute | solution.py:20
  121.2 7.2 %collective-permute-start.8 = (f32[8,18,1,128]{3,0,2,1:T(8,128)S(1)}, f32[8,18,1,128]{3,0,2,1:T(8,128)S(1)}, u32[]{:S(2)}, u32[]{:S(2)}) collective-permute-start(f32[8,18,1,128]{3,0,2,1:T(8,128)S(1)} %get-tuple-element.12), channel_id=1, source_target_pairs={{0,1},{1,2},{2,3},{3,4},{4,5},{5,6},{6,7},{8,9},{9,10},{10,11},{11... | collective-permute-start | bytes 221192 | tf_op jit(solution)/shard_map/ppermute | solution.py:19
  128.8 4.3 %copy-start.3 = (f32[16]{0:T(128)S(1)}, f32[16]{0:T(128)}, u32[]{:S(2)}) copy-start(f32[16]{0:T(128)} %param.6) | copy-start | bytes 196
  128.8 10.4 %collective-permute-start.10 = (f32[8,16,8,1]{3,0,2,1:T(8,128)S(1)}, f32[8,16,8,1]{3,0,2,1:T(8,128)S(1)}, u32[]{:S(2)}, u32[]{:S(2)}) collective-permute-start(f32[8,16,8,1]{3,0,2,1:T(8,128)S(1)} %get-tuple-element.13), channel_id=1, source_target_pairs={{0,64},{64,128},{128,192},{192,256},{256,320},{320,384},{384,448},... | collective-permute-start | bytes 12296 | tf_op jit(solution)/shard_map/ppermute | solution.py:19
  133.0 8.6 %collective-permute-start.9 = (f32[8,16,8,1]{3,0,2,1:T(8,128)S(1)}, f32[8,16,8,1]{3,0,2,1:T(8,128)S(1)}, u32[]{:S(2)}, u32[]{:S(2)}) collective-permute-start(f32[8,16,8,1]{3,0,2,1:T(8,128)S(1)} %get-tuple-element.14), channel_id=1, source_target_pairs={{64,0},{128,64},{192,128},{256,192},{320,256},{384,320},{448,384},... | collective-permute-start | bytes 12296 | tf_op jit(solution)/shard_map/ppermute | solution.py:20
where the time goes:
time: 146 us; the launch traced here: 143 us
  waiting for transfers between devices  96.3 us (66%)
  starting transfers between devices  38.6 us (26%)
  other arithmetic  4.01 us (3%)
  local copies, waits for them, and re-layouts  3.98 us (3%)
    ppermute x5, waiting for transfers between devices, shifted_2(): lax.ppermute(array, axis, [(i, (i + by) % peers) for i in range(peers)])  85.1 us
    ppermute x3, starting transfers between devices, extended_2(): before = lax.ppermute(last, axis, up)  27.6 us
    ppermute x5, starting transfers between devices, shifted_2(): lax.ppermute(array, axis, [(i, (i + by) % peers) for i in range(peers)])  8.38 us
    ppermute x3, waiting for transfers between devices, extended_2(): before = lax.ppermute(last, axis, up)  7.96 us
    ppermute x3, waiting for transfers between devices, extended_2(): after = lax.ppermute(initial, axis, down)  3.17 us
  transfers between devices with their start and end apart: 11, of which 10 were waited for; matrix products, arithmetic and copies ran while one was open for 0% of the time, Pallas kernels for 0%

commit v1 on v0

v1 whole, which is shorter than its diff:
```python
import jax
import jax.numpy as jnp
from jax import lax
from jax.sharding import PartitionSpec as P


def barrel(block, amounts, span):
    result = block
    for level in range(span.bit_length()):
        moved = jnp.roll(result, 1 << level, axis=2)
        chosen = amounts // (1 << level) % 2 == 1
        result = jnp.where(chosen[:, None, None], moved, result)
    return result


def halo_pairs(rows, halves, fields, step):
    pairs = []
    for r in range(rows):
        for f in range(fields):
            for h in range(halves):
                nh, nr = h + step, r
                if nh == halves:
                    nh, nr = 0, r + 1
                elif nh < 0:
                    nh, nr = halves - 1, r - 1
                if 0 <= nr < rows:
                    pairs.append(((f * halves + h) * rows + r, (f * halves + nh) * rows + nr))
    return pairs


def per_device(fields, shear_shift, remap_fraction, diffusivity):
    nf, nrow, nz, width = fields.shape
    loop = lax.axis_size("az")
    halves = loop // nf
    rows = nrow // halves
    x = fields.reshape(nf * halves, rows, nz, width)
    y = lax.all_to_all(x, "az", 0, 3, tiled=True)[0]
    length = y.shape[2]
    me = lax.axis_index("az")
    f = me // halves
    h = me % halves
    amounts = lax.dynamic_slice_in_dim(shear_shift, h * rows, rows)
    fraction = lax.dynamic_slice_in_dim(remap_fraction, h * rows, rows)[:, None, None]
    coefficient = diffusivity[f]
    shifted = barrel(y, amounts, length - 1)

    nrad = lax.axis_size("rad")
    nvert = lax.axis_size("vert")
    both = ("az", "rad")
    prev_row = lax.ppermute(shifted[-1:], both, halo_pairs(nrad, halves, nf, 1))
    next_row = lax.ppermute(shifted[:1], both, halo_pairs(nrad, halves, nf, -1))
    up = [(i, i + 1) for i in range(nvert - 1)]
    down = [(i + 1, i) for i in range(nvert - 1)]
    below = lax.ppermute(shifted[:, -1:], "vert", up)
    above = lax.ppermute(shifted[:, :1], "vert", down)

    r_plus = jnp.concatenate([shifted[1:], next_row], axis=0)
    r_minus = jnp.concatenate([prev_row, shifted[:-1]], axis=0)
    z_plus = jnp.concatenate([shifted[:, 1:], above], axis=1)
    z_minus = jnp.concatenate([below, shifted[:, :-1]], axis=1)
    laplace = r_plus + r_minus + z_plus + z_minus - 4.0 * shifted
    diffused = shifted + coefficient * laplace
    after = jnp.roll(diffused, -1, axis=2)
    before = jnp.roll(diffused, 1, axis=2)
    out = (
        diffused
        - 0.5 * fraction * (after - before)
        + 0.5 * fraction * fraction * (after - 2.0 * diffused + before)
    )
    back = lax.all_to_all(out[None], "az", 3, 0, tiled=True)
    return back.reshape(nf, nrow, nz, width)


def solution(mesh):
    in_specs = (P(None, "rad", "vert", "az"), P("rad"), P("rad"), P())
    out_specs = P(None, "rad", "vert", "az")
    return jax.shard_map(
        per_device, mesh=mesh, in_specs=in_specs, out_specs=out_specs, check_vma=False
    )
```

time: 146 us -> 102 us (0.70); the launches traced: 143 us -> 102 us
  waiting for transfers between devices: 96.3 us -> 18 us
  local copies, waits for them, and re-layouts: 3.98 us -> 28.3 us
  blocking collectives: 0 us -> 20.5 us
  starting transfers between devices: 38.6 us -> 25.6 us
  other arithmetic: 4.01 us -> 9.13 us
    ppermute x11 -> x4, waiting for transfers between devices: 96.3 us -> 3.42 us  [the longest x1 3.41 us: per_device(): above = lax.ppermute(shifted[:, :1], 'vert', down)]
    ppermute x11 -> x4, starting transfers between devices: 38.6 us -> 8.15 us  [the longest x1 3.64 us: per_device(): prev_row = lax.ppermute(shifted[-1:], both, halo_pairs(nrad, halves, nf, 1))]
    all_to_all x0 -> x1, blocking collectives: none -> 20.5 us  [per_device(): back = lax.all_to_all(out[None], 'az', 3, 0, tiled=True)]
    all_to_all x0 -> x1, starting transfers between devices: none -> 17.5 us  [per_device(): y = lax.all_to_all(x, 'az', 0, 3, tiled=True)[0]]
    all_to_all x0 -> x1, waiting for transfers between devices: none -> 14.5 us  [per_device(): y = lax.all_to_all(x, 'az', 0, 3, tiled=True)[0]]
    unnamed x9 -> x2, local copies, waits for them, and re-layouts: 1.44 us -> 13.3 us
    all_to_all x0 -> x3, local copies, waits for them, and re-layouts: none -> 6.67 us  [the longest x2 6.36 us: per_device(): back = lax.all_to_all(out[None], 'az', 3, 0, tiled=True)]
    add x1, local copies, waits for them, and re-layouts: 0.89 us -> 4.66 us  [per_device(): diffused - 0.5 * fraction * (after - before)]
  transfers between devices with their start and end apart: 11 -> 5, of which waited for: 10 -> 2; matrix products, arithmetic and copies ran while one was open for 0% -> 3% of each run, Pallas kernels for 0% -> 0%
where the time goes in v1:
time: 102 us
  local copies, waits for them, and re-layouts  28.3 us (28%)
  starting transfers between devices  25.6 us (25%)
  blocking collectives  20.5 us (20%)
  waiting for transfers between devices  18 us (18%)
  other arithmetic  9.13 us (9%)
    all_to_all x1, blocking collectives, per_device(): back = lax.all_to_all(out[None], 'az', 3, 0, tiled=True)  20.5 us
    all_to_all x1, starting transfers between devices, per_device(): y = lax.all_to_all(x, 'az', 0, 3, tiled=True)[0]  17.5 us
    all_to_all x1, waiting for transfers between devices, per_device(): y = lax.all_to_all(x, 'az', 0, 3, tiled=True)[0]  14.5 us
    unnamed x2, local copies, waits for them, and re-layouts  13.3 us
    all_to_all x2, local copies, waits for them, and re-layouts, per_device(): back = lax.all_to_all(out[None], 'az', 3, 0, tiled=True)  6.36 us
    add x1, local copies, waits for them, and re-layouts, per_device(): diffused - 0.5 * fraction * (after - before)  4.66 us
    ppermute x1, starting transfers between devices, per_device(): prev_row = lax.ppermute(shifted[-1:], both, halo_pairs(nrad, halves, nf, 1))  3.64 us
    ppermute x1, waiting for transfers between devices, per_device(): above = lax.ppermute(shifted[:, :1], 'vert', down)  3.41 us
  transfers between devices with their start and end apart: 5, of which 2 were waited for; matrix products, arithmetic and copies ran while one was open for 3% of the time, Pallas kernels for 0%

profile of v1, /device:TPU:1, one launch (start us, length us, event | category | flops | bytes accessed | tf_op | source)
XLA Modules:
  0.0 101.9 jit_solution(15942968666282587873)
XLA Ops:
  0.0 17.5 %all-to-all-start = ((f32[16,8,8,128]{3,2,1,0:T(8,128)}), f32[16,8,8,128]{3,2,1,0:T(8,128)S(1)}, u32[]{:S(2)}, u32[]{:S(2)}) async-start(f32[16,8,8,128]{3,2,1,0:T(8,128)} %bitcast.86), calls=%async_computation | async-start | bytes 1048576 | tf_op jit(solution)/shard_map/all_to_all | solution.py:37
  17.5 1.2 %dynamic_slice.10 = f32[1]{0:T(128)} dynamic-slice(f32[8]{0:T(128)} %param.7, s32[]{:T(128)S(6)} %select_n.275), dynamic_slice_sizes={1} | dynamic-slice | bytes 12 | tf_op jit(solution)/shard_map/dynamic_slice | solution.py:44
  18.7 0.7 broadcast_multiply_fusion
  19.4 0.7 fusion.10
  20.2 14.5 %all-to-all-done = f32[16,8,8,128]{3,2,1,0:T(8,128)S(1)} async-done(((f32[16,8,8,128]{3,2,1,0:T(8,128)}), f32[16,8,8,128]{3,2,1,0:T(8,128)S(1)}, u32[]{:S(2)}, u32[]{:S(2)}) %all-to-all-start) | async-done | bytes 524320 | tf_op jit(solution)/shard_map/all_to_all | solution.py:37
  34.8 0.3 copy.297
  35.3 0.2 maximum_select_fusion
  35.7 0.2 maximum_select_fusion.1
  36.1 0.2 maximum_select_fusion.2
  36.5 0.2 maximum_select_fusion.3
  36.8 0.2 maximum_select_fusion.4
  37.2 0.2 maximum_select_fusion.5
  37.6 0.2 maximum_select_fusion.6
  38.3 0.1 maximum_select_fusion.9
  38.6 0.1 maximum_select_fusion.21
  38.8 0.1 fusion.33
  39.0 1.9 %collective-permute-start = (f32[1,8,2048]{2,1,0:T(8,128)S(1)}, f32[1,8,2048]{2,1,0:T(8,128)S(1)}, u32[]{:S(2)}, u32[]{:S(2)}) collective-permute-start(f32[1,8,2048]{2,1,0:T(8,128)S(1)} %get-tuple-element.67), channel_id=1, source_target_pairs={{64,0},{192,128},{320,256},{448,384},{576,512},{704,640},{832,768}... | collective-permute-start | bytes 196616 | tf_op jit(solution)/shard_map/ppermute | solution.py:51
  40.9 3.6 %collective-permute-start.1 = (f32[1,8,2048]{2,1,0:T(8,128)S(1)}, f32[1,8,2048]{2,1,0:T(8,128)S(1)}, u32[]{:S(2)}, u32[]{:S(2)}) collective-permute-start(f32[1,8,2048]{2,1,0:T(8,128)S(1)} %get-tuple-element.68), channel_id=1, source_target_pairs={{0,64},{64,8},{128,192},{192,136},{256,320},{320,264},{384,448},{4... | collective-permute-start | bytes 196616 | tf_op jit(solution)/shard_map/ppermute | solution.py:50
  44.6 1.3 %collective-permute-start.3 = (f32[8,1,2048]{2,0,1:T(8,128)S(1)}, f32[8,1,2048]{2,0,1:T(8,128)S(1)}, u32[]{:S(2)}, u32[]{:S(2)}) collective-permute-start(f32[8,1,2048]{2,0,1:T(8,128)S(1)} %copy.283), channel_id=1, source_target_pairs={{0,1},{1,2},{2,3},{3,4},{4,5},{5,6},{6,7},{8,9},{9,10},{10,11},{11... | collective-permute-start | bytes 196616 | tf_op jit(solution)/shard_map/ppermute | solution.py:54
  45.9 1.3 %collective-permute-start.2 = (f32[8,1,2048]{2,0,1:T(8,128)S(1)}, f32[8,1,2048]{2,0,1:T(8,128)S(1)}, u32[]{:S(2)}, u32[]{:S(2)}) collective-permute-start(f32[8,1,2048]{2,0,1:T(8,128)S(1)} %copy.281), channel_id=1, source_target_pairs={{1,0},{2,1},{3,2},{4,3},{5,4},{6,5},{7,6},{9,8},{10,9},{11,10},{12... | collective-permute-start | bytes 196616 | tf_op jit(solution)/shard_map/ppermute | solution.py:55
  47.2 0.2 fusion.34
  47.5 3.4 %collective-permute-done.2 = f32[8,1,2048]{2,0,1:T(8,128)S(1)} collective-permute-done((f32[8,1,2048]{2,0,1:T(8,128)S(1)}, f32[8,1,2048]{2,0,1:T(8,128)S(1)}, u32[]{:S(2)}, u32[]{:S(2)}) %collective-permute-start.2) | collective-permute-done | bytes 65568 | tf_op jit(solution)/shard_map/ppermute | solution.py:55
  51.0 1.0 fusion.9
  52.1 0.2 slice_bitcast_fusion.1
  52.5 2.7 %multiply_add_fusion = f32[1,8,8,2048]{3,2,1,0:T(8,128)S(1)} fusion(f32[1,8,7,2048]{3,2,1,0:T(8,128)S(1)} %get-tuple-element.61, f32[1,8,1,2048]{3,2,1,0:T(1,128)S(1)} %copy.284, f32[1,8,1,2048]{3,2,1,0:T(1,128)S(1)} %copy.282, f32[1,8,7,2048]{3,2,1,0:T(8,128)S(1)} %get-tuple-element.60, f32[1,7,8,2048]{3,2,1,0:T(8,128)S(1)} %get-tuple-element.65, ...), kind=kLoop, calls=%fused_computation.38 | loop fusion | flops 5636096 | bytes 9961628 | tf_op jit(solution)/shard_map/add | solution.py:66
  55.2 4.7 %copy.289 = f32[1,8,8,2048]{2,1,0,3:T(8,128)} copy(f32[1,8,8,2048]{3,2,1,0:T(8,128)S(1)} %multiply_add_fusion) | data formatting | bytes 1048576 | tf_op jit(solution)/shard_map/add | solution.py:66
  59.9 6.6 %reshape.600 = f32[16,1,8192]{2,1,0:T(1,128)S(1)} reshape(f32[2048,1,8,8]{3,2,1,0:T(8,128)} %bitcast.82) | data formatting | bytes 1048576
  66.5 20.5 %all_to_all.30 = f32[16,1,8192]{2,1,0:T(1,128)S(1)} all-to-all(f32[16,1,8192]{2,1,0:T(1,128)S(1)} %reshape.600), channel_id=1, replica_groups=mesh['az'=16,'rad'=8,'vert'=8] {'az'}, dimensions={0} | all-to-all | bytes 1048576 | tf_op jit(solution)/shard_map/all_to_all | solution.py:70
  86.9 0.5 broadcast.263
  87.5 1.9 %reduce = f32[16,8192]{1,0:T(8,128)S(1)} reduce(f32[16,1,8192]{2,1,0:T(1,128)S(1)} %all_to_all.30, f32[]{:T(128)} %broadcast.263), dimensions={1}, to_apply=%all_to_all.25.reduce_sub_computation | reduce | bytes 1048580 | tf_op jit(solution)/shard_map/all_to_all | solution.py:70
  89.4 6.7 %reshape.601 = f32[2048,1,8,8]{3,2,1,0:T(8,128)} reshape(f32[16,8192]{1,0:T(8,128)S(1)} %reduce) | data formatting | bytes 1048576
  96.0 5.8 %copy.290 = f32[16,1,8,8,128]{4,3,2,0,1:T(8,128)} copy(f32[16,1,8,8,128]{3,2,4,0,1:T(8,128)} %bitcast.83) | data formatting | bytes 1048576 | tf_op jit(solution)/shard_map/all_to_all | solution.py:70
  (37 shorter events, 2.2 us)
Async XLA Ops:
  0.0 34.8 %all-to-all-start = ((f32[16,8,8,128]{3,2,1,0:T(8,128)}), f32[16,8,8,128]{3,2,1,0:T(8,128)S(1)}, u32[]{:S(2)}, u32[]{:S(2)}) async-start(f32[16,8,8,128]{3,2,1,0:T(8,128)} %bitcast.86), calls=%async_computation | async-start | bytes 1048576 | tf_op jit(solution)/shard_map/all_to_all | solution.py:37
  39.0 12.0 %collective-permute-start = (f32[1,8,2048]{2,1,0:T(8,128)S(1)}, f32[1,8,2048]{2,1,0:T(8,128)S(1)}, u32[]{:S(2)}, u32[]{:S(2)}) collective-permute-start(f32[1,8,2048]{2,1,0:T(8,128)S(1)} %get-tuple-element.67), channel_id=1, source_target_pairs={{64,0},{192,128},{320,256},{448,384},{576,512},{704,640},{832,768}... | collective-permute-start | bytes 196616 | tf_op jit(solution)/shard_map/ppermute | solution.py:51
  40.9 10.1 %collective-permute-start.1 = (f32[1,8,2048]{2,1,0:T(8,128)S(1)}, f32[1,8,2048]{2,1,0:T(8,128)S(1)}, u32[]{:S(2)}, u32[]{:S(2)}) collective-permute-start(f32[1,8,2048]{2,1,0:T(8,128)S(1)} %get-tuple-element.68), channel_id=1, source_target_pairs={{0,64},{64,8},{128,192},{192,136},{256,320},{320,264},{384,448},{4... | collective-permute-start | bytes 196616 | tf_op jit(solution)/shard_map/ppermute | solution.py:50
  44.6 2.8 %collective-permute-start.3 = (f32[8,1,2048]{2,0,1:T(8,128)S(1)}, f32[8,1,2048]{2,0,1:T(8,128)S(1)}, u32[]{:S(2)}, u32[]{:S(2)}) collective-permute-start(f32[8,1,2048]{2,0,1:T(8,128)S(1)} %copy.283), channel_id=1, source_target_pairs={{0,1},{1,2},{2,3},{3,4},{4,5},{5,6},{6,7},{8,9},{9,10},{10,11},{11... | collective-permute-start | bytes 196616 | tf_op jit(solution)/shard_map/ppermute | solution.py:54
  45.9 5.0 %collective-permute-start.2 = (f32[8,1,2048]{2,0,1:T(8,128)S(1)}, f32[8,1,2048]{2,0,1:T(8,128)S(1)}, u32[]{:S(2)}, u32[]{:S(2)}) collective-permute-start(f32[8,1,2048]{2,0,1:T(8,128)S(1)} %copy.281), channel_id=1, source_target_pairs={{1,0},{2,1},{3,2},{4,3},{5,4},{6,5},{7,6},{9,8},{10,9},{11,10},{12... | collective-permute-start | bytes 196616 | tf_op jit(solution)/shard_map/ppermute | solution.py:55

commit v2 on v1

--- a/solution.py
+++ b/solution.py
@@ -34,7 +34,8 @@
     halves = loop // nf
     rows = nrow // halves
     x = fields.reshape(nf * halves, rows, nz, width)
-    y = lax.all_to_all(x, "az", 0, 3, tiled=True)[0]
+    y = lax.all_to_all(x, "az", 0, 0, tiled=True)
+    y = jnp.transpose(y, (1, 2, 0, 3)).reshape(rows, nz, loop * width)
     length = y.shape[2]
     me = lax.axis_index("az")
     f = me // halves
@@ -67,7 +68,8 @@
         - 0.5 * fraction * (after - before)
         + 0.5 * fraction * fraction * (after - 2.0 * diffused + before)
     )
-    back = lax.all_to_all(out[None], "az", 3, 0, tiled=True)
+    blocks = jnp.transpose(out.reshape(rows, nz, loop, width), (2, 0, 1, 3))
+    back = lax.all_to_all(blocks, "az", 0, 0, tiled=True)
     return back.reshape(nf, nrow, nz, width)
 
 

time: 102 us -> 93.6 us (0.918)
  local copies, waits for them, and re-layouts: 28.3 us -> 16 us
  other arithmetic: 9.13 us -> 12.9 us
  starting transfers between devices: 25.6 us -> 28.9 us
  waiting for transfers between devices: 18 us -> 15.1 us
    unnamed x2 -> x69, local copies, waits for them, and re-layouts: 13.3 us -> 4.01 us
    unnamed x0 -> x11, other arithmetic: none -> 8.36 us
    all_to_all x3 -> x0, local copies, waits for them, and re-layouts: 6.67 us -> none  [the longest x2 6.36 us: per_device(): back = lax.all_to_all(out[None], 'az', 3, 0, tiled=True)]
    add x1 -> x0, local copies, waits for them, and re-layouts: 4.66 us -> none  [per_device(): diffused - 0.5 * fraction * (after - before)]
    concatenate x1 -> x3, local copies, waits for them, and re-layouts: 0.07 us -> 4 us  [per_device(): z_plus = jnp.concatenate([shifted[:, 1:], above], axis=1)]
    ppermute x1, waiting for transfers between devices: 3.41 us -> 0.01 us  [per_device(): above = lax.ppermute(shifted[:, :1], 'vert', down)]
    ppermute x1, starting transfers between devices: 1.29 us -> 4.61 us  [per_device(): below = lax.ppermute(shifted[:, -1:], 'vert', up)]
    concatenate x1 -> x3, local copies, waits for them, and re-layouts: 0.07 us -> 3.11 us  [per_device(): z_minus = jnp.concatenate([below, shifted[:, :-1]], axis=1)]
  transfers between devices with their start and end apart: 5 -> 5, of which waited for: 2 -> 1; matrix products, arithmetic and copies ran while one was open for 3% -> 9% of each run, Pallas kernels for 0% -> 0%
where the time goes in v2:
time: 93.6 us; the launch traced here: 93 us
  starting transfers between devices  28.9 us (31%)
  blocking collectives  19.6 us (21%)
  local copies, waits for them, and re-layouts  16 us (17%)
  waiting for transfers between devices  15.1 us (16%)
  other arithmetic  12.9 us (14%)
    all_to_all x1, blocking collectives, per_device(): back = lax.all_to_all(blocks, 'az', 0, 0, tiled=True)  19.6 us
    all_to_all x1, starting transfers between devices, per_device(): y = lax.all_to_all(x, 'az', 0, 0, tiled=True)  17.5 us
    all_to_all x1, waiting for transfers between devices, per_device(): y = lax.all_to_all(x, 'az', 0, 0, tiled=True)  15.1 us
    unnamed x11, other arithmetic  8.36 us
    ppermute x1, starting transfers between devices, per_device(): below = lax.ppermute(shifted[:, -1:], 'vert', up)  4.61 us
    unnamed x69, local copies, waits for them, and re-layouts  4.01 us
    concatenate x3, local copies, waits for them, and re-layouts, per_device(): z_plus = jnp.concatenate([shifted[:, 1:], above], axis=1)  4 us
    ppermute x1, starting transfers between devices, per_device(): prev_row = lax.ppermute(shifted[-1:], both, halo_pairs(nrad, halves, nf, 1))  3.64 us
  transfers between devices with their start and end apart: 5, of which 1 were waited for; matrix products, arithmetic and copies ran while one was open for 9% of the time, Pallas kernels for 0%

profile of v2, /device:TPU:1, one launch (start us, length us, event | category | flops | bytes accessed | tf_op | source)
XLA Modules:
  0.0 93.0 jit_solution(3185214350126621970)
XLA Ops:
  0.0 17.5 %all-to-all-start = ((f32[16,8,8,128]{3,2,1,0:T(8,128)}), f32[16,8,8,128]{3,2,1,0:T(8,128)S(1)}, u32[]{:S(2)}, u32[]{:S(2)}) async-start(f32[16,8,8,128]{3,2,1,0:T(8,128)} %bitcast.157), calls=%async_computation | async-start | bytes 1048576 | tf_op jit(solution)/shard_map/all_to_all | solution.py:37
  17.5 0.6 copy-done.32
  18.1 0.7 dynamic_slice.10
  19.7 15.1 %all-to-all-done = f32[16,8,8,128]{3,2,1,0:T(8,128)S(1)} async-done(((f32[16,8,8,128]{3,2,1,0:T(8,128)}), f32[16,8,8,128]{3,2,1,0:T(8,128)S(1)}, u32[]{:S(2)}, u32[]{:S(2)}) %all-to-all-start) | async-done | bytes 524320 | tf_op jit(solution)/shard_map/all_to_all | solution.py:37
  35.5 1.0 %fusion.39 = (f32[8,1,16,8,128]{4,3,2,1,0:T(8,128)}, f32[8,8,2048]{2,1,0:T(8,128)S(1)}) fusion(f32[8,8,2044]{2,1,0:T(8,128)S(1)} %bitcast.150, f32[8,8,4]{2,1,0:T(8,128)S(1)} %slice.164, f32[8,8,2048]{2,1,0:T(8,128)S(1)} %get-tuple-element.20, pred[8]{0:T(512)(128)(4,1)S(1)} %get-tuple-element.49), kind=kLoop, calls=%fused_computation.61 | loop fusion | flops 262144 | bytes 2097160
  36.6 1.0 %fusion.37 = (f32[8,1,16,8,128]{4,3,2,1,0:T(8,128)}, f32[8,8,2048]{2,1,0:T(8,128)S(1)}) fusion(f32[8,8,2040]{2,1,0:T(8,128)S(1)} %bitcast.151, f32[8,8,8]{2,1,0:T(8,128)S(1)} %slice.166, f32[8,8,2048]{2,1,0:T(8,128)S(1)} %get-tuple-element.18, pred[8]{0:T(512)(128)(4,1)S(1)} %get-tuple-element.51), kind=kLoop, calls=%fused_computation.59 | loop fusion | flops 262144 | bytes 2097160
  37.7 1.0 %fusion.35 = (f32[8,1,16,8,128]{4,3,2,1,0:T(8,128)}, f32[8,8,2048]{2,1,0:T(8,128)S(1)}) fusion(f32[8,8,2032]{2,1,0:T(8,128)S(1)} %bitcast.152, f32[8,8,16]{2,1,0:T(8,128)S(1)} %slice.168, f32[8,8,2048]{2,1,0:T(8,128)S(1)} %get-tuple-element.16, pred[8]{0:T(512)(128)(4,1)S(1)} %get-tuple-element.54), kind=kLoop, calls=%fused_computation.57 | loop fusion | flops 262144 | bytes 2097160
  38.8 1.0 %fusion.33 = (f32[8,1,16,8,128]{4,3,2,1,0:T(8,128)}, f32[8,8,2048]{2,1,0:T(8,128)S(1)}) fusion(f32[8,8,2016]{2,1,0:T(8,128)S(1)} %bitcast.153, f32[8,8,32]{2,1,0:T(8,128)S(1)} %slice.170, f32[8,8,2048]{2,1,0:T(8,128)S(1)} %get-tuple-element.14, pred[8]{0:T(512)(128)(4,1)S(1)} %get-tuple-element.55), kind=kLoop, calls=%fused_computation.55 | loop fusion | flops 262144 | bytes 2097160
  39.9 1.0 %fusion.31 = (f32[8,1,16,8,128]{4,3,2,1,0:T(8,128)}, f32[8,8,2048]{2,1,0:T(8,128)S(1)}) fusion(f32[8,8,1984]{2,1,0:T(8,128)S(1)} %bitcast.154, f32[8,8,64]{2,1,0:T(8,128)S(1)} %slice.172, f32[8,8,2048]{2,1,0:T(8,128)S(1)} %get-tuple-element.12, pred[8]{0:T(512)(128)(4,1)S(1)} %get-tuple-element.48), kind=kLoop, calls=%fused_computation.53 | loop fusion | flops 262144 | bytes 2097160
  41.0 0.9 fusion.29
  41.9 0.9 fusion.27
  42.9 0.8 fusion.25
  43.9 1.2 %slice_bitcast_fusion.3 = (f32[7,1,16,8,128]{4,3,2,1,0:T(8,128)S(1)}, f32[7,1,16,8,128]{4,3,2,1,0:T(8,128)S(1)}, f32[7,8,2048]{2,1,0:T(8,128)}, f32[7,8,2048]{2,1,0:T(8,128)}) fusion(f32[8,8,2048]{2,1,0:T(8,128)S(1)} %maximum_select_fusion), kind=kLoop, calls=%fused_computation.159 | loop fusion | bytes 2752512
  45.2 0.7 fusion.71
  45.9 0.7 fusion.69
  46.6 1.9 %collective-permute-start = (f32[1,8,2048]{2,1,0:T(8,128)}, f32[1,8,2048]{2,1,0:T(8,128)S(1)}, u32[]{:S(2)}, u32[]{:S(2)}) collective-permute-start(f32[1,8,2048]{2,1,0:T(8,128)} %get-tuple-element.46), channel_id=1, source_target_pairs={{64,0},{192,128},{320,256},{448,384},{576,512},{704,640},{832,768}... | collective-permute-start | bytes 196616 | tf_op jit(solution)/shard_map/ppermute | solution.py:52
  48.5 3.6 %collective-permute-start.1 = (f32[1,8,2048]{2,1,0:T(8,128)}, f32[1,8,2048]{2,1,0:T(8,128)S(1)}, u32[]{:S(2)}, u32[]{:S(2)}) collective-permute-start(f32[1,8,2048]{2,1,0:T(8,128)} %get-tuple-element.45), channel_id=1, source_target_pairs={{0,64},{64,8},{128,192},{192,136},{256,320},{320,264},{384,448},{4... | collective-permute-start | bytes 196616 | tf_op jit(solution)/shard_map/ppermute | solution.py:51
  52.2 1.3 %collective-permute-start.2 = (f32[8,1,2048]{2,1,0:T(1,128)}, f32[8,1,2048]{2,1,0:T(1,128)}, u32[]{:S(2)}, u32[]{:S(2)}) collective-permute-start(f32[8,1,2048]{2,1,0:T(1,128)} %get-tuple-element.42), channel_id=1, source_target_pairs={{1,0},{2,1},{3,2},{4,3},{5,4},{6,5},{7,6},{9,8},{10,9},{11,10},{12... | collective-permute-start | bytes 196616 | tf_op jit(solution)/shard_map/ppermute | solution.py:56
  53.5 4.6 %collective-permute-start.3 = (f32[8,1,2048]{2,1,0:T(1,128)}, f32[8,1,2048]{2,1,0:T(1,128)}, u32[]{:S(2)}, u32[]{:S(2)}) collective-permute-start(f32[8,1,2048]{2,1,0:T(1,128)} %get-tuple-element.41), channel_id=1, source_target_pairs={{0,1},{1,2},{2,3},{3,4},{4,5},{5,6},{6,7},{8,9},{9,10},{10,11},{11... | collective-permute-start | bytes 196616 | tf_op jit(solution)/shard_map/ppermute | solution.py:55
  58.1 1.0 %copy_bitcast_fusion.1 = (f32[7,8,16,128]{3,1,0,2:T(8,128)}, f32[7,8,16,128]{3,1,0,2:T(8,128)}) fusion(f32[7,1,16,8,128]{4,3,2,1,0:T(8,128)S(1)} %get-tuple-element.34, f32[7,1,16,8,128]{4,3,2,1,0:T(8,128)S(1)} %get-tuple-element.33), kind=kLoop, calls=%fused_computation.45 | loop fusion | bytes 1835008 | tf_op jit(solution)/shard_map/concatenate | solution.py:59
  59.1 0.7 copy_bitcast_fusion.3
  59.8 0.9 %reshape.50 = f32[8,7,16,128]{3,2,1,0:T(8,128)} reshape(f32[8,7,2048]{2,1,0:T(8,128)S(1)} %get-tuple-element.44) | data formatting | bytes 917504 | tf_op jit(solution)/shard_map/concatenate | solution.py:60
  60.8 2.0 %copy.27 = f32[8,7,16,128]{3,1,0,2:T(8,128)} copy(f32[8,7,16,128]{3,2,1,0:T(8,128)} %reshape.50) | data formatting | bytes 917504 | tf_op jit(solution)/shard_map/concatenate | solution.py:60
  62.8 0.9 %reshape.51 = f32[8,7,16,128]{3,2,1,0:T(8,128)} reshape(f32[8,7,2048]{2,1,0:T(8,128)S(1)} %get-tuple-element.43) | data formatting | bytes 917504 | tf_op jit(solution)/shard_map/concatenate | solution.py:61
  63.7 1.3 %copy.31 = f32[8,7,16,128]{3,1,0,2:T(8,128)S(1)} copy(f32[8,7,16,128]{3,2,1,0:T(8,128)} %reshape.51) | data formatting | bytes 917504 | tf_op jit(solution)/shard_map/concatenate | solution.py:61
  65.1 2.0 %fusion.24 = f32[8,8,2048]{2,1,0:T(8,128)S(1)} fusion(f32[8,8,2048]{2,1,0:T(8,128)S(1)} %maximum_select_fusion, f32[1,8,2048]{2,1,0:T(8,128)S(1)} %collective-permute-done, f32[7,8,2048]{2,1,0:T(8,128)S(1)} %copy-done.10, f32[7,8,2048]{2,1,0:T(8,128)S(1)} %copy-done.9, f32[1,8,2048]{2,1,0:T(8,128)S(1)} %collective-permute-done.1, ...), kind=kLoop, calls=%fused_computation.42 | loop fusion | flops 1441792 | bytes 3145732 | tf_op jit(solution)/shard_map/add | solution.py:63
  67.4 1.1 %copy.28 = f32[8,1,16,128]{3,1,0,2:T(1,128)S(1)} copy(f32[8,1,16,128]{3,2,1,0:T(8,128)} %bitcast.5) | data formatting | bytes 131072 | tf_op jit(solution)/shard_map/concatenate | solution.py:60
  68.5 0.9 copy.30
  69.8 0.6 copy-done
  71.0 1.7 %fusion.3 = f32[16,8,8,128]{3,2,1,0:T(8,128)S(1)} fusion(f32[8,1,16,8,128]{4,3,2,1,0:T(8,128)S(1)} %get-tuple-element.64, f32[8,1,16,8,128]{4,3,2,1,0:T(8,128)S(1)} %get-tuple-element.63, f32[8,7,16,128]{3,1,0,2:T(8,128)S(1)} %copy.31, f32[8,1,16,128]{3,1,0,2:T(1,128)S(1)} %copy.30, f32[8,1,16,128]{3,1,0,2:T(1,128)S(1)} %copy.28, ...), kind=kLoop, calls=%fused_computation.6 | loop fusion | flops 4063232 | bytes 9961628 | tf_op jit(solution)/shard_map/transpose | solution.py:71
  72.7 19.6 %all_to_all.10 = f32[16,8,8,128]{3,2,1,0:T(8,128)S(1)} all-to-all(f32[16,8,8,128]{3,2,1,0:T(8,128)S(1)} %fusion.3), channel_id=1, replica_groups=mesh['az'=16,'rad'=8,'vert'=8] {'az'}, dimensions={0} | all-to-all | bytes 1048576 | tf_op jit(solution)/shard_map/all_to_all | solution.py:72
  92.2 0.8 copy.97
  (93 shorter events, 3.3 us)
Async XLA Ops:
  0.0 34.8 %all-to-all-start = ((f32[16,8,8,128]{3,2,1,0:T(8,128)}), f32[16,8,8,128]{3,2,1,0:T(8,128)S(1)}, u32[]{:S(2)}, u32[]{:S(2)}) async-start(f32[16,8,8,128]{3,2,1,0:T(8,128)} %bitcast.157), calls=%async_computation | async-start | bytes 1048576 | tf_op jit(solution)/shard_map/all_to_all | solution.py:37
  19.6 15.3 %copy-start.26 = (pred[8]{0:T(512)(128)(4,1)}, pred[8]{0:T(512)(128)(4,1)S(1)}, u32[]{:S(2)}) copy-start(pred[8]{0:T(512)(128)(4,1)S(1)} %get-tuple-element.56) | copy-start | bytes 28
  19.6 15.6 %copy-start.20 = (pred[8]{0:T(512)(128)(4,1)}, pred[8]{0:T(512)(128)(4,1)S(1)}, u32[]{:S(2)}) copy-start(pred[8]{0:T(512)(128)(4,1)S(1)} %get-tuple-element.53) | copy-start | bytes 28
  19.6 17.0 %copy-start.16 = (pred[8]{0:T(512)(128)(4,1)}, pred[8]{0:T(512)(128)(4,1)S(1)}, u32[]{:S(2)}) copy-start(pred[8]{0:T(512)(128)(4,1)S(1)} %get-tuple-element.51) | copy-start | bytes 28
  19.6 18.1 %copy-start.22 = (pred[8]{0:T(512)(128)(4,1)}, pred[8]{0:T(512)(128)(4,1)S(1)}, u32[]{:S(2)}) copy-start(pred[8]{0:T(512)(128)(4,1)S(1)} %get-tuple-element.54) | copy-start | bytes 28
  19.6 19.2 %copy-start.24 = (pred[8]{0:T(512)(128)(4,1)}, pred[8]{0:T(512)(128)(4,1)S(1)}, u32[]{:S(2)}) copy-start(pred[8]{0:T(512)(128)(4,1)S(1)} %get-tuple-element.55) | copy-start | bytes 28
  19.6 21.4 %copy-start.14 = (pred[8]{0:T(512)(128)(4,1)}, pred[8]{0:T(512)(128)(4,1)S(1)}, u32[]{:S(2)}) copy-start(pred[8]{0:T(512)(128)(4,1)S(1)} %get-tuple-element.50) | copy-start | bytes 28
  19.6 22.3 %copy-start.18 = (pred[8]{0:T(512)(128)(4,1)}, pred[8]{0:T(512)(128)(4,1)S(1)}, u32[]{:S(2)}) copy-start(pred[8]{0:T(512)(128)(4,1)S(1)} %get-tuple-element.52) | copy-start | bytes 28
  46.6 18.4 %collective-permute-start = (f32[1,8,2048]{2,1,0:T(8,128)}, f32[1,8,2048]{2,1,0:T(8,128)S(1)}, u32[]{:S(2)}, u32[]{:S(2)}) collective-permute-start(f32[1,8,2048]{2,1,0:T(8,128)} %get-tuple-element.46), channel_id=1, source_target_pairs={{64,0},{192,128},{320,256},{448,384},{576,512},{704,640},{832,768}... | collective-permute-start | bytes 196616 | tf_op jit(solution)/shard_map/ppermute | solution.py:52
  48.5 16.5 %collective-permute-start.1 = (f32[1,8,2048]{2,1,0:T(8,128)}, f32[1,8,2048]{2,1,0:T(8,128)S(1)}, u32[]{:S(2)}, u32[]{:S(2)}) collective-permute-start(f32[1,8,2048]{2,1,0:T(8,128)} %get-tuple-element.45), channel_id=1, source_target_pairs={{0,64},{64,8},{128,192},{192,136},{256,320},{320,264},{384,448},{4... | collective-permute-start | bytes 196616 | tf_op jit(solution)/shard_map/ppermute | solution.py:51
  52.2 12.8 %collective-permute-start.2 = (f32[8,1,2048]{2,1,0:T(1,128)}, f32[8,1,2048]{2,1,0:T(1,128)}, u32[]{:S(2)}, u32[]{:S(2)}) collective-permute-start(f32[8,1,2048]{2,1,0:T(1,128)} %get-tuple-element.42), channel_id=1, source_target_pairs={{1,0},{2,1},{3,2},{4,3},{5,4},{6,5},{7,6},{9,8},{10,9},{11,10},{12... | collective-permute-start | bytes 196616 | tf_op jit(solution)/shard_map/ppermute | solution.py:56
  53.5 11.5 %collective-permute-start.3 = (f32[8,1,2048]{2,1,0:T(1,128)}, f32[8,1,2048]{2,1,0:T(1,128)}, u32[]{:S(2)}, u32[]{:S(2)}) collective-permute-start(f32[8,1,2048]{2,1,0:T(1,128)} %get-tuple-element.41), channel_id=1, source_target_pairs={{0,1},{1,2},{2,3},{3,4},{4,5},{5,6},{6,7},{8,9},{9,10},{10,11},{11... | collective-permute-start | bytes 196616 | tf_op jit(solution)/shard_map/ppermute | solution.py:55
  63.7 1.3 %copy-start.9 = (f32[7,8,2048]{2,1,0:T(8,128)S(1)}, f32[7,8,2048]{2,1,0:T(8,128)}, u32[]{:S(2)}) copy-start(f32[7,8,2048]{2,1,0:T(8,128)} %get-tuple-element.35) | copy-start | bytes 1376260
  63.7 1.3 %copy-start.10 = (f32[7,8,2048]{2,1,0:T(8,128)S(1)}, f32[7,8,2048]{2,1,0:T(8,128)}, u32[]{:S(2)}) copy-start(f32[7,8,2048]{2,1,0:T(8,128)} %get-tuple-element.36) | copy-start | bytes 1376260
  65.1 4.7 %copy-start.8 = (f32[8,7,16,128]{3,1,0,2:T(8,128)S(1)}, f32[8,7,16,128]{3,1,0,2:T(8,128)}, u32[]{:S(2)}) copy-start(f32[8,7,16,128]{3,1,0,2:T(8,128)} %copy.27) | copy-start | bytes 1376260
  65.1 4.7 %copy-start.12 = (f32[7,8,16,128]{3,1,0,2:T(8,128)S(1)}, f32[7,8,16,128]{3,1,0,2:T(8,128)}, u32[]{:S(2)}) copy-start(f32[7,8,16,128]{3,1,0,2:T(8,128)} %get-tuple-element.62) | copy-start | bytes 1376260
  65.1 4.7 %copy-start.13 = (f32[8,8,8,128]{3,1,0,2:T(8,128)S(1)}, f32[8,8,8,128]{3,1,0,2:T(8,128)}, u32[]{:S(2)}) copy-start(f32[8,8,8,128]{3,1,0,2:T(8,128)} %get-tuple-element.60) | copy-start | bytes 786436
  67.1 2.7 %copy-start.4 = (f32[8,1,16,8,128]{4,3,2,1,0:T(8,128)S(1)}, f32[8,1,16,8,128]{4,3,2,1,0:T(8,128)}, u32[]{:S(2)}) copy-start(f32[8,1,16,8,128]{4,3,2,1,0:T(8,128)} %get-tuple-element.9) | copy-start | bytes 1572868
  67.1 2.7 %copy-start.5 = (f32[8,1,16,8,128]{4,3,2,1,0:T(8,128)S(1)}, f32[8,1,16,8,128]{4,3,2,1,0:T(8,128)}, u32[]{:S(2)}) copy-start(f32[8,1,16,8,128]{4,3,2,1,0:T(8,128)} %get-tuple-element.31) | copy-start | bytes 1572868
  67.1 2.7 %copy-start.6 = (f32[8,1,16,8,128]{4,3,2,1,0:T(8,128)S(1)}, f32[8,1,16,8,128]{4,3,2,1,0:T(8,128)}, u32[]{:S(2)}) copy-start(f32[8,1,16,8,128]{4,3,2,1,0:T(8,128)} %get-tuple-element.29) | copy-start | bytes 1572868
  67.1 2.7 %copy-start.7 = (f32[8,1,16,8,128]{4,3,2,1,0:T(8,128)S(1)}, f32[8,1,16,8,128]{4,3,2,1,0:T(8,128)}, u32[]{:S(2)}) copy-start(f32[8,1,16,8,128]{4,3,2,1,0:T(8,128)} %get-tuple-element.27) | copy-start | bytes 1572868
  67.3 2.5 %copy-start.11 = (f32[7,8,16,128]{3,1,0,2:T(8,128)S(1)}, f32[7,8,16,128]{3,1,0,2:T(8,128)}, u32[]{:S(2)}) copy-start(f32[7,8,16,128]{3,1,0,2:T(8,128)} %get-tuple-element.61) | copy-start | bytes 1376260
  69.4 1.3 %copy-start.2 = (f32[8,1,16,8,128]{4,3,2,1,0:T(8,128)S(1)}, f32[8,1,16,8,128]{4,3,2,1,0:T(8,128)}, u32[]{:S(2)}) copy-start(f32[8,1,16,8,128]{4,3,2,1,0:T(8,128)} %get-tuple-element.13) | copy-start | bytes 1572868
  69.4 1.5 %copy-start.3 = (f32[8,1,16,8,128]{4,3,2,1,0:T(8,128)S(1)}, f32[8,1,16,8,128]{4,3,2,1,0:T(8,128)}, u32[]{:S(2)}) copy-start(f32[8,1,16,8,128]{4,3,2,1,0:T(8,128)} %get-tuple-element.11) | copy-start | bytes 1572868
  69.4 1.5 %copy-start.21 = (pred[8]{0:T(512)(128)(4,1)S(1)}, pred[8]{0:T(512)(128)(4,1)}, u32[]{:S(2)}) copy-start(pred[8]{0:T(512)(128)(4,1)} %copy-done.20) | copy-start | bytes 28
  69.4 1.5 %copy-start.23 = (pred[8]{0:T(512)(128)(4,1)S(1)}, pred[8]{0:T(512)(128)(4,1)}, u32[]{:S(2)}) copy-start(pred[8]{0:T(512)(128)(4,1)} %copy-done.22) | copy-start | bytes 28
  69.4 1.5 %copy-start.25 = (pred[8]{0:T(512)(128)(4,1)S(1)}, pred[8]{0:T(512)(128)(4,1)}, u32[]{:S(2)}) copy-start(pred[8]{0:T(512)(128)(4,1)} %copy-done.24) | copy-start | bytes 28
  69.5 1.5 %copy-start.27 = (pred[8]{0:T(512)(128)(4,1)S(1)}, pred[8]{0:T(512)(128)(4,1)}, u32[]{:S(2)}) copy-start(pred[8]{0:T(512)(128)(4,1)} %copy-done.26) | copy-start | bytes 28
  69.5 1.5 %copy-start.28 = (f32[8]{0:T(128)S(1)}, f32[8]{0:T(128)}, u32[]{:S(2)}) copy-start(f32[8]{0:T(128)} %get-tuple-element.57) | copy-start | bytes 100
  69.5 1.5 %copy-start.29 = (f32[8]{0:T(128)S(1)}, f32[8]{0:T(128)}, u32[]{:S(2)}) copy-start(f32[8]{0:T(128)} %get-tuple-element.58) | copy-start | bytes 100
  69.7 1.2 %copy-start.15 = (pred[8]{0:T(512)(128)(4,1)S(1)}, pred[8]{0:T(512)(128)(4,1)}, u32[]{:S(2)}) copy-start(pred[8]{0:T(512)(128)(4,1)} %copy-done.14) | copy-start | bytes 28
  69.7 1.2 %copy-start.17 = (pred[8]{0:T(512)(128)(4,1)S(1)}, pred[8]{0:T(512)(128)(4,1)}, u32[]{:S(2)}) copy-start(pred[8]{0:T(512)(128)(4,1)} %copy-done.16) | copy-start | bytes 28
  (6 other events, 5.4 us)

commit v3 on v2

v3 whole, which is shorter than its diff:
```python
import jax
import jax.numpy as jnp
from jax import lax
from jax.experimental import pallas as pl
from jax.experimental.pallas import tpu as pltpu
from jax.sharding import PartitionSpec as P


def shift_kernel(amount_ref, x_ref, o_ref, last_ref, first_ref, low_ref, high_ref):
    nblk, rows, nz, width = x_ref.shape
    lane = lax.broadcasted_iota(jnp.int32, (nz, width), 1)
    for k in range(rows):
        s = amount_ref[k]
        b = s // width
        rem = s % width
        late = lane >= width - rem
        for j in range(nblk):
            near = x_ref[(j - b + nblk) % nblk, k]
            far = x_ref[(j - b - 1 + 2 * nblk) % nblk, k]
            v = pltpu.roll(jnp.where(late, far, near), rem, 1)
            cols = slice(j * width, (j + 1) * width)
            o_ref[k, :, cols] = v
            low_ref[k : k + 1, cols] = v[0:1]
            high_ref[k : k + 1, cols] = v[nz - 1 : nz]
            if k == 0:
                first_ref[0, :, cols] = v
            if k == rows - 1:
                last_ref[0, :, cols] = v


def diffuse_kernel(c_ref, e_ref, s_ref, prev_ref, next_ref, below_ref, above_ref, o_ref):
    nblk, rows, nz, width = o_ref.shape
    length = s_ref.shape[2]
    sub = lax.broadcasted_iota(jnp.int32, (nz, length), 0)
    c = c_ref[0]
    for k in range(rows):
        shifted = s_ref[k]
        r_plus = s_ref[k + 1] if k < rows - 1 else next_ref[0]
        r_minus = s_ref[k - 1] if k > 0 else prev_ref[0]
        z_plus = jnp.where(sub == nz - 1, above_ref[k : k + 1, :], pltpu.roll(shifted, nz - 1, 0))
        z_minus = jnp.where(sub == 0, below_ref[k : k + 1, :], pltpu.roll(shifted, 1, 0))
        laplace = r_plus + r_minus + z_plus + z_minus - 4.0 * shifted
        diffused = shifted + c * laplace
        after = pltpu.roll(diffused, length - 1, 1)
        before = pltpu.roll(diffused, 1, 1)
        e = e_ref[k]
        half = 0.5 * e
        out = diffused - half * (after - before) + half * e * (after - 2.0 * diffused + before)
        for j in range(nblk):
            o_ref[j, k] = out[:, j * width : (j + 1) * width]


def barrel(block, amounts, span):
    result = block
    for level in range(span.bit_length()):
        moved = jnp.roll(result, 1 << level, axis=2)
        chosen = amounts // (1 << level) % 2 == 1
        result = jnp.where(chosen[:, None, None], moved, result)
    return result


def halo_pairs(rows, halves, fields, step):
    pairs = []
    for r in range(rows):
        for f in range(fields):
            for h in range(halves):
                nh, nr = h + step, r
                if nh == halves:
                    nh, nr = 0, r + 1
                elif nh < 0:
                    nh, nr = halves - 1, r - 1
                if 0 <= nr < rows:
                    pairs.append(((f * halves + h) * rows + r, (f * halves + nh) * rows + nr))
    return pairs


def per_device(fields, shear_shift, remap_fraction, diffusivity):
    nf, nrow, nz, width = fields.shape
    loop = lax.axis_size("az")
    halves = loop // nf
    rows = nrow // halves
    x = fields.reshape(nf * halves, rows, nz, width)
    y = lax.all_to_all(x, "az", 0, 0, tiled=True)
    me = lax.axis_index("az")
    f = me // halves
    h = me % halves
    amounts = lax.dynamic_slice_in_dim(shear_shift, h * rows, rows)
    fraction = lax.dynamic_slice_in_dim(remap_fraction, h * rows, rows)
    coefficient = lax.dynamic_slice_in_dim(diffusivity, f, 1)
    length = loop * width
    smem = pl.BlockSpec(memory_space=pltpu.SMEM)
    vmem = pl.BlockSpec(memory_space=pltpu.VMEM)
    shifted, last, first, low, high = pl.pallas_call(
        shift_kernel,
        out_shape=(
            jax.ShapeDtypeStruct((rows, nz, length), y.dtype),
            jax.ShapeDtypeStruct((1, nz, length), y.dtype),
            jax.ShapeDtypeStruct((1, nz, length), y.dtype),
            jax.ShapeDtypeStruct((rows, length), y.dtype),
            jax.ShapeDtypeStruct((rows, length), y.dtype),
        ),
        in_specs=[smem, vmem],
        out_specs=(vmem,) * 5,
    )(amounts, y)

    nrad = lax.axis_size("rad")
    nvert = lax.axis_size("vert")
    both = ("az", "rad")
    prev_row = lax.ppermute(last, both, halo_pairs(nrad, halves, nf, 1))
    next_row = lax.ppermute(first, both, halo_pairs(nrad, halves, nf, -1))
    up = [(i, i + 1) for i in range(nvert - 1)]
    down = [(i + 1, i) for i in range(nvert - 1)]
    below = lax.ppermute(high, "vert", up)
    above = lax.ppermute(low, "vert", down)

    blocks = pl.pallas_call(
        diffuse_kernel,
        out_shape=jax.ShapeDtypeStruct((loop, rows, nz, width), y.dtype),
        in_specs=[smem, smem] + [vmem] * 5,
        out_specs=vmem,
    )(coefficient, fraction, shifted, prev_row, next_row, below, above)
    back = lax.all_to_all(blocks, "az", 0, 0, tiled=True)
    return back.reshape(nf, nrow, nz, width)


def solution(mesh):
    in_specs = (P(None, "rad", "vert", "az"), P("rad"), P("rad"), P())
    out_specs = P(None, "rad", "vert", "az")
    return jax.shard_map(
        per_device, mesh=mesh, in_specs=in_specs, out_specs=out_specs, check_vma=False
    )
```

time: 93.6 us -> 76 us (0.81)
  other arithmetic: 12.9 us -> 0 us
  local copies, waits for them, and re-layouts: 16 us -> 6.13 us
  Pallas kernels: 0 us -> 5.93 us
  starting transfers between devices: 28.9 us -> 24.4 us
  waiting for transfers between devices: 15.1 us -> 17.9 us
  blocking collectives: 19.6 us -> 21 us
    concatenate x8 -> x0, local copies, waits for them, and re-layouts: 8.88 us -> none  [the longest x3 4 us: per_device(): z_plus = jnp.concatenate([shifted[:, 1:], above], axis=1)]
    unnamed x11 -> x0, other arithmetic: 8.36 us -> none
    pallas_call x0 -> x2, Pallas kernels: none -> 5.93 us  [the longest x1 3.05 us: per_device(): pl.pallas_call(diffuse_kernel, out_shape=jax.ShapeDtypeStruct((loop, rows...]
    ppermute x4, starting transfers between devices: 11.4 us -> 6.9 us  [the longest x1 2.4 us: per_device(): next_row = lax.ppermute(first, both, halo_pairs(nrad, halves, nf, -1))]
    slice x18 -> x0, local copies, waits for them, and re-layouts: 2.39 us -> none  [the longest x1 0.73 us: per_device(): below = lax.ppermute(shifted[:, -1:], 'vert', up)]
    add x1 -> x0, other arithmetic: 1.98 us -> none  [per_device(): diffused = shifted + coefficient * laplace]
    ppermute x4, waiting for transfers between devices: 0.01 us -> 1.92 us  [the longest x1 1.91 us: per_device(): above = lax.ppermute(low, 'vert', down)]
    transpose x1 -> x0, other arithmetic: 1.7 us -> none  [per_device(): blocks = jnp.transpose(out.reshape(rows, nz, loop, width), (2, 0, 1, 3))]
  transfers between devices with their start and end apart: 5 -> 5, of which waited for: 1 -> 2; matrix products, arithmetic and copies ran while one was open for 9% -> 3% of each run, Pallas kernels for 0% -> 0%
where the time goes in v3:
time: 76 us; the launch traced here: 75.5 us
  starting transfers between devices  24.4 us (32%)
  blocking collectives  21 us (28%)
  waiting for transfers between devices  17.9 us (24%)
  local copies, waits for them, and re-layouts  6.13 us (8%)
  Pallas kernels  5.93 us (8%)
    all_to_all x1, blocking collectives, per_device(): back = lax.all_to_all(blocks, 'az', 0, 0, tiled=True)  21 us
    all_to_all x1, starting transfers between devices, per_device(): y = lax.all_to_all(x, 'az', 0, 0, tiled=True)  17.5 us
    all_to_all x1, waiting for transfers between devices, per_device(): y = lax.all_to_all(x, 'az', 0, 0, tiled=True)  16 us
    unnamed x17, local copies, waits for them, and re-layouts  4.15 us
    pallas_call x1, Pallas kernels, per_device(): pl.pallas_call(diffuse_kernel, out_shape=jax.ShapeDtypeStruct((loop, rows...  3.05 us
    pallas_call x1, Pallas kernels, per_device(): pl.pallas_call(shift_kernel, out_shape=(jax.ShapeDtypeStruct((rows, nz, l...  2.87 us
    ppermute x1, starting transfers between devices, per_device(): next_row = lax.ppermute(first, both, halo_pairs(nrad, halves, nf, -1))  2.4 us
    ppermute x1, waiting for transfers between devices, per_device(): above = lax.ppermute(low, 'vert', down)  1.91 us
  transfers between devices with their start and end apart: 5, of which 2 were waited for; matrix products, arithmetic and copies ran while one was open for 3% of the time, Pallas kernels for 0%

profile of v3, /device:TPU:1, one launch (start us, length us, event | category | flops | bytes accessed | tf_op | source)
XLA Modules:
  0.0 75.5 jit_solution(5461361987600157757)
XLA Ops:
  0.0 17.5 %all-to-all-start = ((f32[16,8,8,128]{3,2,1,0:T(8,128)}), f32[16,8,8,128]{3,2,1,0:T(8,128)S(1)}, u32[]{:S(2)}, u32[]{:S(2)}) async-start(f32[16,8,8,128]{3,2,1,0:T(8,128)} %bitcast.3), calls=%async_computation | async-start | bytes 1048576 | tf_op jit(solution)/shard_map/all_to_all | solution.py:83
  17.5 0.0 copy-start.5
  17.5 0.6 copy-done.5
  18.1 0.7 dynamic_slice.11.amount_ref
  18.8 16.0 %all-to-all-done.x_ref = f32[16,8,8,128]{3,2,1,0:T(8,128)S(1)} async-done(((f32[16,8,8,128]{3,2,1,0:T(8,128)}), f32[16,8,8,128]{3,2,1,0:T(8,128)S(1)}, u32[]{:S(2)}, u32[]{:S(2)}) %all-to-all-start) | async-done | bytes 524320 | tf_op jit(solution)/shard_map/all_to_all | solution.py:83
  34.8 0.0 copy-start
  34.8 0.8 %copy-done = f32[16,8,8,128]{3,2,1,0:T(8,128)} copy-done((f32[16,8,8,128]{3,2,1,0:T(8,128)}, f32[16,8,8,128]{3,2,1,0:T(8,128)S(1)}, u32[]{:S(2)}) %copy-start) | copy-done | bytes 524312
  35.6 2.9 %shard_map.46 = (f32[8,8,2048]{2,1,0:T(8,128)}, f32[1,8,2048]{2,1,0:T(8,128)}, f32[1,8,2048]{2,1,0:T(8,128)}, f32[8,2048]{1,0:T(8,128)}, f32[8,2048]{1,0:T(8,128)}) custom-call(s32[8]{0:T(128)} %dynamic_slice.11.amount_ref, f32[16,8,8,128]{3,2,1,0:T(8,128)} %copy-done), custom_call_target="tpu_custom_call" | custom-call | tf_op jit(solution)/shard_map/pallas_call | solution.py:93
  38.5 1.9 %collective-permute-start = (f32[1,8,2048]{2,1,0:T(8,128)}, f32[1,8,2048]{2,1,0:T(8,128)S(1)}, u32[]{:S(2)}, u32[]{:S(2)}) collective-permute-start(f32[1,8,2048]{2,1,0:T(8,128)} %get-tuple-element.11), channel_id=1, source_target_pairs={{0,64},{64,8},{128,192},{192,136},{256,320},{320,264},{384,448},{4... | collective-permute-start | bytes 196616 | tf_op jit(solution)/shard_map/ppermute | solution.py:109
  40.4 2.4 %collective-permute-start.1 = (f32[1,8,2048]{2,1,0:T(8,128)}, f32[1,8,2048]{2,1,0:T(8,128)S(1)}, u32[]{:S(2)}, u32[]{:S(2)}) collective-permute-start(f32[1,8,2048]{2,1,0:T(8,128)} %get-tuple-element.12), channel_id=1, source_target_pairs={{64,0},{192,128},{320,256},{448,384},{576,512},{704,640},{832,768}... | collective-permute-start | bytes 196616 | tf_op jit(solution)/shard_map/ppermute | solution.py:110
  42.8 1.3 %collective-permute-start.2 = (f32[8,2048]{1,0:T(8,128)}, f32[8,2048]{1,0:T(8,128)S(1)}, u32[]{:S(2)}, u32[]{:S(2)}) collective-permute-start(f32[8,2048]{1,0:T(8,128)} %get-tuple-element.13), channel_id=1, source_target_pairs={{0,1},{1,2},{2,3},{3,4},{4,5},{5,6},{6,7},{8,9},{9,10},{10,11},{11... | collective-permute-start | bytes 196616 | tf_op jit(solution)/shard_map/ppermute | solution.py:113
  44.1 1.3 %collective-permute-start.3 = (f32[8,2048]{1,0:T(8,128)}, f32[8,2048]{1,0:T(8,128)S(1)}, u32[]{:S(2)}, u32[]{:S(2)}) collective-permute-start(f32[8,2048]{1,0:T(8,128)} %get-tuple-element.14), channel_id=1, source_target_pairs={{1,0},{2,1},{3,2},{4,3},{5,4},{6,5},{7,6},{9,8},{10,9},{11,10},{12... | collective-permute-start | bytes 196616 | tf_op jit(solution)/shard_map/ppermute | solution.py:114
  45.4 0.0 copy-start.6
  45.4 0.6 copy-done.6
  46.1 0.7 dynamic_slice.10.e_ref
  46.7 0.0 copy-start.7
  46.7 0.7 copy-done.7
  47.4 0.7 dynamic_slice.9.c_ref
  48.0 0.0 collective-permute-done.prev_ref
  48.0 0.0 copy-start.1
  48.0 0.0 collective-permute-done.1.next_ref
  48.0 0.0 copy-start.2
  48.1 0.0 collective-permute-done.2.below_ref
  48.1 0.0 copy-start.3
  48.1 1.9 %collective-permute-done.3.above_ref = f32[8,2048]{1,0:T(8,128)S(1)} collective-permute-done((f32[8,2048]{1,0:T(8,128)}, f32[8,2048]{1,0:T(8,128)S(1)}, u32[]{:S(2)}, u32[]{:S(2)}) %collective-permute-start.3) | collective-permute-done | bytes 65568 | tf_op jit(solution)/shard_map/ppermute | solution.py:114
  50.0 0.0 copy-done.1
  50.0 0.0 copy-done.2
  50.0 0.0 copy-done.3
  50.0 0.6 copy-done.4
  50.6 3.1 %shard_map.47 = f32[16,8,8,128]{3,2,1,0:T(8,128)} custom-call(f32[1]{0:T(128)} %dynamic_slice.9.c_ref, f32[8]{0:T(128)} %dynamic_slice.10.e_ref, f32[8,8,2048]{2,1,0:T(8,128)} %get-tuple-element.10.s_ref, f32[1,8,2048]{2,1,0:T(8,128)} %copy-done.1, f32[1,8,2048]{2,1,0:T(8,128)} %copy-done.2, f32[8,2048]{1,0:T(8,128)} %copy-done.3, f32[8,2048]{1,0:T(8,128)} %copy-done.4), custom_call_target="tpu_custom_call" | custom-call | tf_op jit(solution)/shard_map/pallas_call | solution.py:116
  53.7 21.0 %all_to_all.10 = f32[16,8,8,128]{3,2,1,0:T(8,128)S(1)} all-to-all(f32[16,8,8,128]{3,2,1,0:T(8,128)} %shard_map.47), channel_id=1, replica_groups=mesh['az'=16,'rad'=8,'vert'=8] {'az'}, dimensions={0} | all-to-all | bytes 1048576 | tf_op jit(solution)/shard_map/all_to_all | solution.py:122
  74.7 0.8 %copy.6 = f32[8,16,8,128]{3,2,1,0:T(8,128)} copy(f32[8,16,8,128]{3,2,1,0:T(8,128)S(1)} %bitcast.2) | data formatting | bytes 1048576
  (1 shorter events, 0.0 us)
Async XLA Ops:
  0.0 34.8 %all-to-all-start = ((f32[16,8,8,128]{3,2,1,0:T(8,128)}), f32[16,8,8,128]{3,2,1,0:T(8,128)S(1)}, u32[]{:S(2)}, u32[]{:S(2)}) async-start(f32[16,8,8,128]{3,2,1,0:T(8,128)} %bitcast.3), calls=%async_computation | async-start | bytes 1048576 | tf_op jit(solution)/shard_map/all_to_all | solution.py:83
  17.5 0.7 copy-start.5
  34.8 0.8 %copy-start = (f32[16,8,8,128]{3,2,1,0:T(8,128)}, f32[16,8,8,128]{3,2,1,0:T(8,128)S(1)}, u32[]{:S(2)}) copy-start(f32[16,8,8,128]{3,2,1,0:T(8,128)S(1)} %all-to-all-done.x_ref) | copy-start | bytes 1572868
  38.5 9.6 %collective-permute-start = (f32[1,8,2048]{2,1,0:T(8,128)}, f32[1,8,2048]{2,1,0:T(8,128)S(1)}, u32[]{:S(2)}, u32[]{:S(2)}) collective-permute-start(f32[1,8,2048]{2,1,0:T(8,128)} %get-tuple-element.11), channel_id=1, source_target_pairs={{0,64},{64,8},{128,192},{192,136},{256,320},{320,264},{384,448},{4... | collective-permute-start | bytes 196616 | tf_op jit(solution)/shard_map/ppermute | solution.py:109
  40.4 7.7 %collective-permute-start.1 = (f32[1,8,2048]{2,1,0:T(8,128)}, f32[1,8,2048]{2,1,0:T(8,128)S(1)}, u32[]{:S(2)}, u32[]{:S(2)}) collective-permute-start(f32[1,8,2048]{2,1,0:T(8,128)} %get-tuple-element.12), channel_id=1, source_target_pairs={{64,0},{192,128},{320,256},{448,384},{576,512},{704,640},{832,768}... | collective-permute-start | bytes 196616 | tf_op jit(solution)/shard_map/ppermute | solution.py:110
  42.8 5.3 %collective-permute-start.2 = (f32[8,2048]{1,0:T(8,128)}, f32[8,2048]{1,0:T(8,128)S(1)}, u32[]{:S(2)}, u32[]{:S(2)}) collective-permute-start(f32[8,2048]{1,0:T(8,128)} %get-tuple-element.13), channel_id=1, source_target_pairs={{0,1},{1,2},{2,3},{3,4},{4,5},{5,6},{6,7},{8,9},{9,10},{10,11},{11... | collective-permute-start | bytes 196616 | tf_op jit(solution)/shard_map/ppermute | solution.py:113
  44.1 5.9 %collective-permute-start.3 = (f32[8,2048]{1,0:T(8,128)}, f32[8,2048]{1,0:T(8,128)S(1)}, u32[]{:S(2)}, u32[]{:S(2)}) collective-permute-start(f32[8,2048]{1,0:T(8,128)} %get-tuple-element.14), channel_id=1, source_target_pairs={{1,0},{2,1},{3,2},{4,3},{5,4},{6,5},{7,6},{9,8},{10,9},{11,10},{12... | collective-permute-start | bytes 196616 | tf_op jit(solution)/shard_map/ppermute | solution.py:114
  45.4 0.7 copy-start.6
  46.7 0.7 copy-start.7
  48.0 2.0 %copy-start.1 = (f32[1,8,2048]{2,1,0:T(8,128)}, f32[1,8,2048]{2,1,0:T(8,128)S(1)}, u32[]{:S(2)}) copy-start(f32[1,8,2048]{2,1,0:T(8,128)S(1)} %collective-permute-done.prev_ref) | copy-start | bytes 196612
  48.0 1.9 %copy-start.2 = (f32[1,8,2048]{2,1,0:T(8,128)}, f32[1,8,2048]{2,1,0:T(8,128)S(1)}, u32[]{:S(2)}) copy-start(f32[1,8,2048]{2,1,0:T(8,128)S(1)} %collective-permute-done.1.next_ref) | copy-start | bytes 196612
  48.1 1.9 %copy-start.3 = (f32[8,2048]{1,0:T(8,128)}, f32[8,2048]{1,0:T(8,128)S(1)}, u32[]{:S(2)}) copy-start(f32[8,2048]{1,0:T(8,128)S(1)} %collective-permute-done.2.below_ref) | copy-start | bytes 196612
  50.0 0.6 copy-start.4

commit v4 on v3

--- a/solution.py
+++ b/solution.py
@@ -1,3 +1,5 @@
+import functools
+
 import jax
 import jax.numpy as jnp
 from jax import lax
@@ -5,12 +7,15 @@
 from jax.experimental.pallas import tpu as pltpu
 from jax.sharding import PartitionSpec as P
 
+ROUNDS = 2
 
-def shift_kernel(amount_ref, x_ref, o_ref, last_ref, first_ref, low_ref, high_ref):
+
+def shift_kernel(parts, amount_ref, x_ref, o_ref, last_ref, first_ref, low_ref, high_ref):
     nblk, rows, nz, width = x_ref.shape
     lane = lax.broadcasted_iota(jnp.int32, (nz, width), 1)
+    base = lax.axis_index("az") % parts * rows
     for k in range(rows):
-        s = amount_ref[k]
+        s = amount_ref[base + k]
         b = s // width
         rem = s % width
         late = lane >= width - rem
@@ -28,11 +33,13 @@
                 last_ref[0, :, cols] = v
 
 
-def diffuse_kernel(c_ref, e_ref, s_ref, prev_ref, next_ref, below_ref, above_ref, o_ref):
+def diffuse_kernel(parts, offset, c_ref, e_ref, s_ref, prev_ref, next_ref, below_ref, above_ref, o_ref):
     nblk, rows, nz, width = o_ref.shape
     length = s_ref.shape[2]
     sub = lax.broadcasted_iota(jnp.int32, (nz, length), 0)
-    c = c_ref[0]
+    me = lax.axis_index("az")
+    base = me % parts * rows
+    c = c_ref[me // parts + offset]
     for k in range(rows):
         shifted = s_ref[k]
         r_plus = s_ref[k + 1] if k < rows - 1 else next_ref[0]
@@ -43,20 +50,11 @@
         diffused = shifted + c * laplace
         after = pltpu.roll(diffused, length - 1, 1)
         before = pltpu.roll(diffused, 1, 1)
-        e = e_ref[k]
+        e = e_ref[base + k]
         half = 0.5 * e
         out = diffused - half * (after - before) + half * e * (after - 2.0 * diffused + before)
         for j in range(nblk):
             o_ref[j, k] = out[:, j * width : (j + 1) * width]
-
-
-def barrel(block, amounts, span):
-    result = block
-    for level in range(span.bit_length()):
-        moved = jnp.roll(result, 1 << level, axis=2)
-        chosen = amounts // (1 << level) % 2 == 1
-        result = jnp.where(chosen[:, None, None], moved, result)
-    return result
 
 
 def halo_pairs(rows, halves, fields, step):
@@ -74,24 +72,18 @@
     return pairs
 
 
-def per_device(fields, shear_shift, remap_fraction, diffusivity):
-    nf, nrow, nz, width = fields.shape
+def one_round(block, offset, shear_shift, remap_fraction, diffusivity):
+    nf, nrow, nz, width = block.shape
     loop = lax.axis_size("az")
-    halves = loop // nf
-    rows = nrow // halves
-    x = fields.reshape(nf * halves, rows, nz, width)
+    parts = loop // nf
+    rows = nrow // parts
+    x = block.reshape(nf * parts, rows, nz, width)
     y = lax.all_to_all(x, "az", 0, 0, tiled=True)
-    me = lax.axis_index("az")
-    f = me // halves
-    h = me % halves
-    amounts = lax.dynamic_slice_in_dim(shear_shift, h * rows, rows)
-    fraction = lax.dynamic_slice_in_dim(remap_fraction, h * rows, rows)
-    coefficient = lax.dynamic_slice_in_dim(diffusivity, f, 1)
     length = loop * width
     smem = pl.BlockSpec(memory_space=pltpu.SMEM)
     vmem = pl.BlockSpec(memory_space=pltpu.VMEM)
     shifted, last, first, low, high = pl.pallas_call(
-        shift_kernel,
+        functools.partial(shift_kernel, parts),
         out_shape=(
             jax.ShapeDtypeStruct((rows, nz, length), y.dtype),
             jax.ShapeDtypeStruct((1, nz, length), y.dtype),
@@ -101,26 +93,36 @@
         ),
         in_specs=[smem, vmem],
         out_specs=(vmem,) * 5,
-    )(amounts, y)
+    )(shear_shift, y)
 
     nrad = lax.axis_size("rad")
     nvert = lax.axis_size("vert")
     both = ("az", "rad")
-    prev_row = lax.ppermute(last, both, halo_pairs(nrad, halves, nf, 1))
-    next_row = lax.ppermute(first, both, halo_pairs(nrad, halves, nf, -1))
+    prev_row = lax.ppermute(last, both, halo_pairs(nrad, parts, nf, 1))
+    next_row = lax.ppermute(first, both, halo_pairs(nrad, parts, nf, -1))
     up = [(i, i + 1) for i in range(nvert - 1)]
     down = [(i + 1, i) for i in range(nvert - 1)]
     below = lax.ppermute(high, "vert", up)
     above = lax.ppermute(low, "vert", down)
 
     blocks = pl.pallas_call(
-        diffuse_kernel,
+        functools.partial(diffuse_kernel, parts, offset),
         out_shape=jax.ShapeDtypeStruct((loop, rows, nz, width), y.dtype),
         in_specs=[smem, smem] + [vmem] * 5,
         out_specs=vmem,
-    )(coefficient, fraction, shifted, prev_row, next_row, below, above)
+    )(diffusivity, remap_fraction, shifted, prev_row, next_row, below, above)
     back = lax.all_to_all(blocks, "az", 0, 0, tiled=True)
     return back.reshape(nf, nrow, nz, width)
+
+
+def per_device(fields, shear_shift, remap_fraction, diffusivity):
+    nf = fields.shape[0]
+    step = nf // ROUNDS
+    outs = [
+        one_round(fields[i : i + step], i, shear_shift, remap_fraction, diffusivity)
+        for i in range(0, nf, step)
+    ]
+    return outs[0] if len(outs) == 1 else jnp.concatenate(outs, axis=0)
 
 
 def solution(mesh):

time: 76 us -> 103 us (1.36)
  the two profiles are of different devices: /device:TPU:1 before, /device:TPU:65 now
where the time goes in v4:
time: 103 us; the launch traced here: 102 us
  blocking collectives  41.1 us (40%)
  starting transfers between devices  36.9 us (36%)
  waiting for transfers between devices  11.5 us (11%)
  Pallas kernels  8.4 us (8%)
  local copies, waits for them, and re-layouts  3.06 us (3%)
    all_to_all x1, blocking collectives, one_round(): back = lax.all_to_all(blocks, 'az', 0, 0, tiled=True)  22.2 us
    all_to_all x1, blocking collectives, one_round(): y = lax.all_to_all(x, 'az', 0, 0, tiled=True)  18.9 us
    ppermute x2, waiting for transfers between devices, one_round(): above = lax.ppermute(low, 'vert', down)  11.4 us
    all_to_all x1, starting transfers between devices, one_round(): back = lax.all_to_all(blocks, 'az', 0, 0, tiled=True)  10.6 us
    ppermute x2, starting transfers between devices, one_round(): below = lax.ppermute(high, 'vert', up)  9.81 us
    ppermute x2, starting transfers between devices, one_round(): prev_row = lax.ppermute(last, both, halo_pairs(nrad, parts, nf, 1))  6.6 us
    pallas_call x2, Pallas kernels, one_round(): pl.pallas_call(functools.partial(shift_kernel, parts), out_shape=(jax.Sha...  4.49 us
    pallas_call x2, Pallas kernels, one_round(): pl.pallas_call(functools.partial(diffuse_kernel, parts, offset), out_shap...  3.91 us
  transfers between devices with their start and end apart: 10, of which 2 were waited for; matrix products, arithmetic and copies ran while one was open for 0% of the time, Pallas kernels for 8%

profile of v4, /device:TPU:65, one launch (start us, length us, event | category | flops | bytes accessed | tf_op | source)
XLA Modules:
  0.0 101.9 jit_solution(11977008594768556625)
XLA Ops:
  0.0 1.8 %fusion = (f32[4,16,8,128]{3,2,1,0:T(8,128)S(1)}, f32[4,16,8,128]{3,2,1,0:T(8,128)}) fusion(f32[8,16,8,128]{3,2,1,0:T(8,128)} %param.4), kind=kLoop, calls=%fused_computation.1 | loop fusion | bytes 1048576 | tf_op jit(solution)/shard_map/slice | solution.py:122
  1.8 18.9 %all_to_all.20.x_ref = f32[16,4,8,128]{3,2,1,0:T(8,128)} all-to-all(f32[16,4,8,128]{3,2,1,0:T(8,128)S(1)} %bitcast.5), channel_id=1, replica_groups=mesh['az'=16,'rad'=8,'vert'=8] {'az'}, dimensions={0} | all-to-all | bytes 524288 | tf_op jit(solution)/shard_map/all_to_all | solution.py:81
  20.7 3.4 %all-to-all-start.2 = ((f32[16,4,8,128]{3,2,1,0:T(8,128)}), f32[16,4,8,128]{3,2,1,0:T(8,128)S(1)}, u32[]{:S(2)}, u32[]{:S(2)}) async-start(f32[16,4,8,128]{3,2,1,0:T(8,128)} %bitcast.2), calls=%async_computation.2 | async-start | bytes 524288 | tf_op jit(solution)/shard_map/all_to_all | solution.py:81
  24.1 2.2 %shard_map.46 = (f32[4,8,2048]{2,1,0:T(8,128)}, f32[1,8,2048]{2,1,0:T(8,128)}, f32[1,8,2048]{2,1,0:T(8,128)}, f32[4,2048]{1,0:T(4,128)}, f32[4,2048]{1,0:T(4,128)}) custom-call(s32[16]{0:T(128)} %amount_ref.3, f32[16,4,8,128]{3,2,1,0:T(8,128)} %all_to_all.20.x_ref), custom_call_target="tpu_custom_call" | custom-call | tf_op jit(solution)/shard_map/pallas_call | solution.py:85
  26.4 3.1 %collective-permute-start = (f32[1,8,2048]{2,1,0:T(8,128)}, f32[1,8,2048]{2,1,0:T(8,128)S(1)}, u32[]{:S(2)}, u32[]{:S(2)}) collective-permute-start(f32[1,8,2048]{2,1,0:T(8,128)} %get-tuple-element.16), channel_id=1, source_target_pairs={{0,64},{64,128},{128,192},{192,8},{256,320},{320,384},{384,448},{4... | collective-permute-start | bytes 196616 | tf_op jit(solution)/shard_map/ppermute | solution.py:101
  29.5 1.9 %collective-permute-start.1 = (f32[1,8,2048]{2,1,0:T(8,128)}, f32[1,8,2048]{2,1,0:T(8,128)S(1)}, u32[]{:S(2)}, u32[]{:S(2)}) collective-permute-start(f32[1,8,2048]{2,1,0:T(8,128)} %get-tuple-element.17), channel_id=1, source_target_pairs={{64,0},{128,64},{192,128},{320,256},{384,320},{448,384},{576,512},... | collective-permute-start | bytes 196616 | tf_op jit(solution)/shard_map/ppermute | solution.py:102
  31.4 4.9 %collective-permute-start.2 = (f32[4,2048]{1,0:T(4,128)}, f32[4,2048]{1,0:T(4,128)S(1)}, u32[]{:S(2)}, u32[]{:S(2)}) collective-permute-start(f32[4,2048]{1,0:T(4,128)} %get-tuple-element.18), channel_id=1, source_target_pairs={{0,1},{1,2},{2,3},{3,4},{4,5},{5,6},{6,7},{8,9},{9,10},{10,11},{11... | collective-permute-start | bytes 98312 | tf_op jit(solution)/shard_map/ppermute | solution.py:105
  36.3 1.3 %collective-permute-start.3 = (f32[4,2048]{1,0:T(4,128)}, f32[4,2048]{1,0:T(4,128)S(1)}, u32[]{:S(2)}, u32[]{:S(2)}) collective-permute-start(f32[4,2048]{1,0:T(4,128)} %get-tuple-element.19), channel_id=1, source_target_pairs={{1,0},{2,1},{3,2},{4,3},{5,4},{6,5},{7,6},{9,8},{10,9},{11,10},{12... | collective-permute-start | bytes 98312 | tf_op jit(solution)/shard_map/ppermute | solution.py:106
  37.6 0.0 collective-permute-done.2.below_ref
  37.6 5.1 %collective-permute-done.3.above_ref = f32[4,2048]{1,0:T(4,128)S(1)} collective-permute-done((f32[4,2048]{1,0:T(4,128)}, f32[4,2048]{1,0:T(4,128)S(1)}, u32[]{:S(2)}, u32[]{:S(2)}) %collective-permute-start.3) | collective-permute-done | bytes 32800 | tf_op jit(solution)/shard_map/ppermute | solution.py:106
  42.7 0.6 copy-done.7
  43.3 0.0 copy-done.1
  43.4 0.0 copy-done.3
  43.4 2.0 %shard_map.47 = f32[16,4,8,128]{3,2,1,0:T(8,128)} custom-call(f32[8]{0:T(128)} %c_ref.3, f32[16]{0:T(128)} %e_ref.3, f32[4,8,2048]{2,1,0:T(8,128)} %get-tuple-element.15.s_ref, f32[1,8,2048]{2,1,0:T(8,128)} %copy-done.1, f32[1,8,2048]{2,1,0:T(8,128)} %copy-done.3, f32[4,2048]{1,0:T(4,128)} %copy-done.5, f32[4,2048]{1,0:T(4,128)} %copy-done.7), custom_call_target="tpu_custom_call" | custom-call | tf_op jit(solution)/shard_map/pallas_call | solution.py:108
  45.3 0.0 all-to-all-done.2.x_ref
  45.3 10.6 %all-to-all-start.1 = ((f32[16,4,8,128]{3,2,1,0:T(8,128)}), f32[16,4,8,128]{3,2,1,0:T(8,128)S(1)}, u32[]{:S(2)}, u32[]{:S(2)}) async-start(f32[16,4,8,128]{3,2,1,0:T(8,128)} %shard_map.47), calls=%async_computation.1 | async-start | bytes 524288 | tf_op jit(solution)/shard_map/all_to_all | solution.py:114
  56.0 2.2 %shard_map.48 = (f32[4,8,2048]{2,1,0:T(8,128)}, f32[1,8,2048]{2,1,0:T(8,128)}, f32[1,8,2048]{2,1,0:T(8,128)}, f32[4,2048]{1,0:T(4,128)}, f32[4,2048]{1,0:T(4,128)}) custom-call(s32[16]{0:T(128)} %amount_ref.3, f32[16,4,8,128]{3,2,1,0:T(8,128)} %copy-done), custom_call_target="tpu_custom_call" | custom-call | tf_op jit(solution)/shard_map/pallas_call | solution.py:85
  58.2 3.5 %collective-permute-start.4 = (f32[1,8,2048]{2,1,0:T(8,128)}, f32[1,8,2048]{2,1,0:T(8,128)S(1)}, u32[]{:S(2)}, u32[]{:S(2)}) collective-permute-start(f32[1,8,2048]{2,1,0:T(8,128)} %get-tuple-element.21), channel_id=1, source_target_pairs={{0,64},{64,128},{128,192},{192,8},{256,320},{320,384},{384,448},{4... | collective-permute-start | bytes 196616 | tf_op jit(solution)/shard_map/ppermute | solution.py:101
  61.8 1.9 %collective-permute-start.5 = (f32[1,8,2048]{2,1,0:T(8,128)}, f32[1,8,2048]{2,1,0:T(8,128)S(1)}, u32[]{:S(2)}, u32[]{:S(2)}) collective-permute-start(f32[1,8,2048]{2,1,0:T(8,128)} %get-tuple-element.22), channel_id=1, source_target_pairs={{64,0},{128,64},{192,128},{320,256},{384,320},{448,384},{576,512},... | collective-permute-start | bytes 196616 | tf_op jit(solution)/shard_map/ppermute | solution.py:102
  63.7 4.9 %collective-permute-start.6 = (f32[4,2048]{1,0:T(4,128)}, f32[4,2048]{1,0:T(4,128)S(1)}, u32[]{:S(2)}, u32[]{:S(2)}) collective-permute-start(f32[4,2048]{1,0:T(4,128)} %get-tuple-element.23), channel_id=1, source_target_pairs={{0,1},{1,2},{2,3},{3,4},{4,5},{5,6},{6,7},{8,9},{9,10},{10,11},{11... | collective-permute-start | bytes 98312 | tf_op jit(solution)/shard_map/ppermute | solution.py:105
  68.6 1.3 %collective-permute-start.7 = (f32[4,2048]{1,0:T(4,128)}, f32[4,2048]{1,0:T(4,128)S(1)}, u32[]{:S(2)}, u32[]{:S(2)}) collective-permute-start(f32[4,2048]{1,0:T(4,128)} %get-tuple-element.24), channel_id=1, source_target_pairs={{1,0},{2,1},{3,2},{4,3},{5,4},{6,5},{7,6},{9,8},{10,9},{11,10},{12... | collective-permute-start | bytes 98312 | tf_op jit(solution)/shard_map/ppermute | solution.py:106
  69.9 0.0 collective-permute-done.6.below_ref
  69.9 6.3 %collective-permute-done.7.above_ref = f32[4,2048]{1,0:T(4,128)S(1)} collective-permute-done((f32[4,2048]{1,0:T(4,128)}, f32[4,2048]{1,0:T(4,128)S(1)}, u32[]{:S(2)}, u32[]{:S(2)}) %collective-permute-start.7) | collective-permute-done | bytes 32800 | tf_op jit(solution)/shard_map/ppermute | solution.py:106
  76.2 0.0 collective-permute-done.4.prev_ref
  76.2 0.0 collective-permute-done.5.next_ref
  76.3 0.6 copy-done.8
  76.8 0.0 copy-done.2
  76.9 0.0 copy-done.4
  76.9 2.0 %shard_map.49 = f32[16,4,8,128]{3,2,1,0:T(8,128)} custom-call(f32[8]{0:T(128)} %c_ref.3, f32[16]{0:T(128)} %e_ref.3, f32[4,8,2048]{2,1,0:T(8,128)} %get-tuple-element.20.s_ref, f32[1,8,2048]{2,1,0:T(8,128)} %copy-done.2, f32[1,8,2048]{2,1,0:T(8,128)} %copy-done.4, f32[4,2048]{1,0:T(4,128)} %copy-done.6, f32[4,2048]{1,0:T(4,128)} %copy-done.8), custom_call_target="tpu_custom_call" | custom-call | tf_op jit(solution)/shard_map/pallas_call | solution.py:108
  78.9 0.0 all-to-all-done.1
  78.9 22.2 %all_to_all.21 = f32[16,4,8,128]{3,2,1,0:T(8,128)S(1)} all-to-all(f32[16,4,8,128]{3,2,1,0:T(8,128)} %shard_map.49), channel_id=1, replica_groups=mesh['az'=16,'rad'=8,'vert'=8] {'az'}, dimensions={0} | all-to-all | bytes 524288 | tf_op jit(solution)/shard_map/all_to_all | solution.py:114
  101.0 0.8 pad_maximum_fusion
  (14 shorter events, 0.0 us)
Async XLA Ops:
  20.7 24.7 %all-to-all-start.2 = ((f32[16,4,8,128]{3,2,1,0:T(8,128)}), f32[16,4,8,128]{3,2,1,0:T(8,128)S(1)}, u32[]{:S(2)}, u32[]{:S(2)}) async-start(f32[16,4,8,128]{3,2,1,0:T(8,128)} %bitcast.2), calls=%async_computation.2 | async-start | bytes 524288 | tf_op jit(solution)/shard_map/all_to_all | solution.py:81
  26.4 16.3 %collective-permute-start = (f32[1,8,2048]{2,1,0:T(8,128)}, f32[1,8,2048]{2,1,0:T(8,128)S(1)}, u32[]{:S(2)}, u32[]{:S(2)}) collective-permute-start(f32[1,8,2048]{2,1,0:T(8,128)} %get-tuple-element.16), channel_id=1, source_target_pairs={{0,64},{64,128},{128,192},{192,8},{256,320},{320,384},{384,448},{4... | collective-permute-start | bytes 196616 | tf_op jit(solution)/shard_map/ppermute | solution.py:101
  29.5 13.3 %collective-permute-start.1 = (f32[1,8,2048]{2,1,0:T(8,128)}, f32[1,8,2048]{2,1,0:T(8,128)S(1)}, u32[]{:S(2)}, u32[]{:S(2)}) collective-permute-start(f32[1,8,2048]{2,1,0:T(8,128)} %get-tuple-element.17), channel_id=1, source_target_pairs={{64,0},{128,64},{192,128},{320,256},{384,320},{448,384},{576,512},... | collective-permute-start | bytes 196616 | tf_op jit(solution)/shard_map/ppermute | solution.py:102
  31.4 6.2 %collective-permute-start.2 = (f32[4,2048]{1,0:T(4,128)}, f32[4,2048]{1,0:T(4,128)S(1)}, u32[]{:S(2)}, u32[]{:S(2)}) collective-permute-start(f32[4,2048]{1,0:T(4,128)} %get-tuple-element.18), channel_id=1, source_target_pairs={{0,1},{1,2},{2,3},{3,4},{4,5},{5,6},{6,7},{8,9},{9,10},{10,11},{11... | collective-permute-start | bytes 98312 | tf_op jit(solution)/shard_map/ppermute | solution.py:105
  36.3 6.4 %collective-permute-start.3 = (f32[4,2048]{1,0:T(4,128)}, f32[4,2048]{1,0:T(4,128)S(1)}, u32[]{:S(2)}, u32[]{:S(2)}) collective-permute-start(f32[4,2048]{1,0:T(4,128)} %get-tuple-element.19), channel_id=1, source_target_pairs={{1,0},{2,1},{3,2},{4,3},{5,4},{6,5},{7,6},{9,8},{10,9},{11,10},{12... | collective-permute-start | bytes 98312 | tf_op jit(solution)/shard_map/ppermute | solution.py:106
  37.6 5.1 %copy-start.5 = (f32[4,2048]{1,0:T(4,128)}, f32[4,2048]{1,0:T(4,128)S(1)}, u32[]{:S(2)}) copy-start(f32[4,2048]{1,0:T(4,128)S(1)} %collective-permute-done.2.below_ref) | copy-start | bytes 98308
  42.7 0.6 copy-start.7
  42.7 0.6 copy-start.1
  42.7 0.7 copy-start.3
  45.3 10.6 %copy-start = (f32[16,4,8,128]{3,2,1,0:T(8,128)}, f32[16,4,8,128]{3,2,1,0:T(8,128)S(1)}, u32[]{:S(2)}) copy-start(f32[16,4,8,128]{3,2,1,0:T(8,128)S(1)} %all-to-all-done.2.x_ref) | copy-start | bytes 786436
  45.3 33.5 %all-to-all-start.1 = ((f32[16,4,8,128]{3,2,1,0:T(8,128)}), f32[16,4,8,128]{3,2,1,0:T(8,128)S(1)}, u32[]{:S(2)}, u32[]{:S(2)}) async-start(f32[16,4,8,128]{3,2,1,0:T(8,128)} %shard_map.47), calls=%async_computation.1 | async-start | bytes 524288 | tf_op jit(solution)/shard_map/all_to_all | solution.py:114
  58.2 18.0 %collective-permute-start.4 = (f32[1,8,2048]{2,1,0:T(8,128)}, f32[1,8,2048]{2,1,0:T(8,128)S(1)}, u32[]{:S(2)}, u32[]{:S(2)}) collective-permute-start(f32[1,8,2048]{2,1,0:T(8,128)} %get-tuple-element.21), channel_id=1, source_target_pairs={{0,64},{64,128},{128,192},{192,8},{256,320},{320,384},{384,448},{4... | collective-permute-start | bytes 196616 | tf_op jit(solution)/shard_map/ppermute | solution.py:101
  61.8 14.5 %collective-permute-start.5 = (f32[1,8,2048]{2,1,0:T(8,128)}, f32[1,8,2048]{2,1,0:T(8,128)S(1)}, u32[]{:S(2)}, u32[]{:S(2)}) collective-permute-start(f32[1,8,2048]{2,1,0:T(8,128)} %get-tuple-element.22), channel_id=1, source_target_pairs={{64,0},{128,64},{192,128},{320,256},{384,320},{448,384},{576,512},... | collective-permute-start | bytes 196616 | tf_op jit(solution)/shard_map/ppermute | solution.py:102
  63.7 6.2 %collective-permute-start.6 = (f32[4,2048]{1,0:T(4,128)}, f32[4,2048]{1,0:T(4,128)S(1)}, u32[]{:S(2)}, u32[]{:S(2)}) collective-permute-start(f32[4,2048]{1,0:T(4,128)} %get-tuple-element.23), channel_id=1, source_target_pairs={{0,1},{1,2},{2,3},{3,4},{4,5},{5,6},{6,7},{8,9},{9,10},{10,11},{11... | collective-permute-start | bytes 98312 | tf_op jit(solution)/shard_map/ppermute | solution.py:105
  68.6 7.6 %collective-permute-start.7 = (f32[4,2048]{1,0:T(4,128)}, f32[4,2048]{1,0:T(4,128)S(1)}, u32[]{:S(2)}, u32[]{:S(2)}) collective-permute-start(f32[4,2048]{1,0:T(4,128)} %get-tuple-element.24), channel_id=1, source_target_pairs={{1,0},{2,1},{3,2},{4,3},{5,4},{6,5},{7,6},{9,8},{10,9},{11,10},{12... | collective-permute-start | bytes 98312 | tf_op jit(solution)/shard_map/ppermute | solution.py:106
  69.9 6.3 %copy-start.6 = (f32[4,2048]{1,0:T(4,128)}, f32[4,2048]{1,0:T(4,128)S(1)}, u32[]{:S(2)}) copy-start(f32[4,2048]{1,0:T(4,128)S(1)} %collective-permute-done.6.below_ref) | copy-start | bytes 98308
  76.2 0.6 copy-start.8
  76.2 0.6 copy-start.2
  76.2 0.7 copy-start.4

commit v5 on v4

--- a/solution.py
+++ b/solution.py
@@ -7,7 +7,7 @@
 from jax.experimental.pallas import tpu as pltpu
 from jax.sharding import PartitionSpec as P
 
-ROUNDS = 2
+ROUNDS = 1
 
 
 def shift_kernel(parts, amount_ref, x_ref, o_ref, last_ref, first_ref, low_ref, high_ref):

time: 103 us -> 75.1 us (0.73)
  the two profiles are of different devices: /device:TPU:65 before, /device:TPU:1 now
where the time goes in v5:
time: 75.1 us; the launch traced here: 74.7 us
  blocking collectives  56.5 us (75%)
  starting transfers between devices  6.9 us (9%)
  Pallas kernels  5.22 us (7%)
  waiting for transfers between devices  4.58 us (6%)
  local copies, waits for them, and re-layouts  1.41 us (2%)
    all_to_all x1, blocking collectives, one_round(): y = lax.all_to_all(x, 'az', 0, 0, tiled=True)  35.5 us
    all_to_all x1, blocking collectives, one_round(): back = lax.all_to_all(blocks, 'az', 0, 0, tiled=True)  21 us
    ppermute x1, waiting for transfers between devices, one_round(): above = lax.ppermute(low, 'vert', down)  3.81 us
    pallas_call x1, Pallas kernels, one_round(): pl.pallas_call(functools.partial(shift_kernel, parts), out_shape=(jax.Sha...  2.84 us
    ppermute x1, starting transfers between devices, one_round(): next_row = lax.ppermute(first, both, halo_pairs(nrad, parts, nf, -1))  2.4 us
    pallas_call x1, Pallas kernels, one_round(): pl.pallas_call(functools.partial(diffuse_kernel, parts, offset), out_shap...  2.38 us
    ppermute x1, starting transfers between devices, one_round(): prev_row = lax.ppermute(last, both, halo_pairs(nrad, parts, nf, 1))  1.91 us
  transfers between devices with their start and end apart: 4, of which 2 were waited for; matrix products, arithmetic and copies ran while one was open for 0% of the time, Pallas kernels for 0%

profile of v5, /device:TPU:1, one launch (start us, length us, event | category | flops | bytes accessed | tf_op | source)
XLA Modules:
  0.0 74.7 jit_solution(6484857568679449674)
XLA Ops:
  0.0 35.5 %all_to_all.10.x_ref = f32[16,8,8,128]{3,2,1,0:T(8,128)} all-to-all(f32[16,8,8,128]{3,2,1,0:T(8,128)} %bitcast.3), channel_id=1, replica_groups=mesh['az'=16,'rad'=8,'vert'=8] {'az'}, dimensions={0} | all-to-all | bytes 1048576 | tf_op jit(solution)/shard_map/all_to_all | solution.py:81
  35.5 2.8 %shard_map.46 = (f32[8,8,2048]{2,1,0:T(8,128)}, f32[1,8,2048]{2,1,0:T(8,128)}, f32[1,8,2048]{2,1,0:T(8,128)}, f32[8,2048]{1,0:T(8,128)}, f32[8,2048]{1,0:T(8,128)}) custom-call(s32[16]{0:T(128)} %amount_ref.1, f32[16,8,8,128]{3,2,1,0:T(8,128)} %all_to_all.10.x_ref), custom_call_target="tpu_custom_call" | custom-call | tf_op jit(solution)/shard_map/pallas_call | solution.py:85
  38.3 1.9 %collective-permute-start = (f32[1,8,2048]{2,1,0:T(8,128)}, f32[1,8,2048]{2,1,0:T(8,128)S(1)}, u32[]{:S(2)}, u32[]{:S(2)}) collective-permute-start(f32[1,8,2048]{2,1,0:T(8,128)} %get-tuple-element.11), channel_id=1, source_target_pairs={{0,64},{64,8},{128,192},{192,136},{256,320},{320,264},{384,448},{4... | collective-permute-start | bytes 196616 | tf_op jit(solution)/shard_map/ppermute | solution.py:101
  40.2 2.4 %collective-permute-start.1 = (f32[1,8,2048]{2,1,0:T(8,128)}, f32[1,8,2048]{2,1,0:T(8,128)S(1)}, u32[]{:S(2)}, u32[]{:S(2)}) collective-permute-start(f32[1,8,2048]{2,1,0:T(8,128)} %get-tuple-element.12), channel_id=1, source_target_pairs={{64,0},{192,128},{320,256},{448,384},{576,512},{704,640},{832,768}... | collective-permute-start | bytes 196616 | tf_op jit(solution)/shard_map/ppermute | solution.py:102
  42.7 1.3 %collective-permute-start.2 = (f32[8,2048]{1,0:T(8,128)}, f32[8,2048]{1,0:T(8,128)S(1)}, u32[]{:S(2)}, u32[]{:S(2)}) collective-permute-start(f32[8,2048]{1,0:T(8,128)} %get-tuple-element.13), channel_id=1, source_target_pairs={{0,1},{1,2},{2,3},{3,4},{4,5},{5,6},{6,7},{8,9},{9,10},{10,11},{11... | collective-permute-start | bytes 196616 | tf_op jit(solution)/shard_map/ppermute | solution.py:105
  44.0 1.3 %collective-permute-start.3 = (f32[8,2048]{1,0:T(8,128)}, f32[8,2048]{1,0:T(8,128)S(1)}, u32[]{:S(2)}, u32[]{:S(2)}) collective-permute-start(f32[8,2048]{1,0:T(8,128)} %get-tuple-element.14), channel_id=1, source_target_pairs={{1,0},{2,1},{3,2},{4,3},{5,4},{6,5},{7,6},{9,8},{10,9},{11,10},{12... | collective-permute-start | bytes 196616 | tf_op jit(solution)/shard_map/ppermute | solution.py:106
  45.3 0.0 collective-permute-done.prev_ref
  45.3 0.0 copy-start
  45.3 0.8 %collective-permute-done.1.next_ref = f32[1,8,2048]{2,1,0:T(8,128)S(1)} collective-permute-done((f32[1,8,2048]{2,1,0:T(8,128)}, f32[1,8,2048]{2,1,0:T(8,128)S(1)}, u32[]{:S(2)}, u32[]{:S(2)}) %collective-permute-start.1) | collective-permute-done | bytes 65568 | tf_op jit(solution)/shard_map/ppermute | solution.py:102
  46.0 0.0 copy-start.1
  46.0 0.0 collective-permute-done.2.below_ref
  46.0 0.0 copy-start.2
  46.0 3.8 %collective-permute-done.3.above_ref = f32[8,2048]{1,0:T(8,128)S(1)} collective-permute-done((f32[8,2048]{1,0:T(8,128)}, f32[8,2048]{1,0:T(8,128)S(1)}, u32[]{:S(2)}, u32[]{:S(2)}) %collective-permute-start.3) | collective-permute-done | bytes 65568 | tf_op jit(solution)/shard_map/ppermute | solution.py:106
  49.9 0.0 copy-start.3
  49.9 0.0 copy-done
  49.9 0.0 copy-done.1
  49.9 0.0 copy-done.2
  49.9 0.6 copy-done.3
  50.5 2.4 %shard_map.47 = f32[16,8,8,128]{3,2,1,0:T(8,128)} custom-call(f32[8]{0:T(128)} %c_ref.1, f32[16]{0:T(128)} %e_ref.1, f32[8,8,2048]{2,1,0:T(8,128)} %get-tuple-element.10.s_ref, f32[1,8,2048]{2,1,0:T(8,128)} %copy-done, f32[1,8,2048]{2,1,0:T(8,128)} %copy-done.1, f32[8,2048]{1,0:T(8,128)} %copy-done.2, f32[8,2048]{1,0:T(8,128)} %copy-done.3), custom_call_target="tpu_custom_call" | custom-call | tf_op jit(solution)/shard_map/pallas_call | solution.py:108
  52.8 21.0 %all_to_all.11 = f32[16,8,8,128]{3,2,1,0:T(8,128)S(1)} all-to-all(f32[16,8,8,128]{3,2,1,0:T(8,128)} %shard_map.47), channel_id=1, replica_groups=mesh['az'=16,'rad'=8,'vert'=8] {'az'}, dimensions={0} | all-to-all | bytes 1048576 | tf_op jit(solution)/shard_map/all_to_all | solution.py:114
  73.9 0.8 %copy.6 = f32[8,16,8,128]{3,2,1,0:T(8,128)} copy(f32[8,16,8,128]{3,2,1,0:T(8,128)S(1)} %bitcast.2) | data formatting | bytes 1048576
Async XLA Ops:
  38.3 6.9 %collective-permute-start = (f32[1,8,2048]{2,1,0:T(8,128)}, f32[1,8,2048]{2,1,0:T(8,128)S(1)}, u32[]{:S(2)}, u32[]{:S(2)}) collective-permute-start(f32[1,8,2048]{2,1,0:T(8,128)} %get-tuple-element.11), channel_id=1, source_target_pairs={{0,64},{64,8},{128,192},{192,136},{256,320},{320,264},{384,448},{4... | collective-permute-start | bytes 196616 | tf_op jit(solution)/shard_map/ppermute | solution.py:101
  40.2 5.8 %collective-permute-start.1 = (f32[1,8,2048]{2,1,0:T(8,128)}, f32[1,8,2048]{2,1,0:T(8,128)S(1)}, u32[]{:S(2)}, u32[]{:S(2)}) collective-permute-start(f32[1,8,2048]{2,1,0:T(8,128)} %get-tuple-element.12), channel_id=1, source_target_pairs={{64,0},{192,128},{320,256},{448,384},{576,512},{704,640},{832,768}... | collective-permute-start | bytes 196616 | tf_op jit(solution)/shard_map/ppermute | solution.py:102
  42.7 3.4 %collective-permute-start.2 = (f32[8,2048]{1,0:T(8,128)}, f32[8,2048]{1,0:T(8,128)S(1)}, u32[]{:S(2)}, u32[]{:S(2)}) collective-permute-start(f32[8,2048]{1,0:T(8,128)} %get-tuple-element.13), channel_id=1, source_target_pairs={{0,1},{1,2},{2,3},{3,4},{4,5},{5,6},{6,7},{8,9},{9,10},{10,11},{11... | collective-permute-start | bytes 196616 | tf_op jit(solution)/shard_map/ppermute | solution.py:105
  44.0 5.9 %collective-permute-start.3 = (f32[8,2048]{1,0:T(8,128)}, f32[8,2048]{1,0:T(8,128)S(1)}, u32[]{:S(2)}, u32[]{:S(2)}) collective-permute-start(f32[8,2048]{1,0:T(8,128)} %get-tuple-element.14), channel_id=1, source_target_pairs={{1,0},{2,1},{3,2},{4,3},{5,4},{6,5},{7,6},{9,8},{10,9},{11,10},{12... | collective-permute-start | bytes 196616 | tf_op jit(solution)/shard_map/ppermute | solution.py:106
  45.3 4.6 %copy-start = (f32[1,8,2048]{2,1,0:T(8,128)}, f32[1,8,2048]{2,1,0:T(8,128)S(1)}, u32[]{:S(2)}) copy-start(f32[1,8,2048]{2,1,0:T(8,128)S(1)} %collective-permute-done.prev_ref) | copy-start | bytes 196612
  46.0 3.8 %copy-start.1 = (f32[1,8,2048]{2,1,0:T(8,128)}, f32[1,8,2048]{2,1,0:T(8,128)S(1)}, u32[]{:S(2)}) copy-start(f32[1,8,2048]{2,1,0:T(8,128)S(1)} %collective-permute-done.1.next_ref) | copy-start | bytes 196612
  46.0 3.8 %copy-start.2 = (f32[8,2048]{1,0:T(8,128)}, f32[8,2048]{1,0:T(8,128)S(1)}, u32[]{:S(2)}) copy-start(f32[8,2048]{1,0:T(8,128)S(1)} %collective-permute-done.2.below_ref) | copy-start | bytes 196612
  49.9 0.6 copy-start.3

commit v6 on v5

--- a/solution.py
+++ b/solution.py
@@ -7,13 +7,15 @@
 from jax.experimental.pallas import tpu as pltpu
 from jax.sharding import PartitionSpec as P
 
+
 ROUNDS = 1
 
 
-def shift_kernel(parts, amount_ref, x_ref, o_ref, last_ref, first_ref, low_ref, high_ref):
+def shift_kernel(parts, amount_ref, x_ref, o_ref, intra_ref, cross_ref, low_ref, high_ref):
     nblk, rows, nz, width = x_ref.shape
     lane = lax.broadcasted_iota(jnp.int32, (nz, width), 1)
-    base = lax.axis_index("az") % parts * rows
+    h = lax.axis_index("az") % parts
+    base = h * rows
     for k in range(rows):
         s = amount_ref[base + k]
         b = s // width
@@ -28,22 +30,39 @@
             low_ref[k : k + 1, cols] = v[0:1]
             high_ref[k : k + 1, cols] = v[nz - 1 : nz]
             if k == 0:
-                first_ref[0, :, cols] = v
+
+                @pl.when(h == 1)
+                def _():
+                    intra_ref[0, :, cols] = v
+
+                @pl.when(h == 0)
+                def _():
+                    cross_ref[0, :, cols] = v
+
             if k == rows - 1:
-                last_ref[0, :, cols] = v
+
+                @pl.when(h == 0)
+                def _():
+                    intra_ref[0, :, cols] = v
+
+                @pl.when(h == 1)
+                def _():
+                    cross_ref[0, :, cols] = v
 
 
-def diffuse_kernel(parts, offset, c_ref, e_ref, s_ref, prev_ref, next_ref, below_ref, above_ref, o_ref):
+def diffuse_kernel(parts, offset, c_ref, e_ref, s_ref, intra_ref, cross_ref, below_ref, above_ref, o_ref):
     nblk, rows, nz, width = o_ref.shape
     length = s_ref.shape[2]
     sub = lax.broadcasted_iota(jnp.int32, (nz, length), 0)
     me = lax.axis_index("az")
-    base = me % parts * rows
+    h = me % parts
+    base = h * rows
     c = c_ref[me // parts + offset]
+    top = h == 0
     for k in range(rows):
         shifted = s_ref[k]
-        r_plus = s_ref[k + 1] if k < rows - 1 else next_ref[0]
-        r_minus = s_ref[k - 1] if k > 0 else prev_ref[0]
+        r_plus = s_ref[k + 1] if k < rows - 1 else jnp.where(top, intra_ref[0], cross_ref[0])
+        r_minus = s_ref[k - 1] if k > 0 else jnp.where(top, cross_ref[0], intra_ref[0])
         z_plus = jnp.where(sub == nz - 1, above_ref[k : k + 1, :], pltpu.roll(shifted, nz - 1, 0))
         z_minus = jnp.where(sub == 0, below_ref[k : k + 1, :], pltpu.roll(shifted, 1, 0))
         laplace = r_plus + r_minus + z_plus + z_minus - 4.0 * shifted
@@ -57,18 +76,14 @@
             o_ref[j, k] = out[:, j * width : (j + 1) * width]
 
 
-def halo_pairs(rows, halves, fields, step):
+def cross_pairs(nrad, loop):
     pairs = []
-    for r in range(rows):
-        for f in range(fields):
-            for h in range(halves):
-                nh, nr = h + step, r
-                if nh == halves:
-                    nh, nr = 0, r + 1
-                elif nh < 0:
-                    nh, nr = halves - 1, r - 1
-                if 0 <= nr < rows:
-                    pairs.append(((f * halves + h) * rows + r, (f * halves + nh) * rows + nr))
+    for a in range(loop):
+        for r in range(nrad):
+            if a % 2 == 1 and r + 1 < nrad:
+                pairs.append((a * nrad + r, (a - 1) * nrad + r + 1))
+            if a % 2 == 0 and r > 0:
+                pairs.append((a * nrad + r, (a + 1) * nrad + r - 1))
     return pairs
 
 
@@ -76,13 +91,14 @@
     nf, nrow, nz, width = block.shape
     loop = lax.axis_size("az")
     parts = loop // nf
+    assert parts == 2
     rows = nrow // parts
     x = block.reshape(nf * parts, rows, nz, width)
     y = lax.all_to_all(x, "az", 0, 0, tiled=True)
     length = loop * width
     smem = pl.BlockSpec(memory_space=pltpu.SMEM)
     vmem = pl.BlockSpec(memory_space=pltpu.VMEM)
-    shifted, last, first, low, high = pl.pallas_call(
+    shifted, intra, cross, low, high = pl.pallas_call(
         functools.partial(shift_kernel, parts),
         out_shape=(
             jax.ShapeDtypeStruct((rows, nz, length), y.dtype),
@@ -98,19 +114,19 @@
     nrad = lax.axis_size("rad")
     nvert = lax.axis_size("vert")
     both = ("az", "rad")
-    prev_row = lax.ppermute(last, both, halo_pairs(nrad, parts, nf, 1))
-    next_row = lax.ppermute(first, both, halo_pairs(nrad, parts, nf, -1))
     up = [(i, i + 1) for i in range(nvert - 1)]
     down = [(i + 1, i) for i in range(nvert - 1)]
     below = lax.ppermute(high, "vert", up)
     above = lax.ppermute(low, "vert", down)
+    cross_in = lax.ppermute(cross, both, cross_pairs(nrad, loop))
+    intra_in = lax.ppermute(intra, "az", [(i, i ^ 1) for i in range(loop)])
 
     blocks = pl.pallas_call(
         functools.partial(diffuse_kernel, parts, offset),
         out_shape=jax.ShapeDtypeStruct((loop, rows, nz, width), y.dtype),
         in_specs=[smem, smem] + [vmem] * 5,
         out_specs=vmem,
-    )(diffusivity, remap_fraction, shifted, prev_row, next_row, below, above)
+    )(diffusivity, remap_fraction, shifted, intra_in, cross_in, below, above)
     back = lax.all_to_all(blocks, "az", 0, 0, tiled=True)
     return back.reshape(nf, nrow, nz, width)
 

time: 75.1 us -> 76.3 us (1.016)
  Pallas kernels: 5.22 us -> 7.21 us
    pallas_call x1, Pallas kernels: 2.84 us -> 4.82 us  [one_round(): pl.pallas_call(functools.partial(shift_kernel, parts), out_shape=(jax.Sha...]
where the time goes in v6:
time: 76.3 us; the launch traced here: 75.9 us
  blocking collectives  56.5 us (74%)
  Pallas kernels  7.21 us (9%)
  starting transfers between devices  6.41 us (8%)
  waiting for transfers between devices  4.3 us (6%)
  local copies, waits for them, and re-layouts  1.41 us (2%)
    all_to_all x1, blocking collectives, one_round(): y = lax.all_to_all(x, 'az', 0, 0, tiled=True)  35.5 us
    all_to_all x1, blocking collectives, one_round(): back = lax.all_to_all(blocks, 'az', 0, 0, tiled=True)  21 us
    pallas_call x1, Pallas kernels, one_round(): pl.pallas_call(functools.partial(shift_kernel, parts), out_shape=(jax.Sha...  4.82 us
    ppermute x1, waiting for transfers between devices, one_round(): above = lax.ppermute(low, 'vert', down)  3.05 us
    pallas_call x1, Pallas kernels, one_round(): pl.pallas_call(functools.partial(diffuse_kernel, parts, offset), out_shap...  2.38 us
    ppermute x1, starting transfers between devices, one_round(): cross_in = lax.ppermute(cross, both, cross_pairs(nrad, loop))  1.92 us
    ppermute x1, starting transfers between devices, one_round(): intra_in = lax.ppermute(intra, 'az', [(i, i ^ 1) for i in range(loop)])  1.91 us
  transfers between devices with their start and end apart: 4, of which 2 were waited for; matrix products, arithmetic and copies ran while one was open for 0% of the time, Pallas kernels for 0%

profile of v6, /device:TPU:1, one launch (start us, length us, event | category | flops | bytes accessed | tf_op | source)
XLA Modules:
  0.0 75.9 jit_solution(14254863097864501591)
XLA Ops:
  0.0 35.5 %all_to_all.10.x_ref = f32[16,8,8,128]{3,2,1,0:T(8,128)} all-to-all(f32[16,8,8,128]{3,2,1,0:T(8,128)} %bitcast.3), channel_id=1, replica_groups=mesh['az'=16,'rad'=8,'vert'=8] {'az'}, dimensions={0} | all-to-all | bytes 1048576 | tf_op jit(solution)/shard_map/all_to_all | solution.py:97
  35.5 4.8 %shard_map.46 = (f32[8,8,2048]{2,1,0:T(8,128)}, f32[1,8,2048]{2,1,0:T(8,128)}, f32[1,8,2048]{2,1,0:T(8,128)}, f32[8,2048]{1,0:T(8,128)}, f32[8,2048]{1,0:T(8,128)}) custom-call(s32[16]{0:T(128)} %amount_ref.1, f32[16,8,8,128]{3,2,1,0:T(8,128)} %all_to_all.10.x_ref), custom_call_target="tpu_custom_call" | custom-call | tf_op jit(solution)/shard_map/pallas_call | solution.py:101
  40.3 1.9 %collective-permute-start = (f32[1,8,2048]{2,1,0:T(8,128)}, f32[1,8,2048]{2,1,0:T(8,128)S(1)}, u32[]{:S(2)}, u32[]{:S(2)}) collective-permute-start(f32[1,8,2048]{2,1,0:T(8,128)} %get-tuple-element.11), channel_id=1, source_target_pairs={{0,64},{64,0},{128,192},{192,128},{256,320},{320,256},{384,448},{4... | collective-permute-start | bytes 196616 | tf_op jit(solution)/shard_map/ppermute | solution.py:122
  42.2 1.9 %collective-permute-start.1 = (f32[1,8,2048]{2,1,0:T(8,128)}, f32[1,8,2048]{2,1,0:T(8,128)S(1)}, u32[]{:S(2)}, u32[]{:S(2)}) collective-permute-start(f32[1,8,2048]{2,1,0:T(8,128)} %get-tuple-element.12), channel_id=1, source_target_pairs={{8,64},{16,72},{24,80},{32,88},{40,96},{48,104},{56,112},{64,8},{7... | collective-permute-start | bytes 196616 | tf_op jit(solution)/shard_map/ppermute | solution.py:121
  44.1 1.3 %collective-permute-start.2 = (f32[8,2048]{1,0:T(8,128)}, f32[8,2048]{1,0:T(8,128)S(1)}, u32[]{:S(2)}, u32[]{:S(2)}) collective-permute-start(f32[8,2048]{1,0:T(8,128)} %get-tuple-element.13), channel_id=1, source_target_pairs={{0,1},{1,2},{2,3},{3,4},{4,5},{5,6},{6,7},{8,9},{9,10},{10,11},{11... | collective-permute-start | bytes 196616 | tf_op jit(solution)/shard_map/ppermute | solution.py:119
  45.4 1.3 %collective-permute-start.3 = (f32[8,2048]{1,0:T(8,128)}, f32[8,2048]{1,0:T(8,128)S(1)}, u32[]{:S(2)}, u32[]{:S(2)}) collective-permute-start(f32[8,2048]{1,0:T(8,128)} %get-tuple-element.14), channel_id=1, source_target_pairs={{1,0},{2,1},{3,2},{4,3},{5,4},{6,5},{7,6},{9,8},{10,9},{11,10},{12... | collective-permute-start | bytes 196616 | tf_op jit(solution)/shard_map/ppermute | solution.py:120
  46.7 0.0 collective-permute-done.intra_ref
  46.8 0.0 copy-start
  46.8 1.2 %collective-permute-done.1.cross_ref = f32[1,8,2048]{2,1,0:T(8,128)S(1)} collective-permute-done((f32[1,8,2048]{2,1,0:T(8,128)}, f32[1,8,2048]{2,1,0:T(8,128)S(1)}, u32[]{:S(2)}, u32[]{:S(2)}) %collective-permute-start.1) | collective-permute-done | bytes 65568 | tf_op jit(solution)/shard_map/ppermute | solution.py:121
  48.0 0.0 copy-start.1
  48.0 0.0 collective-permute-done.2.below_ref
  48.0 0.0 copy-start.2
  48.0 3.1 %collective-permute-done.3.above_ref = f32[8,2048]{1,0:T(8,128)S(1)} collective-permute-done((f32[8,2048]{1,0:T(8,128)}, f32[8,2048]{1,0:T(8,128)S(1)}, u32[]{:S(2)}, u32[]{:S(2)}) %collective-permute-start.3) | collective-permute-done | bytes 65568 | tf_op jit(solution)/shard_map/ppermute | solution.py:120
  51.1 0.0 copy-start.3
  51.1 0.0 copy-done
  51.1 0.0 copy-done.1
  51.1 0.0 copy-done.2
  51.1 0.6 copy-done.3
  51.7 2.4 %shard_map.47 = f32[16,8,8,128]{3,2,1,0:T(8,128)} custom-call(f32[8]{0:T(128)} %c_ref.1, f32[16]{0:T(128)} %e_ref.1, f32[8,8,2048]{2,1,0:T(8,128)} %get-tuple-element.10.s_ref, f32[1,8,2048]{2,1,0:T(8,128)} %copy-done, f32[1,8,2048]{2,1,0:T(8,128)} %copy-done.1, f32[8,2048]{1,0:T(8,128)} %copy-done.2, f32[8,2048]{1,0:T(8,128)} %copy-done.3), custom_call_target="tpu_custom_call" | custom-call | tf_op jit(solution)/shard_map/pallas_call | solution.py:124
  54.1 21.0 %all_to_all.11 = f32[16,8,8,128]{3,2,1,0:T(8,128)S(1)} all-to-all(f32[16,8,8,128]{3,2,1,0:T(8,128)} %shard_map.47), channel_id=1, replica_groups=mesh['az'=16,'rad'=8,'vert'=8] {'az'}, dimensions={0} | all-to-all | bytes 1048576 | tf_op jit(solution)/shard_map/all_to_all | solution.py:130
  75.1 0.8 %copy.6 = f32[8,16,8,128]{3,2,1,0:T(8,128)} copy(f32[8,16,8,128]{3,2,1,0:T(8,128)S(1)} %bitcast.2) | data formatting | bytes 1048576
Async XLA Ops:
  40.3 6.4 %collective-permute-start = (f32[1,8,2048]{2,1,0:T(8,128)}, f32[1,8,2048]{2,1,0:T(8,128)S(1)}, u32[]{:S(2)}, u32[]{:S(2)}) collective-permute-start(f32[1,8,2048]{2,1,0:T(8,128)} %get-tuple-element.11), channel_id=1, source_target_pairs={{0,64},{64,0},{128,192},{192,128},{256,320},{320,256},{384,448},{4... | collective-permute-start | bytes 196616 | tf_op jit(solution)/shard_map/ppermute | solution.py:122
  42.2 5.8 %collective-permute-start.1 = (f32[1,8,2048]{2,1,0:T(8,128)}, f32[1,8,2048]{2,1,0:T(8,128)S(1)}, u32[]{:S(2)}, u32[]{:S(2)}) collective-permute-start(f32[1,8,2048]{2,1,0:T(8,128)} %get-tuple-element.12), channel_id=1, source_target_pairs={{8,64},{16,72},{24,80},{32,88},{40,96},{48,104},{56,112},{64,8},{7... | collective-permute-start | bytes 196616 | tf_op jit(solution)/shard_map/ppermute | solution.py:121
  44.1 3.9 %collective-permute-start.2 = (f32[8,2048]{1,0:T(8,128)}, f32[8,2048]{1,0:T(8,128)S(1)}, u32[]{:S(2)}, u32[]{:S(2)}) collective-permute-start(f32[8,2048]{1,0:T(8,128)} %get-tuple-element.13), channel_id=1, source_target_pairs={{0,1},{1,2},{2,3},{3,4},{4,5},{5,6},{6,7},{8,9},{9,10},{10,11},{11... | collective-permute-start | bytes 196616 | tf_op jit(solution)/shard_map/ppermute | solution.py:119
  45.4 5.6 %collective-permute-start.3 = (f32[8,2048]{1,0:T(8,128)}, f32[8,2048]{1,0:T(8,128)S(1)}, u32[]{:S(2)}, u32[]{:S(2)}) collective-permute-start(f32[8,2048]{1,0:T(8,128)} %get-tuple-element.14), channel_id=1, source_target_pairs={{1,0},{2,1},{3,2},{4,3},{5,4},{6,5},{7,6},{9,8},{10,9},{11,10},{12... | collective-permute-start | bytes 196616 | tf_op jit(solution)/shard_map/ppermute | solution.py:120
  46.8 4.3 %copy-start = (f32[1,8,2048]{2,1,0:T(8,128)}, f32[1,8,2048]{2,1,0:T(8,128)S(1)}, u32[]{:S(2)}) copy-start(f32[1,8,2048]{2,1,0:T(8,128)S(1)} %collective-permute-done.intra_ref) | copy-start | bytes 196612
  48.0 3.1 %copy-start.1 = (f32[1,8,2048]{2,1,0:T(8,128)}, f32[1,8,2048]{2,1,0:T(8,128)S(1)}, u32[]{:S(2)}) copy-start(f32[1,8,2048]{2,1,0:T(8,128)S(1)} %collective-permute-done.1.cross_ref) | copy-start | bytes 196612
  48.0 3.1 %copy-start.2 = (f32[8,2048]{1,0:T(8,128)}, f32[8,2048]{1,0:T(8,128)S(1)}, u32[]{:S(2)}) copy-start(f32[8,2048]{1,0:T(8,128)S(1)} %collective-permute-done.2.below_ref) | copy-start | bytes 196612
  51.1 0.6 copy-start.3

commit v7 on v6

--- a/solution.py
+++ b/solution.py
@@ -11,10 +11,11 @@
 ROUNDS = 1
 
 
-def shift_kernel(parts, amount_ref, x_ref, o_ref, intra_ref, cross_ref, low_ref, high_ref):
+def shift_kernel(parts, amount_ref, x_ref, o_ref, intra_ref, cross_ref, low_ref, high_ref, first_buf):
     nblk, rows, nz, width = x_ref.shape
     lane = lax.broadcasted_iota(jnp.int32, (nz, width), 1)
     h = lax.axis_index("az") % parts
+    top = h == 0
     base = h * rows
     for k in range(rows):
         s = amount_ref[base + k]
@@ -30,24 +31,11 @@
             low_ref[k : k + 1, cols] = v[0:1]
             high_ref[k : k + 1, cols] = v[nz - 1 : nz]
             if k == 0:
-
-                @pl.when(h == 1)
-                def _():
-                    intra_ref[0, :, cols] = v
-
-                @pl.when(h == 0)
-                def _():
-                    cross_ref[0, :, cols] = v
-
+                first_buf[:, cols] = v
             if k == rows - 1:
-
-                @pl.when(h == 0)
-                def _():
-                    intra_ref[0, :, cols] = v
-
-                @pl.when(h == 1)
-                def _():
-                    cross_ref[0, :, cols] = v
+                first = first_buf[:, cols]
+                intra_ref[0, :, cols] = jnp.where(top, v, first)
+                cross_ref[0, :, cols] = jnp.where(top, first, v)
 
 
 def diffuse_kernel(parts, offset, c_ref, e_ref, s_ref, intra_ref, cross_ref, below_ref, above_ref, o_ref):
@@ -109,6 +97,7 @@
         ),
         in_specs=[smem, vmem],
         out_specs=(vmem,) * 5,
+        scratch_shapes=[pltpu.VMEM((nz, length), y.dtype)],
     )(shear_shift, y)
 
     nrad = lax.axis_size("rad")

time: 76.3 us -> 74.4 us (0.975)
  Pallas kernels: 7.21 us -> 5.23 us
    pallas_call x1, Pallas kernels: 4.82 us -> 2.84 us  [one_round(): pl.pallas_call(functools.partial(shift_kernel, parts), out_shape=(jax.Sha...]
where the time goes in v7:
time: 74.4 us; the launch traced here: 73.9 us
  blocking collectives  56.5 us (76%)
  starting transfers between devices  6.41 us (9%)
  Pallas kernels  5.23 us (7%)
  waiting for transfers between devices  4.3 us (6%)
  local copies, waits for them, and re-layouts  1.41 us (2%)
    all_to_all x1, blocking collectives, one_round(): y = lax.all_to_all(x, 'az', 0, 0, tiled=True)  35.5 us
    all_to_all x1, blocking collectives, one_round(): back = lax.all_to_all(blocks, 'az', 0, 0, tiled=True)  21 us
    ppermute x1, waiting for transfers between devices, one_round(): above = lax.ppermute(low, 'vert', down)  3.05 us
    pallas_call x1, Pallas kernels, one_round(): pl.pallas_call(functools.partial(shift_kernel, parts), out_shape=(jax.Sha...  2.84 us
    pallas_call x1, Pallas kernels, one_round(): pl.pallas_call(functools.partial(diffuse_kernel, parts, offset), out_shap...  2.38 us
    ppermute x1, starting transfers between devices, one_round(): cross_in = lax.ppermute(cross, both, cross_pairs(nrad, loop))  1.92 us
    ppermute x1, starting transfers between devices, one_round(): intra_in = lax.ppermute(intra, 'az', [(i, i ^ 1) for i in range(loop)])  1.91 us
  transfers between devices with their start and end apart: 4, of which 2 were waited for; matrix products, arithmetic and copies ran while one was open for 0% of the time, Pallas kernels for 0%

profile of v7, /device:TPU:1, one launch (start us, length us, event | category | flops | bytes accessed | tf_op | source)
XLA Modules:
  0.0 73.9 jit_solution(15334539031378859442)
XLA Ops:
  0.0 35.5 %all_to_all.10.x_ref = f32[16,8,8,128]{3,2,1,0:T(8,128)} all-to-all(f32[16,8,8,128]{3,2,1,0:T(8,128)} %bitcast.3), channel_id=1, replica_groups=mesh['az'=16,'rad'=8,'vert'=8] {'az'}, dimensions={0} | all-to-all | bytes 1048576 | tf_op jit(solution)/shard_map/all_to_all | solution.py:85
  35.5 2.8 %shard_map.46 = (f32[8,8,2048]{2,1,0:T(8,128)}, f32[1,8,2048]{2,1,0:T(8,128)}, f32[1,8,2048]{2,1,0:T(8,128)}, f32[8,2048]{1,0:T(8,128)}, f32[8,2048]{1,0:T(8,128)}) custom-call(s32[16]{0:T(128)} %amount_ref.1, f32[16,8,8,128]{3,2,1,0:T(8,128)} %all_to_all.10.x_ref), custom_call_target="tpu_custom_call" | custom-call | tf_op jit(solution)/shard_map/pallas_call | solution.py:89
  38.3 1.9 %collective-permute-start = (f32[1,8,2048]{2,1,0:T(8,128)}, f32[1,8,2048]{2,1,0:T(8,128)S(1)}, u32[]{:S(2)}, u32[]{:S(2)}) collective-permute-start(f32[1,8,2048]{2,1,0:T(8,128)} %get-tuple-element.11), channel_id=1, source_target_pairs={{0,64},{64,0},{128,192},{192,128},{256,320},{320,256},{384,448},{4... | collective-permute-start | bytes 196616 | tf_op jit(solution)/shard_map/ppermute | solution.py:111
  40.2 1.9 %collective-permute-start.1 = (f32[1,8,2048]{2,1,0:T(8,128)}, f32[1,8,2048]{2,1,0:T(8,128)S(1)}, u32[]{:S(2)}, u32[]{:S(2)}) collective-permute-start(f32[1,8,2048]{2,1,0:T(8,128)} %get-tuple-element.12), channel_id=1, source_target_pairs={{8,64},{16,72},{24,80},{32,88},{40,96},{48,104},{56,112},{64,8},{7... | collective-permute-start | bytes 196616 | tf_op jit(solution)/shard_map/ppermute | solution.py:110
  42.2 1.3 %collective-permute-start.2 = (f32[8,2048]{1,0:T(8,128)}, f32[8,2048]{1,0:T(8,128)S(1)}, u32[]{:S(2)}, u32[]{:S(2)}) collective-permute-start(f32[8,2048]{1,0:T(8,128)} %get-tuple-element.13), channel_id=1, source_target_pairs={{0,1},{1,2},{2,3},{3,4},{4,5},{5,6},{6,7},{8,9},{9,10},{10,11},{11... | collective-permute-start | bytes 196616 | tf_op jit(solution)/shard_map/ppermute | solution.py:108
  43.5 1.3 %collective-permute-start.3 = (f32[8,2048]{1,0:T(8,128)}, f32[8,2048]{1,0:T(8,128)S(1)}, u32[]{:S(2)}, u32[]{:S(2)}) collective-permute-start(f32[8,2048]{1,0:T(8,128)} %get-tuple-element.14), channel_id=1, source_target_pairs={{1,0},{2,1},{3,2},{4,3},{5,4},{6,5},{7,6},{9,8},{10,9},{11,10},{12... | collective-permute-start | bytes 196616 | tf_op jit(solution)/shard_map/ppermute | solution.py:109
  44.8 0.0 collective-permute-done.intra_ref
  44.8 0.0 copy-start
  44.8 1.2 %collective-permute-done.1.cross_ref = f32[1,8,2048]{2,1,0:T(8,128)S(1)} collective-permute-done((f32[1,8,2048]{2,1,0:T(8,128)}, f32[1,8,2048]{2,1,0:T(8,128)S(1)}, u32[]{:S(2)}, u32[]{:S(2)}) %collective-permute-start.1) | collective-permute-done | bytes 65568 | tf_op jit(solution)/shard_map/ppermute | solution.py:110
  46.0 0.0 copy-start.1
  46.0 0.0 collective-permute-done.2.below_ref
  46.0 0.0 copy-start.2
  46.0 3.1 %collective-permute-done.3.above_ref = f32[8,2048]{1,0:T(8,128)S(1)} collective-permute-done((f32[8,2048]{1,0:T(8,128)}, f32[8,2048]{1,0:T(8,128)S(1)}, u32[]{:S(2)}, u32[]{:S(2)}) %collective-permute-start.3) | collective-permute-done | bytes 65568 | tf_op jit(solution)/shard_map/ppermute | solution.py:109
  49.1 0.0 copy-start.3
  49.1 0.0 copy-done
  49.1 0.0 copy-done.1
  49.1 0.0 copy-done.2
  49.1 0.6 copy-done.3
  49.7 2.4 %shard_map.47 = f32[16,8,8,128]{3,2,1,0:T(8,128)} custom-call(f32[8]{0:T(128)} %c_ref.1, f32[16]{0:T(128)} %e_ref.1, f32[8,8,2048]{2,1,0:T(8,128)} %get-tuple-element.10.s_ref, f32[1,8,2048]{2,1,0:T(8,128)} %copy-done, f32[1,8,2048]{2,1,0:T(8,128)} %copy-done.1, f32[8,2048]{1,0:T(8,128)} %copy-done.2, f32[8,2048]{1,0:T(8,128)} %copy-done.3), custom_call_target="tpu_custom_call" | custom-call | tf_op jit(solution)/shard_map/pallas_call | solution.py:113
  52.1 21.0 %all_to_all.11 = f32[16,8,8,128]{3,2,1,0:T(8,128)S(1)} all-to-all(f32[16,8,8,128]{3,2,1,0:T(8,128)} %shard_map.47), channel_id=1, replica_groups=mesh['az'=16,'rad'=8,'vert'=8] {'az'}, dimensions={0} | all-to-all | bytes 1048576 | tf_op jit(solution)/shard_map/all_to_all | solution.py:119
  73.1 0.8 %copy.6 = f32[8,16,8,128]{3,2,1,0:T(8,128)} copy(f32[8,16,8,128]{3,2,1,0:T(8,128)S(1)} %bitcast.2) | data formatting | bytes 1048576
Async XLA Ops:
  38.3 6.4 %collective-permute-start = (f32[1,8,2048]{2,1,0:T(8,128)}, f32[1,8,2048]{2,1,0:T(8,128)S(1)}, u32[]{:S(2)}, u32[]{:S(2)}) collective-permute-start(f32[1,8,2048]{2,1,0:T(8,128)} %get-tuple-element.11), channel_id=1, source_target_pairs={{0,64},{64,0},{128,192},{192,128},{256,320},{320,256},{384,448},{4... | collective-permute-start | bytes 196616 | tf_op jit(solution)/shard_map/ppermute | solution.py:111
  40.2 5.8 %collective-permute-start.1 = (f32[1,8,2048]{2,1,0:T(8,128)}, f32[1,8,2048]{2,1,0:T(8,128)S(1)}, u32[]{:S(2)}, u32[]{:S(2)}) collective-permute-start(f32[1,8,2048]{2,1,0:T(8,128)} %get-tuple-element.12), channel_id=1, source_target_pairs={{8,64},{16,72},{24,80},{32,88},{40,96},{48,104},{56,112},{64,8},{7... | collective-permute-start | bytes 196616 | tf_op jit(solution)/shard_map/ppermute | solution.py:110
  42.2 3.9 %collective-permute-start.2 = (f32[8,2048]{1,0:T(8,128)}, f32[8,2048]{1,0:T(8,128)S(1)}, u32[]{:S(2)}, u32[]{:S(2)}) collective-permute-start(f32[8,2048]{1,0:T(8,128)} %get-tuple-element.13), channel_id=1, source_target_pairs={{0,1},{1,2},{2,3},{3,4},{4,5},{5,6},{6,7},{8,9},{9,10},{10,11},{11... | collective-permute-start | bytes 196616 | tf_op jit(solution)/shard_map/ppermute | solution.py:108
  43.5 5.6 %collective-permute-start.3 = (f32[8,2048]{1,0:T(8,128)}, f32[8,2048]{1,0:T(8,128)S(1)}, u32[]{:S(2)}, u32[]{:S(2)}) collective-permute-start(f32[8,2048]{1,0:T(8,128)} %get-tuple-element.14), channel_id=1, source_target_pairs={{1,0},{2,1},{3,2},{4,3},{5,4},{6,5},{7,6},{9,8},{10,9},{11,10},{12... | collective-permute-start | bytes 196616 | tf_op jit(solution)/shard_map/ppermute | solution.py:109
  44.8 4.3 %copy-start = (f32[1,8,2048]{2,1,0:T(8,128)}, f32[1,8,2048]{2,1,0:T(8,128)S(1)}, u32[]{:S(2)}) copy-start(f32[1,8,2048]{2,1,0:T(8,128)S(1)} %collective-permute-done.intra_ref) | copy-start | bytes 196612
  46.0 3.1 %copy-start.1 = (f32[1,8,2048]{2,1,0:T(8,128)}, f32[1,8,2048]{2,1,0:T(8,128)S(1)}, u32[]{:S(2)}) copy-start(f32[1,8,2048]{2,1,0:T(8,128)S(1)} %collective-permute-done.1.cross_ref) | copy-start | bytes 196612
  46.0 3.1 %copy-start.2 = (f32[8,2048]{1,0:T(8,128)}, f32[8,2048]{1,0:T(8,128)S(1)}, u32[]{:S(2)}) copy-start(f32[8,2048]{1,0:T(8,128)S(1)} %collective-permute-done.2.below_ref) | copy-start | bytes 196612
  49.1 0.6 copy-start.3

commit v8 on v5

--- a/solution.py
+++ b/solution.py
@@ -7,21 +7,24 @@
 from jax.experimental.pallas import tpu as pltpu
 from jax.sharding import PartitionSpec as P
 
+
 ROUNDS = 1
+LP = pltpu.CompilerParams()
 
 
 def shift_kernel(parts, amount_ref, x_ref, o_ref, last_ref, first_ref, low_ref, high_ref):
     nblk, rows, nz, width = x_ref.shape
     lane = lax.broadcasted_iota(jnp.int32, (nz, width), 1)
     base = lax.axis_index("az") % parts * rows
+    wrap = nblk - 1
     for k in range(rows):
         s = amount_ref[base + k]
         b = s // width
         rem = s % width
         late = lane >= width - rem
         for j in range(nblk):
-            near = x_ref[(j - b + nblk) % nblk, k]
-            far = x_ref[(j - b - 1 + 2 * nblk) % nblk, k]
+            near = x_ref[(j - b) & wrap, k]
+            far = x_ref[(j - b - 1) & wrap, k]
             v = pltpu.roll(jnp.where(late, far, near), rem, 1)
             cols = slice(j * width, (j + 1) * width)
             o_ref[k, :, cols] = v
@@ -76,6 +79,7 @@
     nf, nrow, nz, width = block.shape
     loop = lax.axis_size("az")
     parts = loop // nf
+    assert loop & (loop - 1) == 0
     rows = nrow // parts
     x = block.reshape(nf * parts, rows, nz, width)
     y = lax.all_to_all(x, "az", 0, 0, tiled=True)
@@ -93,23 +97,25 @@
         ),
         in_specs=[smem, vmem],
         out_specs=(vmem,) * 5,
+        compiler_params=LP,
     )(shear_shift, y)
 
     nrad = lax.axis_size("rad")
     nvert = lax.axis_size("vert")
     both = ("az", "rad")
-    prev_row = lax.ppermute(last, both, halo_pairs(nrad, parts, nf, 1))
-    next_row = lax.ppermute(first, both, halo_pairs(nrad, parts, nf, -1))
     up = [(i, i + 1) for i in range(nvert - 1)]
     down = [(i + 1, i) for i in range(nvert - 1)]
     below = lax.ppermute(high, "vert", up)
     above = lax.ppermute(low, "vert", down)
+    prev_row = lax.ppermute(last, both, halo_pairs(nrad, parts, nf, 1))
+    next_row = lax.ppermute(first, both, halo_pairs(nrad, parts, nf, -1))
 
     blocks = pl.pallas_call(
         functools.partial(diffuse_kernel, parts, offset),
         out_shape=jax.ShapeDtypeStruct((loop, rows, nz, width), y.dtype),
         in_specs=[smem, smem] + [vmem] * 5,
         out_specs=vmem,
+        compiler_params=LP,
     )(diffusivity, remap_fraction, shifted, prev_row, next_row, below, above)
     back = lax.all_to_all(blocks, "az", 0, 0, tiled=True)
     return back.reshape(nf, nrow, nz, width)

time: 75.1 us -> 74.5 us (level)
  no operation moved by 1% of the time
where the time goes in v8:
time: 74.5 us; the launch traced here: 74 us
  blocking collectives  56.5 us (76%)
  starting transfers between devices  6.9 us (9%)
  waiting for transfers between devices  4.58 us (6%)
  Pallas kernels  4.57 us (6%)
  local copies, waits for them, and re-layouts  1.41 us (2%)
    all_to_all x1, blocking collectives, one_round(): y = lax.all_to_all(x, 'az', 0, 0, tiled=True)  35.5 us
    all_to_all x1, blocking collectives, one_round(): back = lax.all_to_all(blocks, 'az', 0, 0, tiled=True)  21 us
    ppermute x1, waiting for transfers between devices, one_round(): above = lax.ppermute(low, 'vert', down)  3.81 us
    ppermute x1, starting transfers between devices, one_round(): next_row = lax.ppermute(first, both, halo_pairs(nrad, parts, nf, -1))  2.4 us
    pallas_call x1, Pallas kernels, one_round(): pl.pallas_call(functools.partial(diffuse_kernel, parts, offset), out_shap...  2.38 us
    pallas_call x1, Pallas kernels, one_round(): pl.pallas_call(functools.partial(shift_kernel, parts), out_shape=(jax.Sha...  2.2 us
    ppermute x1, starting transfers between devices, one_round(): prev_row = lax.ppermute(last, both, halo_pairs(nrad, parts, nf, 1))  1.91 us
  transfers between devices with their start and end apart: 4, of which 2 were waited for; matrix products, arithmetic and copies ran while one was open for 0% of the time, Pallas kernels for 0%

profile of v8, /device:TPU:1, one launch (start us, length us, event | category | flops | bytes accessed | tf_op | source)
XLA Modules:
  0.0 74.0 jit_solution(12232030153057963371)
XLA Ops:
  0.0 35.5 %all_to_all.10.x_ref = f32[16,8,8,128]{3,2,1,0:T(8,128)} all-to-all(f32[16,8,8,128]{3,2,1,0:T(8,128)} %bitcast.3), channel_id=1, replica_groups=mesh['az'=16,'rad'=8,'vert'=8] {'az'}, dimensions={0} | all-to-all | bytes 1048576 | tf_op jit(solution)/shard_map/all_to_all | solution.py:85
  35.5 2.2 %shard_map.46 = (f32[8,8,2048]{2,1,0:T(8,128)}, f32[1,8,2048]{2,1,0:T(8,128)}, f32[1,8,2048]{2,1,0:T(8,128)}, f32[8,2048]{1,0:T(8,128)}, f32[8,2048]{1,0:T(8,128)}) custom-call(s32[16]{0:T(128)} %amount_ref.1, f32[16,8,8,128]{3,2,1,0:T(8,128)} %all_to_all.10.x_ref), custom_call_target="tpu_custom_call" | custom-call | tf_op jit(solution)/shard_map/pallas_call | solution.py:89
  37.7 1.9 %collective-permute-start = (f32[1,8,2048]{2,1,0:T(8,128)}, f32[1,8,2048]{2,1,0:T(8,128)S(1)}, u32[]{:S(2)}, u32[]{:S(2)}) collective-permute-start(f32[1,8,2048]{2,1,0:T(8,128)} %get-tuple-element.11), channel_id=1, source_target_pairs={{0,64},{64,8},{128,192},{192,136},{256,320},{320,264},{384,448},{4... | collective-permute-start | bytes 196616 | tf_op jit(solution)/shard_map/ppermute | solution.py:110
  39.6 2.4 %collective-permute-start.1 = (f32[1,8,2048]{2,1,0:T(8,128)}, f32[1,8,2048]{2,1,0:T(8,128)S(1)}, u32[]{:S(2)}, u32[]{:S(2)}) collective-permute-start(f32[1,8,2048]{2,1,0:T(8,128)} %get-tuple-element.12), channel_id=1, source_target_pairs={{64,0},{192,128},{320,256},{448,384},{576,512},{704,640},{832,768}... | collective-permute-start | bytes 196616 | tf_op jit(solution)/shard_map/ppermute | solution.py:111
  42.0 1.3 %collective-permute-start.2 = (f32[8,2048]{1,0:T(8,128)}, f32[8,2048]{1,0:T(8,128)S(1)}, u32[]{:S(2)}, u32[]{:S(2)}) collective-permute-start(f32[8,2048]{1,0:T(8,128)} %get-tuple-element.13), channel_id=1, source_target_pairs={{0,1},{1,2},{2,3},{3,4},{4,5},{5,6},{6,7},{8,9},{9,10},{10,11},{11... | collective-permute-start | bytes 196616 | tf_op jit(solution)/shard_map/ppermute | solution.py:108
  43.3 1.3 %collective-permute-start.3 = (f32[8,2048]{1,0:T(8,128)}, f32[8,2048]{1,0:T(8,128)S(1)}, u32[]{:S(2)}, u32[]{:S(2)}) collective-permute-start(f32[8,2048]{1,0:T(8,128)} %get-tuple-element.14), channel_id=1, source_target_pairs={{1,0},{2,1},{3,2},{4,3},{5,4},{6,5},{7,6},{9,8},{10,9},{11,10},{12... | collective-permute-start | bytes 196616 | tf_op jit(solution)/shard_map/ppermute | solution.py:109
  44.6 0.0 collective-permute-done.prev_ref
  44.6 0.0 copy-start
  44.6 0.8 %collective-permute-done.1.next_ref = f32[1,8,2048]{2,1,0:T(8,128)S(1)} collective-permute-done((f32[1,8,2048]{2,1,0:T(8,128)}, f32[1,8,2048]{2,1,0:T(8,128)S(1)}, u32[]{:S(2)}, u32[]{:S(2)}) %collective-permute-start.1) | collective-permute-done | bytes 65568 | tf_op jit(solution)/shard_map/ppermute | solution.py:111
  45.4 0.0 copy-start.1
  45.4 0.0 collective-permute-done.2.below_ref
  45.4 0.0 copy-start.2
  45.4 3.8 %collective-permute-done.3.above_ref = f32[8,2048]{1,0:T(8,128)S(1)} collective-permute-done((f32[8,2048]{1,0:T(8,128)}, f32[8,2048]{1,0:T(8,128)S(1)}, u32[]{:S(2)}, u32[]{:S(2)}) %collective-permute-start.3) | collective-permute-done | bytes 65568 | tf_op jit(solution)/shard_map/ppermute | solution.py:109
  49.2 0.0 copy-start.3
  49.2 0.0 copy-done
  49.2 0.0 copy-done.1
  49.2 0.0 copy-done.2
  49.2 0.6 copy-done.3
  49.8 2.4 %shard_map.47 = f32[16,8,8,128]{3,2,1,0:T(8,128)} custom-call(f32[8]{0:T(128)} %c_ref.1, f32[16]{0:T(128)} %e_ref.1, f32[8,8,2048]{2,1,0:T(8,128)} %get-tuple-element.10.s_ref, f32[1,8,2048]{2,1,0:T(8,128)} %copy-done, f32[1,8,2048]{2,1,0:T(8,128)} %copy-done.1, f32[8,2048]{1,0:T(8,128)} %copy-done.2, f32[8,2048]{1,0:T(8,128)} %copy-done.3), custom_call_target="tpu_custom_call" | custom-call | tf_op jit(solution)/shard_map/pallas_call | solution.py:113
  52.2 21.0 %all_to_all.11 = f32[16,8,8,128]{3,2,1,0:T(8,128)S(1)} all-to-all(f32[16,8,8,128]{3,2,1,0:T(8,128)} %shard_map.47), channel_id=1, replica_groups=mesh['az'=16,'rad'=8,'vert'=8] {'az'}, dimensions={0} | all-to-all | bytes 1048576 | tf_op jit(solution)/shard_map/all_to_all | solution.py:120
  73.2 0.8 %copy.6 = f32[8,16,8,128]{3,2,1,0:T(8,128)} copy(f32[8,16,8,128]{3,2,1,0:T(8,128)S(1)} %bitcast.2) | data formatting | bytes 1048576
Async XLA Ops:
  37.7 6.9 %collective-permute-start = (f32[1,8,2048]{2,1,0:T(8,128)}, f32[1,8,2048]{2,1,0:T(8,128)S(1)}, u32[]{:S(2)}, u32[]{:S(2)}) collective-permute-start(f32[1,8,2048]{2,1,0:T(8,128)} %get-tuple-element.11), channel_id=1, source_target_pairs={{0,64},{64,8},{128,192},{192,136},{256,320},{320,264},{384,448},{4... | collective-permute-start | bytes 196616 | tf_op jit(solution)/shard_map/ppermute | solution.py:110
  39.6 5.8 %collective-permute-start.1 = (f32[1,8,2048]{2,1,0:T(8,128)}, f32[1,8,2048]{2,1,0:T(8,128)S(1)}, u32[]{:S(2)}, u32[]{:S(2)}) collective-permute-start(f32[1,8,2048]{2,1,0:T(8,128)} %get-tuple-element.12), channel_id=1, source_target_pairs={{64,0},{192,128},{320,256},{448,384},{576,512},{704,640},{832,768}... | collective-permute-start | bytes 196616 | tf_op jit(solution)/shard_map/ppermute | solution.py:111
  42.0 3.4 %collective-permute-start.2 = (f32[8,2048]{1,0:T(8,128)}, f32[8,2048]{1,0:T(8,128)S(1)}, u32[]{:S(2)}, u32[]{:S(2)}) collective-permute-start(f32[8,2048]{1,0:T(8,128)} %get-tuple-element.13), channel_id=1, source_target_pairs={{0,1},{1,2},{2,3},{3,4},{4,5},{5,6},{6,7},{8,9},{9,10},{10,11},{11... | collective-permute-start | bytes 196616 | tf_op jit(solution)/shard_map/ppermute | solution.py:108
  43.3 5.9 %collective-permute-start.3 = (f32[8,2048]{1,0:T(8,128)}, f32[8,2048]{1,0:T(8,128)S(1)}, u32[]{:S(2)}, u32[]{:S(2)}) collective-permute-start(f32[8,2048]{1,0:T(8,128)} %get-tuple-element.14), channel_id=1, source_target_pairs={{1,0},{2,1},{3,2},{4,3},{5,4},{6,5},{7,6},{9,8},{10,9},{11,10},{12... | collective-permute-start | bytes 196616 | tf_op jit(solution)/shard_map/ppermute | solution.py:109
  44.6 4.6 %copy-start = (f32[1,8,2048]{2,1,0:T(8,128)}, f32[1,8,2048]{2,1,0:T(8,128)S(1)}, u32[]{:S(2)}) copy-start(f32[1,8,2048]{2,1,0:T(8,128)S(1)} %collective-permute-done.prev_ref) | copy-start | bytes 196612
  45.4 3.8 %copy-start.1 = (f32[1,8,2048]{2,1,0:T(8,128)}, f32[1,8,2048]{2,1,0:T(8,128)S(1)}, u32[]{:S(2)}) copy-start(f32[1,8,2048]{2,1,0:T(8,128)S(1)} %collective-permute-done.1.next_ref) | copy-start | bytes 196612
  45.4 3.8 %copy-start.2 = (f32[8,2048]{1,0:T(8,128)}, f32[8,2048]{1,0:T(8,128)S(1)}, u32[]{:S(2)}) copy-start(f32[8,2048]{1,0:T(8,128)S(1)} %collective-permute-done.2.below_ref) | copy-start | bytes 196612
  49.2 0.6 copy-start.3

commit v9 on v8

--- a/solution.py
+++ b/solution.py
@@ -9,7 +9,6 @@
 
 
 ROUNDS = 1
-LP = pltpu.CompilerParams()
 
 
 def shift_kernel(parts, amount_ref, x_ref, o_ref, last_ref, first_ref, low_ref, high_ref):
@@ -28,12 +27,12 @@
             v = pltpu.roll(jnp.where(late, far, near), rem, 1)
             cols = slice(j * width, (j + 1) * width)
             o_ref[k, :, cols] = v
-            low_ref[k : k + 1, cols] = v[0:1]
-            high_ref[k : k + 1, cols] = v[nz - 1 : nz]
             if k == 0:
                 first_ref[0, :, cols] = v
             if k == rows - 1:
                 last_ref[0, :, cols] = v
+    low_ref[...] = o_ref[:, 0, :]
+    high_ref[...] = o_ref[:, nz - 1, :]
 
 
 def diffuse_kernel(parts, offset, c_ref, e_ref, s_ref, prev_ref, next_ref, below_ref, above_ref, o_ref):
@@ -97,7 +96,6 @@
         ),
         in_specs=[smem, vmem],
         out_specs=(vmem,) * 5,
-        compiler_params=LP,
     )(shear_shift, y)
 
     nrad = lax.axis_size("rad")
@@ -115,7 +113,6 @@
         out_shape=jax.ShapeDtypeStruct((loop, rows, nz, width), y.dtype),
         in_specs=[smem, smem] + [vmem] * 5,
         out_specs=vmem,
-        compiler_params=LP,
     )(diffusivity, remap_fraction, shifted, prev_row, next_row, below, above)
     back = lax.all_to_all(blocks, "az", 0, 0, tiled=True)
     return back.reshape(nf, nrow, nz, width)

time: 74.5 us -> 74.5 us (level)
  no operation moved by 1% of the time
where the time goes in v9:
time: 74.5 us; the launch traced here: 74 us
  blocking collectives  56.5 us (76%)
  starting transfers between devices  6.9 us (9%)
  Pallas kernels  4.58 us (6%)
  waiting for transfers between devices  4.58 us (6%)
  local copies, waits for them, and re-layouts  1.41 us (2%)
    all_to_all x1, blocking collectives, one_round(): y = lax.all_to_all(x, 'az', 0, 0, tiled=True)  35.5 us
    all_to_all x1, blocking collectives, one_round(): back = lax.all_to_all(blocks, 'az', 0, 0, tiled=True)  21 us
    ppermute x1, waiting for transfers between devices, one_round(): above = lax.ppermute(low, 'vert', down)  3.81 us
    ppermute x1, starting transfers between devices, one_round(): next_row = lax.ppermute(first, both, halo_pairs(nrad, parts, nf, -1))  2.4 us
    pallas_call x1, Pallas kernels, one_round(): pl.pallas_call(functools.partial(diffuse_kernel, parts, offset), out_shap...  2.38 us
    pallas_call x1, Pallas kernels, one_round(): pl.pallas_call(functools.partial(shift_kernel, parts), out_shape=(jax.Sha...  2.2 us
    ppermute x1, starting transfers between devices, one_round(): prev_row = lax.ppermute(last, both, halo_pairs(nrad, parts, nf, 1))  1.91 us
  transfers between devices with their start and end apart: 4, of which 2 were waited for; matrix products, arithmetic and copies ran while one was open for 0% of the time, Pallas kernels for 0%

profile of v9, /device:TPU:1, one launch (start us, length us, event | category | flops | bytes accessed | tf_op | source)
XLA Modules:
  0.0 74.0 jit_solution(3945855560060045186)
XLA Ops:
  0.0 35.5 %all_to_all.10.x_ref = f32[16,8,8,128]{3,2,1,0:T(8,128)} all-to-all(f32[16,8,8,128]{3,2,1,0:T(8,128)} %bitcast.3), channel_id=1, replica_groups=mesh['az'=16,'rad'=8,'vert'=8] {'az'}, dimensions={0} | all-to-all | bytes 1048576 | tf_op jit(solution)/shard_map/all_to_all | solution.py:84
  35.5 2.2 %shard_map.46 = (f32[8,8,2048]{2,1,0:T(8,128)}, f32[1,8,2048]{2,1,0:T(8,128)}, f32[1,8,2048]{2,1,0:T(8,128)}, f32[8,2048]{1,0:T(8,128)}, f32[8,2048]{1,0:T(8,128)}) custom-call(s32[16]{0:T(128)} %amount_ref.1, f32[16,8,8,128]{3,2,1,0:T(8,128)} %all_to_all.10.x_ref), custom_call_target="tpu_custom_call" | custom-call | tf_op jit(solution)/shard_map/pallas_call | solution.py:88
  37.7 1.9 %collective-permute-start = (f32[1,8,2048]{2,1,0:T(8,128)}, f32[1,8,2048]{2,1,0:T(8,128)S(1)}, u32[]{:S(2)}, u32[]{:S(2)}) collective-permute-start(f32[1,8,2048]{2,1,0:T(8,128)} %get-tuple-element.11), channel_id=1, source_target_pairs={{0,64},{64,8},{128,192},{192,136},{256,320},{320,264},{384,448},{4... | collective-permute-start | bytes 196616 | tf_op jit(solution)/shard_map/ppermute | solution.py:108
  39.6 2.4 %collective-permute-start.1 = (f32[1,8,2048]{2,1,0:T(8,128)}, f32[1,8,2048]{2,1,0:T(8,128)S(1)}, u32[]{:S(2)}, u32[]{:S(2)}) collective-permute-start(f32[1,8,2048]{2,1,0:T(8,128)} %get-tuple-element.12), channel_id=1, source_target_pairs={{64,0},{192,128},{320,256},{448,384},{576,512},{704,640},{832,768}... | collective-permute-start | bytes 196616 | tf_op jit(solution)/shard_map/ppermute | solution.py:109
  42.0 1.3 %collective-permute-start.2 = (f32[8,2048]{1,0:T(8,128)}, f32[8,2048]{1,0:T(8,128)S(1)}, u32[]{:S(2)}, u32[]{:S(2)}) collective-permute-start(f32[8,2048]{1,0:T(8,128)} %get-tuple-element.13), channel_id=1, source_target_pairs={{0,1},{1,2},{2,3},{3,4},{4,5},{5,6},{6,7},{8,9},{9,10},{10,11},{11... | collective-permute-start | bytes 196616 | tf_op jit(solution)/shard_map/ppermute | solution.py:106
  43.3 1.3 %collective-permute-start.3 = (f32[8,2048]{1,0:T(8,128)}, f32[8,2048]{1,0:T(8,128)S(1)}, u32[]{:S(2)}, u32[]{:S(2)}) collective-permute-start(f32[8,2048]{1,0:T(8,128)} %get-tuple-element.14), channel_id=1, source_target_pairs={{1,0},{2,1},{3,2},{4,3},{5,4},{6,5},{7,6},{9,8},{10,9},{11,10},{12... | collective-permute-start | bytes 196616 | tf_op jit(solution)/shard_map/ppermute | solution.py:107
  44.6 0.0 collective-permute-done.prev_ref
  44.6 0.0 copy-start
  44.6 0.8 %collective-permute-done.1.next_ref = f32[1,8,2048]{2,1,0:T(8,128)S(1)} collective-permute-done((f32[1,8,2048]{2,1,0:T(8,128)}, f32[1,8,2048]{2,1,0:T(8,128)S(1)}, u32[]{:S(2)}, u32[]{:S(2)}) %collective-permute-start.1) | collective-permute-done | bytes 65568 | tf_op jit(solution)/shard_map/ppermute | solution.py:109
  45.4 0.0 copy-start.1
  45.4 0.0 collective-permute-done.2.below_ref
  45.4 0.0 copy-start.2
  45.4 3.8 %collective-permute-done.3.above_ref = f32[8,2048]{1,0:T(8,128)S(1)} collective-permute-done((f32[8,2048]{1,0:T(8,128)}, f32[8,2048]{1,0:T(8,128)S(1)}, u32[]{:S(2)}, u32[]{:S(2)}) %collective-permute-start.3) | collective-permute-done | bytes 65568 | tf_op jit(solution)/shard_map/ppermute | solution.py:107
  49.2 0.0 copy-start.3
  49.2 0.0 copy-done
  49.2 0.0 copy-done.1
  49.2 0.0 copy-done.2
  49.2 0.6 copy-done.3
  49.8 2.4 %shard_map.47 = f32[16,8,8,128]{3,2,1,0:T(8,128)} custom-call(f32[8]{0:T(128)} %c_ref.1, f32[16]{0:T(128)} %e_ref.1, f32[8,8,2048]{2,1,0:T(8,128)} %get-tuple-element.10.s_ref, f32[1,8,2048]{2,1,0:T(8,128)} %copy-done, f32[1,8,2048]{2,1,0:T(8,128)} %copy-done.1, f32[8,2048]{1,0:T(8,128)} %copy-done.2, f32[8,2048]{1,0:T(8,128)} %copy-done.3), custom_call_target="tpu_custom_call" | custom-call | tf_op jit(solution)/shard_map/pallas_call | solution.py:111
  52.2 21.0 %all_to_all.11 = f32[16,8,8,128]{3,2,1,0:T(8,128)S(1)} all-to-all(f32[16,8,8,128]{3,2,1,0:T(8,128)} %shard_map.47), channel_id=1, replica_groups=mesh['az'=16,'rad'=8,'vert'=8] {'az'}, dimensions={0} | all-to-all | bytes 1048576 | tf_op jit(solution)/shard_map/all_to_all | solution.py:117
  73.2 0.8 %copy.6 = f32[8,16,8,128]{3,2,1,0:T(8,128)} copy(f32[8,16,8,128]{3,2,1,0:T(8,128)S(1)} %bitcast.2) | data formatting | bytes 1048576
Async XLA Ops:
  37.7 6.9 %collective-permute-start = (f32[1,8,2048]{2,1,0:T(8,128)}, f32[1,8,2048]{2,1,0:T(8,128)S(1)}, u32[]{:S(2)}, u32[]{:S(2)}) collective-permute-start(f32[1,8,2048]{2,1,0:T(8,128)} %get-tuple-element.11), channel_id=1, source_target_pairs={{0,64},{64,8},{128,192},{192,136},{256,320},{320,264},{384,448},{4... | collective-permute-start | bytes 196616 | tf_op jit(solution)/shard_map/ppermute | solution.py:108
  39.6 5.8 %collective-permute-start.1 = (f32[1,8,2048]{2,1,0:T(8,128)}, f32[1,8,2048]{2,1,0:T(8,128)S(1)}, u32[]{:S(2)}, u32[]{:S(2)}) collective-permute-start(f32[1,8,2048]{2,1,0:T(8,128)} %get-tuple-element.12), channel_id=1, source_target_pairs={{64,0},{192,128},{320,256},{448,384},{576,512},{704,640},{832,768}... | collective-permute-start | bytes 196616 | tf_op jit(solution)/shard_map/ppermute | solution.py:109
  42.0 3.4 %collective-permute-start.2 = (f32[8,2048]{1,0:T(8,128)}, f32[8,2048]{1,0:T(8,128)S(1)}, u32[]{:S(2)}, u32[]{:S(2)}) collective-permute-start(f32[8,2048]{1,0:T(8,128)} %get-tuple-element.13), channel_id=1, source_target_pairs={{0,1},{1,2},{2,3},{3,4},{4,5},{5,6},{6,7},{8,9},{9,10},{10,11},{11... | collective-permute-start | bytes 196616 | tf_op jit(solution)/shard_map/ppermute | solution.py:106
  43.3 5.9 %collective-permute-start.3 = (f32[8,2048]{1,0:T(8,128)}, f32[8,2048]{1,0:T(8,128)S(1)}, u32[]{:S(2)}, u32[]{:S(2)}) collective-permute-start(f32[8,2048]{1,0:T(8,128)} %get-tuple-element.14), channel_id=1, source_target_pairs={{1,0},{2,1},{3,2},{4,3},{5,4},{6,5},{7,6},{9,8},{10,9},{11,10},{12... | collective-permute-start | bytes 196616 | tf_op jit(solution)/shard_map/ppermute | solution.py:107
  44.6 4.6 %copy-start = (f32[1,8,2048]{2,1,0:T(8,128)}, f32[1,8,2048]{2,1,0:T(8,128)S(1)}, u32[]{:S(2)}) copy-start(f32[1,8,2048]{2,1,0:T(8,128)S(1)} %collective-permute-done.prev_ref) | copy-start | bytes 196612
  45.4 3.8 %copy-start.1 = (f32[1,8,2048]{2,1,0:T(8,128)}, f32[1,8,2048]{2,1,0:T(8,128)S(1)}, u32[]{:S(2)}) copy-start(f32[1,8,2048]{2,1,0:T(8,128)S(1)} %collective-permute-done.1.next_ref) | copy-start | bytes 196612
  45.4 3.8 %copy-start.2 = (f32[8,2048]{1,0:T(8,128)}, f32[8,2048]{1,0:T(8,128)S(1)}, u32[]{:S(2)}) copy-start(f32[8,2048]{1,0:T(8,128)S(1)} %collective-permute-done.2.below_ref) | copy-start | bytes 196612
  49.2 0.6 copy-start.3

commit v10 on v9

--- a/solution.py
+++ b/solution.py
@@ -42,10 +42,10 @@
     me = lax.axis_index("az")
     base = me % parts * rows
     c = c_ref[me // parts + offset]
+    r_minus = prev_ref[0]
+    shifted = s_ref[0]
     for k in range(rows):
-        shifted = s_ref[k]
         r_plus = s_ref[k + 1] if k < rows - 1 else next_ref[0]
-        r_minus = s_ref[k - 1] if k > 0 else prev_ref[0]
         z_plus = jnp.where(sub == nz - 1, above_ref[k : k + 1, :], pltpu.roll(shifted, nz - 1, 0))
         z_minus = jnp.where(sub == 0, below_ref[k : k + 1, :], pltpu.roll(shifted, 1, 0))
         laplace = r_plus + r_minus + z_plus + z_minus - 4.0 * shifted
@@ -57,6 +57,7 @@
         out = diffused - half * (after - before) + half * e * (after - 2.0 * diffused + before)
         for j in range(nblk):
             o_ref[j, k] = out[:, j * width : (j + 1) * width]
+        r_minus, shifted = shifted, r_plus
 
 
 def halo_pairs(rows, halves, fields, step):

time: 74.5 us -> 74.5 us (level)
  no operation moved by 1% of the time
where the time goes in v10:
time: 74.5 us; the launch traced here: 74 us
  blocking collectives  56.5 us (76%)
  starting transfers between devices  6.9 us (9%)
  Pallas kernels  4.58 us (6%)
  waiting for transfers between devices  4.58 us (6%)
  local copies, waits for them, and re-layouts  1.41 us (2%)
    all_to_all x1, blocking collectives, one_round(): y = lax.all_to_all(x, 'az', 0, 0, tiled=True)  35.5 us
    all_to_all x1, blocking collectives, one_round(): back = lax.all_to_all(blocks, 'az', 0, 0, tiled=True)  21 us
    ppermute x1, waiting for transfers between devices, one_round(): above = lax.ppermute(low, 'vert', down)  3.81 us
    ppermute x1, starting transfers between devices, one_round(): next_row = lax.ppermute(first, both, halo_pairs(nrad, parts, nf, -1))  2.4 us
    pallas_call x1, Pallas kernels, one_round(): pl.pallas_call(functools.partial(diffuse_kernel, parts, offset), out_shap...  2.38 us
    pallas_call x1, Pallas kernels, one_round(): pl.pallas_call(functools.partial(shift_kernel, parts), out_shape=(jax.Sha...  2.2 us
    ppermute x1, starting transfers between devices, one_round(): prev_row = lax.ppermute(last, both, halo_pairs(nrad, parts, nf, 1))  1.91 us
  transfers between devices with their start and end apart: 4, of which 2 were waited for; matrix products, arithmetic and copies ran while one was open for 0% of the time, Pallas kernels for 0%

profile of v10, /device:TPU:1, one launch (start us, length us, event | category | flops | bytes accessed | tf_op | source)
XLA Modules:
  0.0 74.0 jit_solution(13729734378579217254)
XLA Ops:
  0.0 35.5 %all_to_all.10.x_ref = f32[16,8,8,128]{3,2,1,0:T(8,128)} all-to-all(f32[16,8,8,128]{3,2,1,0:T(8,128)} %bitcast.3), channel_id=1, replica_groups=mesh['az'=16,'rad'=8,'vert'=8] {'az'}, dimensions={0} | all-to-all | bytes 1048576 | tf_op jit(solution)/shard_map/all_to_all | solution.py:85
  35.5 2.2 %shard_map.46 = (f32[8,8,2048]{2,1,0:T(8,128)}, f32[1,8,2048]{2,1,0:T(8,128)}, f32[1,8,2048]{2,1,0:T(8,128)}, f32[8,2048]{1,0:T(8,128)}, f32[8,2048]{1,0:T(8,128)}) custom-call(s32[16]{0:T(128)} %amount_ref.1, f32[16,8,8,128]{3,2,1,0:T(8,128)} %all_to_all.10.x_ref), custom_call_target="tpu_custom_call" | custom-call | tf_op jit(solution)/shard_map/pallas_call | solution.py:89
  37.7 1.9 %collective-permute-start = (f32[1,8,2048]{2,1,0:T(8,128)}, f32[1,8,2048]{2,1,0:T(8,128)S(1)}, u32[]{:S(2)}, u32[]{:S(2)}) collective-permute-start(f32[1,8,2048]{2,1,0:T(8,128)} %get-tuple-element.11), channel_id=1, source_target_pairs={{0,64},{64,8},{128,192},{192,136},{256,320},{320,264},{384,448},{4... | collective-permute-start | bytes 196616 | tf_op jit(solution)/shard_map/ppermute | solution.py:109
  39.6 2.4 %collective-permute-start.1 = (f32[1,8,2048]{2,1,0:T(8,128)}, f32[1,8,2048]{2,1,0:T(8,128)S(1)}, u32[]{:S(2)}, u32[]{:S(2)}) collective-permute-start(f32[1,8,2048]{2,1,0:T(8,128)} %get-tuple-element.12), channel_id=1, source_target_pairs={{64,0},{192,128},{320,256},{448,384},{576,512},{704,640},{832,768}... | collective-permute-start | bytes 196616 | tf_op jit(solution)/shard_map/ppermute | solution.py:110
  42.0 1.3 %collective-permute-start.2 = (f32[8,2048]{1,0:T(8,128)}, f32[8,2048]{1,0:T(8,128)S(1)}, u32[]{:S(2)}, u32[]{:S(2)}) collective-permute-start(f32[8,2048]{1,0:T(8,128)} %get-tuple-element.13), channel_id=1, source_target_pairs={{0,1},{1,2},{2,3},{3,4},{4,5},{5,6},{6,7},{8,9},{9,10},{10,11},{11... | collective-permute-start | bytes 196616 | tf_op jit(solution)/shard_map/ppermute | solution.py:107
  43.3 1.3 %collective-permute-start.3 = (f32[8,2048]{1,0:T(8,128)}, f32[8,2048]{1,0:T(8,128)S(1)}, u32[]{:S(2)}, u32[]{:S(2)}) collective-permute-start(f32[8,2048]{1,0:T(8,128)} %get-tuple-element.14), channel_id=1, source_target_pairs={{1,0},{2,1},{3,2},{4,3},{5,4},{6,5},{7,6},{9,8},{10,9},{11,10},{12... | collective-permute-start | bytes 196616 | tf_op jit(solution)/shard_map/ppermute | solution.py:108
  44.6 0.0 collective-permute-done.prev_ref
  44.6 0.0 copy-start
  44.6 0.8 %collective-permute-done.1.next_ref = f32[1,8,2048]{2,1,0:T(8,128)S(1)} collective-permute-done((f32[1,8,2048]{2,1,0:T(8,128)}, f32[1,8,2048]{2,1,0:T(8,128)S(1)}, u32[]{:S(2)}, u32[]{:S(2)}) %collective-permute-start.1) | collective-permute-done | bytes 65568 | tf_op jit(solution)/shard_map/ppermute | solution.py:110
  45.4 0.0 copy-start.1
  45.4 0.0 collective-permute-done.2.below_ref
  45.4 0.0 copy-start.2
  45.4 3.8 %collective-permute-done.3.above_ref = f32[8,2048]{1,0:T(8,128)S(1)} collective-permute-done((f32[8,2048]{1,0:T(8,128)}, f32[8,2048]{1,0:T(8,128)S(1)}, u32[]{:S(2)}, u32[]{:S(2)}) %collective-permute-start.3) | collective-permute-done | bytes 65568 | tf_op jit(solution)/shard_map/ppermute | solution.py:108
  49.2 0.0 copy-start.3
  49.2 0.0 copy-done
  49.2 0.0 copy-done.1
  49.2 0.0 copy-done.2
  49.2 0.6 copy-done.3
  49.8 2.4 %shard_map.47 = f32[16,8,8,128]{3,2,1,0:T(8,128)} custom-call(f32[8]{0:T(128)} %c_ref.1, f32[16]{0:T(128)} %e_ref.1, f32[8,8,2048]{2,1,0:T(8,128)} %get-tuple-element.10.s_ref, f32[1,8,2048]{2,1,0:T(8,128)} %copy-done, f32[1,8,2048]{2,1,0:T(8,128)} %copy-done.1, f32[8,2048]{1,0:T(8,128)} %copy-done.2, f32[8,2048]{1,0:T(8,128)} %copy-done.3), custom_call_target="tpu_custom_call" | custom-call | tf_op jit(solution)/shard_map/pallas_call | solution.py:112
  52.2 21.0 %all_to_all.11 = f32[16,8,8,128]{3,2,1,0:T(8,128)S(1)} all-to-all(f32[16,8,8,128]{3,2,1,0:T(8,128)} %shard_map.47), channel_id=1, replica_groups=mesh['az'=16,'rad'=8,'vert'=8] {'az'}, dimensions={0} | all-to-all | bytes 1048576 | tf_op jit(solution)/shard_map/all_to_all | solution.py:118
  73.3 0.8 %copy.6 = f32[8,16,8,128]{3,2,1,0:T(8,128)} copy(f32[8,16,8,128]{3,2,1,0:T(8,128)S(1)} %bitcast.2) | data formatting | bytes 1048576
Async XLA Ops:
  37.7 6.9 %collective-permute-start = (f32[1,8,2048]{2,1,0:T(8,128)}, f32[1,8,2048]{2,1,0:T(8,128)S(1)}, u32[]{:S(2)}, u32[]{:S(2)}) collective-permute-start(f32[1,8,2048]{2,1,0:T(8,128)} %get-tuple-element.11), channel_id=1, source_target_pairs={{0,64},{64,8},{128,192},{192,136},{256,320},{320,264},{384,448},{4... | collective-permute-start | bytes 196616 | tf_op jit(solution)/shard_map/ppermute | solution.py:109
  39.6 5.8 %collective-permute-start.1 = (f32[1,8,2048]{2,1,0:T(8,128)}, f32[1,8,2048]{2,1,0:T(8,128)S(1)}, u32[]{:S(2)}, u32[]{:S(2)}) collective-permute-start(f32[1,8,2048]{2,1,0:T(8,128)} %get-tuple-element.12), channel_id=1, source_target_pairs={{64,0},{192,128},{320,256},{448,384},{576,512},{704,640},{832,768}... | collective-permute-start | bytes 196616 | tf_op jit(solution)/shard_map/ppermute | solution.py:110
  42.0 3.4 %collective-permute-start.2 = (f32[8,2048]{1,0:T(8,128)}, f32[8,2048]{1,0:T(8,128)S(1)}, u32[]{:S(2)}, u32[]{:S(2)}) collective-permute-start(f32[8,2048]{1,0:T(8,128)} %get-tuple-element.13), channel_id=1, source_target_pairs={{0,1},{1,2},{2,3},{3,4},{4,5},{5,6},{6,7},{8,9},{9,10},{10,11},{11... | collective-permute-start | bytes 196616 | tf_op jit(solution)/shard_map/ppermute | solution.py:107
  43.3 5.9 %collective-permute-start.3 = (f32[8,2048]{1,0:T(8,128)}, f32[8,2048]{1,0:T(8,128)S(1)}, u32[]{:S(2)}, u32[]{:S(2)}) collective-permute-start(f32[8,2048]{1,0:T(8,128)} %get-tuple-element.14), channel_id=1, source_target_pairs={{1,0},{2,1},{3,2},{4,3},{5,4},{6,5},{7,6},{9,8},{10,9},{11,10},{12... | collective-permute-start | bytes 196616 | tf_op jit(solution)/shard_map/ppermute | solution.py:108
  44.6 4.6 %copy-start = (f32[1,8,2048]{2,1,0:T(8,128)}, f32[1,8,2048]{2,1,0:T(8,128)S(1)}, u32[]{:S(2)}) copy-start(f32[1,8,2048]{2,1,0:T(8,128)S(1)} %collective-permute-done.prev_ref) | copy-start | bytes 196612
  45.4 3.8 %copy-start.1 = (f32[1,8,2048]{2,1,0:T(8,128)}, f32[1,8,2048]{2,1,0:T(8,128)S(1)}, u32[]{:S(2)}) copy-start(f32[1,8,2048]{2,1,0:T(8,128)S(1)} %collective-permute-done.1.next_ref) | copy-start | bytes 196612
  45.4 3.8 %copy-start.2 = (f32[8,2048]{1,0:T(8,128)}, f32[8,2048]{1,0:T(8,128)S(1)}, u32[]{:S(2)}) copy-start(f32[8,2048]{1,0:T(8,128)S(1)} %collective-permute-done.2.below_ref) | copy-start | bytes 196612
  49.2 0.6 copy-start.3

commit v11 on v10

--- a/solution.py
+++ b/solution.py
@@ -18,8 +18,8 @@
     wrap = nblk - 1
     for k in range(rows):
         s = amount_ref[base + k]
-        b = s // width
-        rem = s % width
+        b = s >> (width.bit_length() - 1)
+        rem = s & (width - 1)
         late = lane >= width - rem
         for j in range(nblk):
             near = x_ref[(j - b) & wrap, k]
@@ -79,7 +79,7 @@
     nf, nrow, nz, width = block.shape
     loop = lax.axis_size("az")
     parts = loop // nf
-    assert loop & (loop - 1) == 0
+    assert loop & (loop - 1) == 0 and width & (width - 1) == 0
     rows = nrow // parts
     x = block.reshape(nf * parts, rows, nz, width)
     y = lax.all_to_all(x, "az", 0, 0, tiled=True)

time: 74.5 us -> 74.4 us (level)
  no operation moved by 1% of the time
where the time goes in v11:
time: 74.4 us; the launch traced here: 74 us
  blocking collectives  56.5 us (76%)
  starting transfers between devices  6.9 us (9%)
  waiting for transfers between devices  4.58 us (6%)
  Pallas kernels  4.54 us (6%)
  local copies, waits for them, and re-layouts  1.41 us (2%)
    all_to_all x1, blocking collectives, one_round(): y = lax.all_to_all(x, 'az', 0, 0, tiled=True)  35.5 us
    all_to_all x1, blocking collectives, one_round(): back = lax.all_to_all(blocks, 'az', 0, 0, tiled=True)  21 us
    ppermute x1, waiting for transfers between devices, one_round(): above = lax.ppermute(low, 'vert', down)  3.81 us
    ppermute x1, starting transfers between devices, one_round(): next_row = lax.ppermute(first, both, halo_pairs(nrad, parts, nf, -1))  2.4 us
    pallas_call x1, Pallas kernels, one_round(): pl.pallas_call(functools.partial(diffuse_kernel, parts, offset), out_shap...  2.38 us
    pallas_call x1, Pallas kernels, one_round(): pl.pallas_call(functools.partial(shift_kernel, parts), out_shape=(jax.Sha...  2.16 us
    ppermute x1, starting transfers between devices, one_round(): prev_row = lax.ppermute(last, both, halo_pairs(nrad, parts, nf, 1))  1.91 us
  transfers between devices with their start and end apart: 4, of which 2 were waited for; matrix products, arithmetic and copies ran while one was open for 0% of the time, Pallas kernels for 0%

profile of v11, /device:TPU:1, one launch (start us, length us, event | category | flops | bytes accessed | tf_op | source)
XLA Modules:
  0.0 74.0 jit_solution(15757990248834876385)
XLA Ops:
  0.0 35.5 %all_to_all.10.x_ref = f32[16,8,8,128]{3,2,1,0:T(8,128)} all-to-all(f32[16,8,8,128]{3,2,1,0:T(8,128)} %bitcast.3), channel_id=1, replica_groups=mesh['az'=16,'rad'=8,'vert'=8] {'az'}, dimensions={0} | all-to-all | bytes 1048576 | tf_op jit(solution)/shard_map/all_to_all | solution.py:85
  35.5 2.2 %shard_map.46 = (f32[8,8,2048]{2,1,0:T(8,128)}, f32[1,8,2048]{2,1,0:T(8,128)}, f32[1,8,2048]{2,1,0:T(8,128)}, f32[8,2048]{1,0:T(8,128)}, f32[8,2048]{1,0:T(8,128)}) custom-call(s32[16]{0:T(128)} %amount_ref.1, f32[16,8,8,128]{3,2,1,0:T(8,128)} %all_to_all.10.x_ref), custom_call_target="tpu_custom_call" | custom-call | tf_op jit(solution)/shard_map/pallas_call | solution.py:89
  37.6 1.9 %collective-permute-start = (f32[1,8,2048]{2,1,0:T(8,128)}, f32[1,8,2048]{2,1,0:T(8,128)S(1)}, u32[]{:S(2)}, u32[]{:S(2)}) collective-permute-start(f32[1,8,2048]{2,1,0:T(8,128)} %get-tuple-element.11), channel_id=1, source_target_pairs={{0,64},{64,8},{128,192},{192,136},{256,320},{320,264},{384,448},{4... | collective-permute-start | bytes 196616 | tf_op jit(solution)/shard_map/ppermute | solution.py:109
  39.6 2.4 %collective-permute-start.1 = (f32[1,8,2048]{2,1,0:T(8,128)}, f32[1,8,2048]{2,1,0:T(8,128)S(1)}, u32[]{:S(2)}, u32[]{:S(2)}) collective-permute-start(f32[1,8,2048]{2,1,0:T(8,128)} %get-tuple-element.12), channel_id=1, source_target_pairs={{64,0},{192,128},{320,256},{448,384},{576,512},{704,640},{832,768}... | collective-permute-start | bytes 196616 | tf_op jit(solution)/shard_map/ppermute | solution.py:110
  42.0 1.3 %collective-permute-start.2 = (f32[8,2048]{1,0:T(8,128)}, f32[8,2048]{1,0:T(8,128)S(1)}, u32[]{:S(2)}, u32[]{:S(2)}) collective-permute-start(f32[8,2048]{1,0:T(8,128)} %get-tuple-element.13), channel_id=1, source_target_pairs={{0,1},{1,2},{2,3},{3,4},{4,5},{5,6},{6,7},{8,9},{9,10},{10,11},{11... | collective-permute-start | bytes 196616 | tf_op jit(solution)/shard_map/ppermute | solution.py:107
  43.3 1.3 %collective-permute-start.3 = (f32[8,2048]{1,0:T(8,128)}, f32[8,2048]{1,0:T(8,128)S(1)}, u32[]{:S(2)}, u32[]{:S(2)}) collective-permute-start(f32[8,2048]{1,0:T(8,128)} %get-tuple-element.14), channel_id=1, source_target_pairs={{1,0},{2,1},{3,2},{4,3},{5,4},{6,5},{7,6},{9,8},{10,9},{11,10},{12... | collective-permute-start | bytes 196616 | tf_op jit(solution)/shard_map/ppermute | solution.py:108
  44.6 0.0 collective-permute-done.prev_ref
  44.6 0.0 copy-start
  44.6 0.8 %collective-permute-done.1.next_ref = f32[1,8,2048]{2,1,0:T(8,128)S(1)} collective-permute-done((f32[1,8,2048]{2,1,0:T(8,128)}, f32[1,8,2048]{2,1,0:T(8,128)S(1)}, u32[]{:S(2)}, u32[]{:S(2)}) %collective-permute-start.1) | collective-permute-done | bytes 65568 | tf_op jit(solution)/shard_map/ppermute | solution.py:110
  45.4 0.0 copy-start.1
  45.4 0.0 collective-permute-done.2.below_ref
  45.4 0.0 copy-start.2
  45.4 3.8 %collective-permute-done.3.above_ref = f32[8,2048]{1,0:T(8,128)S(1)} collective-permute-done((f32[8,2048]{1,0:T(8,128)}, f32[8,2048]{1,0:T(8,128)S(1)}, u32[]{:S(2)}, u32[]{:S(2)}) %collective-permute-start.3) | collective-permute-done | bytes 65568 | tf_op jit(solution)/shard_map/ppermute | solution.py:108
  49.2 0.0 copy-start.3
  49.2 0.0 copy-done
  49.2 0.0 copy-done.1
  49.2 0.0 copy-done.2
  49.2 0.6 copy-done.3
  49.8 2.4 %shard_map.47 = f32[16,8,8,128]{3,2,1,0:T(8,128)} custom-call(f32[8]{0:T(128)} %c_ref.1, f32[16]{0:T(128)} %e_ref.1, f32[8,8,2048]{2,1,0:T(8,128)} %get-tuple-element.10.s_ref, f32[1,8,2048]{2,1,0:T(8,128)} %copy-done, f32[1,8,2048]{2,1,0:T(8,128)} %copy-done.1, f32[8,2048]{1,0:T(8,128)} %copy-done.2, f32[8,2048]{1,0:T(8,128)} %copy-done.3), custom_call_target="tpu_custom_call" | custom-call | tf_op jit(solution)/shard_map/pallas_call | solution.py:112
  52.2 21.0 %all_to_all.11 = f32[16,8,8,128]{3,2,1,0:T(8,128)S(1)} all-to-all(f32[16,8,8,128]{3,2,1,0:T(8,128)} %shard_map.47), channel_id=1, replica_groups=mesh['az'=16,'rad'=8,'vert'=8] {'az'}, dimensions={0} | all-to-all | bytes 1048576 | tf_op jit(solution)/shard_map/all_to_all | solution.py:118
  73.2 0.8 %copy.6 = f32[8,16,8,128]{3,2,1,0:T(8,128)} copy(f32[8,16,8,128]{3,2,1,0:T(8,128)S(1)} %bitcast.2) | data formatting | bytes 1048576
Async XLA Ops:
  37.6 6.9 %collective-permute-start = (f32[1,8,2048]{2,1,0:T(8,128)}, f32[1,8,2048]{2,1,0:T(8,128)S(1)}, u32[]{:S(2)}, u32[]{:S(2)}) collective-permute-start(f32[1,8,2048]{2,1,0:T(8,128)} %get-tuple-element.11), channel_id=1, source_target_pairs={{0,64},{64,8},{128,192},{192,136},{256,320},{320,264},{384,448},{4... | collective-permute-start | bytes 196616 | tf_op jit(solution)/shard_map/ppermute | solution.py:109
  39.6 5.8 %collective-permute-start.1 = (f32[1,8,2048]{2,1,0:T(8,128)}, f32[1,8,2048]{2,1,0:T(8,128)S(1)}, u32[]{:S(2)}, u32[]{:S(2)}) collective-permute-start(f32[1,8,2048]{2,1,0:T(8,128)} %get-tuple-element.12), channel_id=1, source_target_pairs={{64,0},{192,128},{320,256},{448,384},{576,512},{704,640},{832,768}... | collective-permute-start | bytes 196616 | tf_op jit(solution)/shard_map/ppermute | solution.py:110
  42.0 3.4 %collective-permute-start.2 = (f32[8,2048]{1,0:T(8,128)}, f32[8,2048]{1,0:T(8,128)S(1)}, u32[]{:S(2)}, u32[]{:S(2)}) collective-permute-start(f32[8,2048]{1,0:T(8,128)} %get-tuple-element.13), channel_id=1, source_target_pairs={{0,1},{1,2},{2,3},{3,4},{4,5},{5,6},{6,7},{8,9},{9,10},{10,11},{11... | collective-permute-start | bytes 196616 | tf_op jit(solution)/shard_map/ppermute | solution.py:107
  43.3 5.9 %collective-permute-start.3 = (f32[8,2048]{1,0:T(8,128)}, f32[8,2048]{1,0:T(8,128)S(1)}, u32[]{:S(2)}, u32[]{:S(2)}) collective-permute-start(f32[8,2048]{1,0:T(8,128)} %get-tuple-element.14), channel_id=1, source_target_pairs={{1,0},{2,1},{3,2},{4,3},{5,4},{6,5},{7,6},{9,8},{10,9},{11,10},{12... | collective-permute-start | bytes 196616 | tf_op jit(solution)/shard_map/ppermute | solution.py:108
  44.6 4.6 %copy-start = (f32[1,8,2048]{2,1,0:T(8,128)}, f32[1,8,2048]{2,1,0:T(8,128)S(1)}, u32[]{:S(2)}) copy-start(f32[1,8,2048]{2,1,0:T(8,128)S(1)} %collective-permute-done.prev_ref) | copy-start | bytes 196612
  45.4 3.8 %copy-start.1 = (f32[1,8,2048]{2,1,0:T(8,128)}, f32[1,8,2048]{2,1,0:T(8,128)S(1)}, u32[]{:S(2)}) copy-start(f32[1,8,2048]{2,1,0:T(8,128)S(1)} %collective-permute-done.1.next_ref) | copy-start | bytes 196612
  45.4 3.8 %copy-start.2 = (f32[8,2048]{1,0:T(8,128)}, f32[8,2048]{1,0:T(8,128)S(1)}, u32[]{:S(2)}) copy-start(f32[8,2048]{1,0:T(8,128)S(1)} %collective-permute-done.2.below_ref) | copy-start | bytes 196612
  49.2 0.6 copy-start.3
